TPU v7x, 256 devices: a whole 4x4x8 slice. The times are simulated.
256 devices in a mesh: ctx: 32 (over z, y_hi, core), mp: 8 (over x, y_lo).
Axes of the slice: x: 4, y: 4 (y_hi: 2, y_lo: 2; y = y_hi * 2 + y_lo), z: 8, core: 2. Of those that a mesh axis runs over, the one named last changes fastest.
Arguments:
- proj: bfloat16 [8192, 3, 8192], P(('ctx', 'mp')), may hold values from -6 to 6
- conv_weight: float32 [3, 7, 8192], replicated, may hold values from -2 to 2
- residues: float32 [128, 16], P('mp'), may hold values from -1.5 to 1.5
- decays: float32 [128, 16], P('mp'), may hold values from 1.2207031e-05 to 0.03
- doc_lengths: int32 [64], replicated, may hold values from 1 to 768, 8192 in all
Outputs:
- mixed: bfloat16 [8192, 8192], P(('ctx', 'mp'))
All inputs are finite; a program needn't handle non-finite values.
Results may differ from a plain program's by a relative error of at most 0.014.
Values may be sent and summed in bfloat16 or wider, within the bound.
No kernel may reach another device: no remote copies, remote signals or barrier semaphores. Data moves between devices by JAX's collectives and lax.ppermute only.
A program may use at most 64 MiB of HBM per device.

v0:
```python
import jax
import jax.numpy as jnp
from jax import lax
from jax.sharding import PartitionSpec as P


def shifted_2(block, axis, distance):
    devices = range(lax.axis_size(axis))
    route = [(i - distance, i) for i in devices if i - distance in devices]
    return lax.ppermute(block, axis, route)


def document_number_index(doc_lengths, positions):
    doc_starts = jnp.cumsum(doc_lengths) - doc_lengths
    inside = (doc_starts[None, :] <= positions[:, None]).astype(jnp.int32)
    return jnp.sum(inside, axis=1) - 1


def short_convolution(padded, conv_weight, padded_document_ids, padded_pos, out_rows):
    kernel_len = conv_weight.shape[1]
    result = jnp.zeros((out_rows,) + padded.shape[1:], jnp.float32)
    own_docs = padded_document_ids[kernel_len - 1 :]
    for position_shift in range(kernel_len):
        begin_row = kernel_len - 1 - position_shift
        earlier = padded[begin_row : begin_row + out_rows].astype(jnp.float32)
        keep_mask = (padded_document_ids[begin_row : begin_row + out_rows] == own_docs) & (
            padded_pos[begin_row : begin_row + out_rows] >= 0
        )
        result = (
            result
            + conv_weight[:, position_shift, :][None]
            * earlier
            * keep_mask.astype(jnp.float32)[:, None, None]
        )
    return result


def filter_tile(coefficient, decays, out_index, piece_start, width_in):
    span = float(width_in)
    out_float = (out_index - piece_start).astype(jnp.float32)
    shifted = jnp.maximum(out_float - span, -span)
    left_neighbor = coefficient[:, :, None] * jnp.exp(-decays[:, :, None] * shifted[None, None, :])
    in_offsets = jnp.arange(width_in).astype(jnp.float32)
    right_neighbor = jnp.exp(-decays[:, :, None] * (span - in_offsets)[None, None, :])
    token_tile_rows = jnp.einsum(
        "ejz,ejx->ezx", left_neighbor, right_neighbor, precision=lax.Precision.HIGHEST
    )
    lag_matrix = (out_index - piece_start)[:, None] - jnp.arange(width_in, dtype=jnp.int32)[None, :]
    return jnp.where((lag_matrix >= 0)[None], token_tile_rows, 0.0)


def split_product(form, weights, inputs):
    upper_part = weights.astype(jnp.bfloat16)
    lower_part = (weights - upper_part.astype(jnp.float32)).astype(jnp.bfloat16)
    first = jnp.einsum(form, upper_part, inputs, preferred_element_type=jnp.float32)
    return first + jnp.einsum(form, lower_part, inputs, preferred_element_type=jnp.float32)


def long_filter(product, residues, decays, block_begin_position):
    block_len = product.shape[0]
    channels = product.shape[1]
    group_count = residues.shape[0]
    group_width = channels // group_count
    coefficient = residues * jnp.sqrt(decays)
    out_index = block_begin_position + jnp.arange(block_len, dtype=jnp.int32)

    def one_tile(running, rows_part, part_start):
        width_in = rows_part.shape[0]
        token_tile_rows = filter_tile(coefficient, decays, out_index, part_start, width_in)
        inputs = rows_part.reshape(width_in, group_count, group_width)
        return running + split_product("grs,sgc->rgc", token_tile_rows, inputs)

    initial = jnp.zeros((block_len, group_count, group_width), jnp.float32)
    piece_rows = lax.all_gather(product, "ctx", axis=0, tiled=True)
    width_in = piece_rows.shape[0]
    count_blocks = width_in // block_len
    stacked = piece_rows.reshape(count_blocks, block_len, channels)
    starts = block_len * jnp.arange(count_blocks, dtype=jnp.int32)

    def scan_step(carry, pair):
        return (one_tile(carry, pair[0], pair[1]), None)

    result, unused = lax.scan(scan_step, initial, (stacked, starts))
    return result.reshape(block_len, channels).astype(jnp.bfloat16)


def shards(proj, conv_weight, residues, decays, doc_lengths):
    kernel_len = conv_weight.shape[1]
    channel_rows = lax.all_to_all(proj, "mp", split_axis=2, concat_axis=0, tiled=True)
    block_len = channel_rows.shape[0]
    channels = channel_rows.shape[2]
    local_weight = lax.dynamic_slice_in_dim(
        conv_weight, lax.axis_index("mp") * channels, channels, 2
    )
    tail_rows = shifted_2(channel_rows[block_len - (kernel_len - 1) :], "ctx", 1)
    block_begin_position = lax.axis_index("ctx") * block_len
    padded_pos = (
        block_begin_position
        - (kernel_len - 1)
        + jnp.arange(block_len + kernel_len - 1, dtype=jnp.int32)
    )
    padded_document_ids = document_number_index(doc_lengths, padded_pos)
    padded = jnp.concatenate([tail_rows, channel_rows], axis=0)
    conv = short_convolution(padded, local_weight, padded_document_ids, padded_pos, block_len)
    query_part = conv[:, 0]
    product = (conv[:, 1] * conv[:, 2]).astype(jnp.bfloat16)
    filtered = long_filter(product, residues, decays, block_begin_position)
    mixed_out = (query_part * filtered.astype(jnp.float32)).astype(jnp.bfloat16)
    return lax.all_to_all(mixed_out, "mp", split_axis=0, concat_axis=1, tiled=True)


def solution(mesh):
    return jax.shard_map(
        shards,
        mesh=mesh,
        in_specs=(P(("ctx", "mp"), None, None), P(), P("mp", None), P("mp", None), P()),
        out_specs=P(("ctx", "mp"), None),
        check_vma=False,
    )
```

profile of v0, /device:TPU:1, one launch (start us, length us, event | category | flops | bytes accessed | tf_op | source)
XLA Modules:
  0.0 531.0 jit_solution(9122464082286298592)
XLA Ops:
  6.5 10.6 %copy.23 = bf16[32,3,8192]{0,1,2:T(4,128)(2,1)} copy(bf16[32,3,8192]{2,0,1:T(8,128)(2,1)} %param.7) | data formatting | bytes 3145728 | tf_op args[0]
  17.2 9.8 %reshape.117 = bf16[8,2,49152]{2,1,0:T(2,128)(2,1)} reshape(bf16[8192,3,32]{2,1,0:T(4,128)(2,1)} %bitcast.54) | data formatting | bytes 3145728
  27.0 6.0 %all-to-all-start = ((bf16[8,2,49152]{2,1,0:T(2,128)(2,1)}), bf16[8,2,49152]{2,1,0:T(2,128)(2,1)S(1)}, u32[]{:S(2)}, u32[]{:S(2)}) async-start(bf16[8,2,49152]{2,1,0:T(2,128)(2,1)} %reshape.117), calls=%async_computation | async-start | bytes 3145728 | tf_op jit(solution)/shard_map/all_to_all | solution.py:89
  33.4 1.5 constant_dynamic-slice_fusion.6
  35.1 21.0 %all-to-all-done = bf16[8,2,49152]{2,1,0:T(2,128)(2,1)S(1)} async-done(((bf16[8,2,49152]{2,1,0:T(2,128)(2,1)}), bf16[8,2,49152]{2,1,0:T(2,128)(2,1)S(1)}, u32[]{:S(2)}, u32[]{:S(2)}) %all-to-all-start) | async-done | bytes 1572896 | tf_op jit(solution)/shard_map/all_to_all | solution.py:89
  56.1 7.6 %reshape.118 = bf16[8192,3,32]{2,1,0:T(4,128)(2,1)} reshape(bf16[8,2,49152]{2,1,0:T(2,128)(2,1)S(1)} %all-to-all-done) | data formatting | bytes 3145728
  63.7 10.5 %copy.31 = bf16[32,3,8,1024]{3,0,2,1:T(8,128)(2,1)S(1)} copy(bf16[32,3,8,1024]{0,1,3,2:T(4,128)(2,1)} %bitcast.53) | data formatting | bytes 3145728 | tf_op jit(solution)/shard_map/all_to_all | solution.py:89
  74.2 6.2 %collective-permute-start = (bf16[6,3,1024]{2,0,1:T(8,128)(2,1)S(1)}, bf16[6,3,1024]{2,0,1:T(8,128)(2,1)S(1)}, u32[]{:S(2)}, u32[]{:S(2)}) collective-permute-start(bf16[6,3,1024]{2,0,1:T(8,128)(2,1)S(1)} %slice.125), channel_id=1, source_target_pairs={{0,8},{8,16},{16,24},{24,32},{32,40},{40,48},{48,56},{56,64},{64,7... | collective-permute-start | bytes 110600 | tf_op jit(solution)/shard_map/ppermute | solution.py:10
  81.4 3.9 multiply_add_fusion
  85.3 1.4 fusion.28
  86.8 138.6 %all-gather.3.cloned.1.call-done = bf16[8192,1,1024]{2,0,1:T(8,128)(2,1)} async-done(((bf16[256,1,1024]{2,0,1:T(8,128)(2,1)}), bf16[8192,1,1024]{2,0,1:T(8,128)(2,1)}) %all-gather.3.cloned.1.call-update) | async-done | bytes 16777232 | tf_op jit(solution)/shard_map/all_gather | solution.py:74
  225.4 282.1 %while.13 = (s32[]{:T(128)}, f32[256,16,64]{0,2,1:T(8,128)S(1)}, bf16[32,256,1024]{2,1,0:T(8,128)(2,1)}, s32[32]{0:T(128)S(1)}, f32[16,16]{1,0:T(8,128)S(1)}, /*...) while((s32[]{:T(128)}, f32[256,16,64]{0,2,1:T(8,128)S(1)}, ...), condition=%wide.region_3.4_spmd.clone, body=%wide.region_2.3_spmd.clone.sunk | while | flops 477169920 | bytes 20127888 | solution.py:83
  227.4 1.1 constant_dynamic-slice_fusion.9
  228.7 3.7 fusion.42
  236.2 1.1 constant_dynamic-slice_fusion.9
  237.5 3.7 fusion.42
  245.0 1.1 constant_dynamic-slice_fusion.9
  246.3 3.7 fusion.42
  253.8 1.1 constant_dynamic-slice_fusion.9
  255.1 3.7 fusion.42
  263.9 3.7 fusion.42
  272.8 3.7 fusion.42
  281.6 3.7 fusion.42
  290.4 3.7 fusion.42
  297.9 1.1 constant_dynamic-slice_fusion.9
  299.2 3.7 fusion.42
  306.7 1.1 constant_dynamic-slice_fusion.9
  308.0 3.7 fusion.42
  315.6 1.1 constant_dynamic-slice_fusion.9
  316.8 3.7 fusion.42
  324.4 1.1 constant_dynamic-slice_fusion.9
  325.7 3.7 fusion.42
  333.2 1.1 constant_dynamic-slice_fusion.9
  334.5 3.7 fusion.42
  342.0 1.1 constant_dynamic-slice_fusion.9
  343.3 3.7 fusion.42
  352.1 3.7 fusion.42
  360.9 3.7 fusion.42
  369.7 3.7 fusion.42
  378.6 3.7 fusion.42
  386.1 1.1 constant_dynamic-slice_fusion.9
  387.4 3.7 fusion.42
  394.9 1.1 constant_dynamic-slice_fusion.9
  396.2 3.7 fusion.42
  403.7 1.1 constant_dynamic-slice_fusion.9
  405.0 3.7 fusion.42
  412.5 1.1 constant_dynamic-slice_fusion.9
  413.8 3.7 fusion.42
  421.4 1.1 constant_dynamic-slice_fusion.9
  422.7 3.7 fusion.42
  431.5 3.7 fusion.42
  440.3 3.7 fusion.42
  449.1 3.7 fusion.42
  457.9 3.7 fusion.42
  465.4 1.1 constant_dynamic-slice_fusion.9
  466.7 3.7 fusion.42
  474.3 1.1 constant_dynamic-slice_fusion.9
  475.6 3.7 fusion.42
  484.4 3.7 fusion.42
  493.2 3.7 fusion.42
  502.0 3.7 fusion.42
  507.6 1.3 copy.28
  509.5 1.4 multiply_convert_fusion
  510.8 12.5 %all_to_all.34 = bf16[8,32,1024]{2,1,0:T(8,128)(2,1)S(1)} all-to-all(bf16[8,32,1024]{2,1,0:T(8,128)(2,1)S(1)} %multiply_convert_fusion), channel_id=1, replica_groups=mesh['ctx'=32,'mp'=8] {'mp'}, dimensions={0} | all-to-all | bytes 1048576 | tf_op jit(solution)/shard_map/all_to_all | solution.py:109
  (268 shorter events, 145.2 us)
Async XLA Ops:
  27.0 6.1 %copy-start.2 = (s32[64]{0:T(128)S(1)}, s32[64]{0:T(128)}, u32[]{:S(2)}) copy-start(s32[64]{0:T(128)} %param.11) | copy-start | bytes 772
  27.0 29.1 %all-to-all-start = ((bf16[8,2,49152]{2,1,0:T(2,128)(2,1)}), bf16[8,2,49152]{2,1,0:T(2,128)(2,1)S(1)}, u32[]{:S(2)}, u32[]{:S(2)}) async-start(bf16[8,2,49152]{2,1,0:T(2,128)(2,1)} %reshape.117), calls=%async_computation | async-start | bytes 3145728 | tf_op jit(solution)/shard_map/all_to_all | solution.py:89
  32.9 192.4 %all-gather.3.cloned.1.call-start = ((), (), s32[]{:S(2)}) async-start(), calls=%async_computation.2 | async-start | bytes 17301504 | tf_op jit(solution)/shard_map/all_gather | solution.py:74
  74.2 7.1 %collective-permute-start = (bf16[6,3,1024]{2,0,1:T(8,128)(2,1)S(1)}, bf16[6,3,1024]{2,0,1:T(8,128)(2,1)S(1)}, u32[]{:S(2)}, u32[]{:S(2)}) collective-permute-start(bf16[6,3,1024]{2,0,1:T(8,128)(2,1)S(1)} %slice.125), channel_id=1, source_target_pairs={{0,8},{8,16},{16,24},{24,32},{32,40},{40,48},{48,56},{56,64},{64,7... | collective-permute-start | bytes 110600 | tf_op jit(solution)/shard_map/ppermute | solution.py:10
  85.3 1.4 copy-start
  85.3 1.4 copy-start.1
Sparse Core Ops, SparseCore 0:
  86.9 138.4 all-gather.2
where the time goes:
time: 534 us; the launch traced here: 531 us
  matrix products  175 us (33%)
  waiting for transfers between devices  160 us (30%)
  local copies, waits for them, and re-layouts  103 us (19%)
  other arithmetic  52.4 us (10%)
  between operations  13.6 us (3%)
  blocking collectives  12.5 us (2%)
  starting transfers between devices  12.2 us (2%)
    all_gather x1, waiting for transfers between devices, long_filter(): piece_rows = lax.all_gather(product, 'ctx', axis=0, tiled=True)  139 us
    dot_general x32, matrix products, filter_tile(): jnp.einsum('ejz,ejx->ezx', left_neighbor, right_neighbor, precision=lax.P...  119 us
    dynamic_slice x96, local copies, waits for them, and re-layouts, long_filter(): result, unused = lax.scan(scan_step, initial, (stacked, starts))  59.9 us
    dot_general x32, matrix products, split_product(): jnp.einsum(form, lower_part, inputs, preferred_element_type=jnp.float32)  31.6 us
    unnamed x13, local copies, waits for them, and re-layouts  28.1 us
    dot_general x32, matrix products, split_product(): jnp.einsum(form, upper_part, inputs, preferred_element_type=jnp.float32)  23.8 us
    all_to_all x1, waiting for transfers between devices, shards(): lax.all_to_all(proj, 'mp', split_axis=2, concat_axis=0, tiled=True)  21 us
    sub x32, other arithmetic, filter_tile(): span - in_offsets  20.9 us
  transfers between devices with their start and end apart: 3, of which 3 were waited for; matrix products, arithmetic and copies ran while one was open for 0% of the time, Pallas kernels for 0%

commit v1 on v0

v1 whole, which is shorter than its diff:
```python
import jax
import jax.numpy as jnp
from jax import lax
from jax.sharding import PartitionSpec as P

HIGHEST = lax.Precision.HIGHEST


def shifted(block, axis, distance):
    count = lax.axis_size(axis)
    route = [(i, i + distance) for i in range(count - distance)]
    return lax.ppermute(block, axis, route)


def document_number_index(doc_lengths, positions):
    doc_starts = jnp.cumsum(doc_lengths) - doc_lengths
    inside = (doc_starts[None, :] <= positions[:, None]).astype(jnp.int32)
    return jnp.sum(inside, axis=1) - 1


def short_convolution(padded, conv_weight, padded_document_ids, padded_pos, out_rows):
    kernel_len = conv_weight.shape[1]
    result = jnp.zeros((out_rows,) + padded.shape[1:], jnp.float32)
    own_docs = padded_document_ids[kernel_len - 1 :]
    for position_shift in range(kernel_len):
        begin_row = kernel_len - 1 - position_shift
        earlier = padded[begin_row : begin_row + out_rows].astype(jnp.float32)
        keep_mask = (padded_document_ids[begin_row : begin_row + out_rows] == own_docs) & (
            padded_pos[begin_row : begin_row + out_rows] >= 0
        )
        result = (
            result
            + conv_weight[:, position_shift, :][None]
            * earlier
            * keep_mask.astype(jnp.float32)[:, None, None]
        )
    return result


def split_product(form, weights, inputs):
    upper_part = weights.astype(jnp.bfloat16)
    lower_part = (weights - upper_part.astype(jnp.float32)).astype(jnp.bfloat16)
    first = jnp.einsum(form, upper_part, inputs, preferred_element_type=jnp.float32)
    return first + jnp.einsum(form, lower_part, inputs, preferred_element_type=jnp.float32)


def long_filter(product, residues, decays):
    block_len, channels = product.shape
    group_count = residues.shape[0]
    group_width = channels // group_count
    coefficient = residues * jnp.sqrt(decays)
    offsets = jnp.arange(block_len, dtype=jnp.float32)
    left = coefficient[:, None, :] * jnp.exp(-decays[:, None, :] * offsets[None, :, None])
    right = jnp.exp(decays[:, :, None] * offsets[None, None, :])
    tile = jnp.einsum("grm,gms->grs", left, right, precision=HIGHEST)
    lag = jnp.arange(block_len)[:, None] - jnp.arange(block_len)[None, :]
    tile = jnp.where((lag >= 0)[None], tile, 0.0)
    inputs = product.reshape(block_len, group_count, group_width)
    intra = split_product("grs,sgc->rgc", tile, inputs)

    end_weight = jnp.exp(-decays[:, :, None] * (float(block_len) - offsets)[None, None, :])
    local_state = split_product("gms,sgc->gmc", end_weight, inputs)

    state = shifted(local_state, "ctx", 1)
    count = lax.axis_size("ctx")
    distance = 1
    while distance < count:
        decay_k = jnp.exp(-decays * float(block_len * distance))
        state = state + decay_k[:, :, None] * shifted(state, "ctx", distance)
        distance *= 2

    inter = jnp.einsum("grm,gmc->rgc", left, state, precision=HIGHEST)
    return (intra + inter).reshape(block_len, channels).astype(jnp.bfloat16)


def shards(proj, conv_weight, residues, decays, doc_lengths):
    kernel_len = conv_weight.shape[1]
    rows = proj.shape[0]
    lin_axis = ("ctx", "mp")
    tail_rows = shifted(proj[rows - (kernel_len - 1) :], lin_axis, 1)
    lin_index = lax.axis_index("ctx") * lax.axis_size("mp") + lax.axis_index("mp")
    padded_pos = lin_index * rows - (kernel_len - 1) + jnp.arange(rows + kernel_len - 1, dtype=jnp.int32)
    padded_document_ids = document_number_index(doc_lengths, padded_pos)
    padded = jnp.concatenate([tail_rows, proj], axis=0)
    conv = short_convolution(padded, conv_weight, padded_document_ids, padded_pos, rows)
    query_part = conv[:, 0]
    product = (conv[:, 1] * conv[:, 2]).astype(jnp.bfloat16)
    channel_rows = lax.all_to_all(product, "mp", split_axis=1, concat_axis=0, tiled=True)
    filtered = long_filter(channel_rows, residues, decays)
    filtered = lax.all_to_all(filtered, "mp", split_axis=0, concat_axis=1, tiled=True)
    return (query_part * filtered.astype(jnp.float32)).astype(jnp.bfloat16)


def solution(mesh):
    return jax.shard_map(
        shards,
        mesh=mesh,
        in_specs=(P(("ctx", "mp"), None, None), P(), P("mp", None), P("mp", None), P()),
        out_specs=P(("ctx", "mp"), None),
        check_vma=False,
    )
```

time: 534 us -> 119 us (0.22)
  the two profiles are of different devices: /device:TPU:1 before, /device:TPU:160 now
where the time goes in v1:
time: 119 us; the launch traced here: 118 us
  waiting for transfers between devices  49.6 us (42%)
  starting transfers between devices  22.5 us (19%)
  blocking collectives  17.8 us (15%)
  local copies, waits for them, and re-layouts  12.9 us (11%)
  other arithmetic  7.89 us (7%)
  matrix products  7.16 us (6%)
    ppermute x7, waiting for transfers between devices, shifted(): return lax.ppermute(block, axis, route)  39.8 us
    ppermute x7, starting transfers between devices, shifted(): return lax.ppermute(block, axis, route)  17.9 us
    all_to_all x1, blocking collectives, shards(): lax.all_to_all(filtered, 'mp', split_axis=0, concat_axis=1, tiled=True)  17.8 us
    all_to_all x1, waiting for transfers between devices, shards(): lax.all_to_all(product, 'mp', split_axis=1, concat_axis=0, tiled=True)  9.78 us
    all_to_all x1, starting transfers between devices, shards(): lax.all_to_all(product, 'mp', split_axis=1, concat_axis=0, tiled=True)  4.64 us
    slice x1, local copies, waits for them, and re-layouts, short_convolution(): conv_weight[:, position_shift, :][None] * earlier  4.23 us
    add x1, other arithmetic, short_convolution(): result + conv_weight[:, position_shift, :][None] * earlier * keep_mask.as...  3.98 us
    dot_general x1, matrix products, long_filter(): tile = jnp.einsum('grm,gms->grs', left, right, precision=HIGHEST)  3.73 us
  transfers between devices with their start and end apart: 8, of which 8 were waited for; matrix products, arithmetic and copies ran while one was open for 10% of the time, Pallas kernels for 0%

profile of v1, /device:TPU:160, one launch (start us, length us, event | category | flops | bytes accessed | tf_op | source)
XLA Modules:
  0.0 118.2 jit_solution(12967393498618984382)
XLA Ops:
  0.0 0.0 copy-start.1
  0.0 1.2 %slice.97 = bf16[6,3,8192]{2,0,1:T(8,128)(2,1)S(1)} slice(bf16[32,3,8192]{2,0,1:T(8,128)(2,1)} %param.5), slice={[26:32], [0:3], [0:8192]} | slice | bytes 589824 | tf_op jit(solution)/shard_map/slice | solution.py:80
  1.2 3.5 %collective-permute-start = (bf16[6,3,8192]{2,0,1:T(8,128)(2,1)S(1)}, bf16[6,3,8192]{2,0,1:T(8,128)(2,1)S(1)}, u32[]{:S(2)}, u32[]{:S(2)}) collective-permute-start(bf16[6,3,8192]{2,0,1:T(8,128)(2,1)S(1)} %slice.97), channel_id=1, source_target_pairs={{0,1},{1,2},{2,3},{3,4},{4,5},{5,6},{6,7},{7,8},{8,9},{9,10},{10,1... | collective-permute-start | bytes 884744 | tf_op jit(solution)/shard_map/ppermute | solution.py:12
  4.7 0.7 copy.24
  5.5 0.1 reduce-window.9
  5.6 0.1 reduce
  5.7 0.7 sub.44
  6.3 4.2 %fusion.38 = (f32[3,1,8192]{2,1,0:T(1,128)S(1)}, f32[3,1,8192]{2,1,0:T(1,128)S(1)}, f32[3,1,8192]{2,1,0:T(1,128)S(1)}, f32[3,1,8192]{2,1,0:T(1,128)S(1)}, f32[3,...) fusion(f32[3,7,8192]{2,1,0:T(8,128)} %param.6), kind=kLoop, calls=%fused_computation.88 | loop fusion | bytes 1376256 | tf_op jit(solution)/shard_map/slice | solution.py:33
  10.6 0.2 convert_reduce_fusion
  10.8 0.1 copy_bitcast_fusion
  10.9 0.1 copy_bitcast_fusion.2
  11.0 0.1 copy_bitcast_fusion.4
  11.2 0.1 copy.48
  11.3 0.1 and_convert_fusion.5
  11.4 3.3 %collective-permute-done = bf16[6,3,8192]{2,0,1:T(8,128)(2,1)S(1)} collective-permute-done((bf16[6,3,8192]{2,0,1:T(8,128)(2,1)S(1)}, bf16[6,3,8192]{2,0,1:T(8,128)(2,1)S(1)}, u32[]{:S(2)}, u32[]{:S(2)}) %collective-permute-start) | collective-permute-done | bytes 294944 | tf_op jit(solution)/shard_map/ppermute | solution.py:12
  14.6 0.0 copy-done.1
  14.6 4.0 %multiply_add_fusion = f32[32,3,8192]{2,0,1:T(8,128)S(1)} fusion(bf16[32,3,8192]{2,0,1:T(8,128)(2,1)S(1)} %copy-done.1, bf16[6,3,8192]{2,0,1:T(8,128)(2,1)S(1)} %collective-permute-done, f32[32]{0:T(128)S(1)} %get-tuple-element.20, f32[3,8192]{1,0:T(4,128)S(1)} %get-tuple-element.26, f32[32]{0:T(128)S(1)} %get-tuple-element.21, ...), kind=kLoop, calls=%fused_computation.7 | loop fusion | flops 35389440 | bytes 5702528 | tf_op jit(solution)/shard_map/add | solution.py:32
  18.6 0.0 copy-start
  18.6 1.6 %copy-done = f32[32,3,8192]{2,0,1:T(8,128)} copy-done((f32[32,3,8192]{2,0,1:T(8,128)}, f32[32,3,8192]{2,0,1:T(8,128)S(1)}, u32[]{:S(2)}) %copy-start) | copy-done | bytes 3145752
  20.3 0.0 copy-start.2
  20.3 0.0 copy-start.3
  20.3 0.1 fusion.14
  20.4 0.3 copy.40
  20.7 1.1 copy.25
  21.7 4.6 %all-to-all-start = ((bf16[32,8,1024]{2,0,1:T(8,128)(2,1)}), bf16[32,8,1024]{2,0,1:T(8,128)(2,1)S(1)}, u32[]{:S(2)}, u32[]{:S(2)}) async-start(bf16[32,8,1024]{2,0,1:T(8,128)(2,1)} %copy.25), calls=%async_computation | async-start | bytes 1048576 | tf_op jit(solution)/shard_map/all_to_all | solution.py:88
  26.4 0.0 copy-done.2
  26.4 0.0 copy-done.3
  26.4 9.8 %all-to-all-done = bf16[32,8,1024]{2,0,1:T(8,128)(2,1)S(1)} async-done(((bf16[32,8,1024]{2,0,1:T(8,128)(2,1)}), bf16[32,8,1024]{2,0,1:T(8,128)(2,1)S(1)}, u32[]{:S(2)}, u32[]{:S(2)}) %all-to-all-start) | async-done | bytes 524320 | tf_op jit(solution)/shard_map/all_to_all | solution.py:88
  36.2 0.7 reshape.94
  36.9 0.8 copy.26
  37.7 0.3 fusion.22
  38.0 0.3 convolution_add_fusion.1
  38.3 1.9 %collective-permute-start.1 = (f32[16,16,64]{2,1,0:T(8,128)S(1)}, f32[16,16,64]{2,1,0:T(8,128)S(1)}, u32[]{:S(2)}, u32[]{:S(2)}) collective-permute-start(f32[16,16,64]{2,1,0:T(8,128)S(1)} %convolution_add_fusion.1), channel_id=1, source_target_pairs={{0,8},{8,16},{16,24},{24,32},{32,40},{40,48},{48,56},{56,64},{64,7... | collective-permute-start | bytes 196616 | tf_op jit(solution)/shard_map/ppermute | solution.py:12
  40.3 6.8 %collective-permute-done.1 = f32[16,16,64]{2,1,0:T(8,128)S(1)} collective-permute-done((f32[16,16,64]{2,1,0:T(8,128)S(1)}, f32[16,16,64]{2,1,0:T(8,128)S(1)}, u32[]{:S(2)}, u32[]{:S(2)}) %collective-permute-start.1) | collective-permute-done | bytes 65568 | tf_op jit(solution)/shard_map/ppermute | solution.py:12
  47.0 1.9 %collective-permute-start.2 = (f32[16,16,64]{2,1,0:T(8,128)S(1)}, f32[16,16,64]{2,1,0:T(8,128)S(1)}, u32[]{:S(2)}, u32[]{:S(2)}) collective-permute-start(f32[16,16,64]{2,1,0:T(8,128)S(1)} %collective-permute-done.1), channel_id=1, source_target_pairs={{0,8},{8,16},{16,24},{24,32},{32,40},{40,48},{48,56},{56,64},{64,7... | collective-permute-start | bytes 196616 | tf_op jit(solution)/shard_map/ppermute | solution.py:12
  49.0 6.8 %collective-permute-done.2 = f32[16,16,64]{2,1,0:T(8,128)S(1)} collective-permute-done((f32[16,16,64]{2,1,0:T(8,128)S(1)}, f32[16,16,64]{2,1,0:T(8,128)S(1)}, u32[]{:S(2)}, u32[]{:S(2)}) %collective-permute-start.2) | collective-permute-done | bytes 65568 | tf_op jit(solution)/shard_map/ppermute | solution.py:12
  55.7 0.1 multiply_add_fusion.4
  55.8 4.3 %collective-permute-start.3 = (f32[16,16,64]{2,1,0:T(8,128)S(1)}, f32[16,16,64]{2,1,0:T(8,128)S(1)}, u32[]{:S(2)}, u32[]{:S(2)}) collective-permute-start(f32[16,16,64]{2,1,0:T(8,128)S(1)} %multiply_add_fusion.4), channel_id=1, source_target_pairs={{0,16},{8,24},{16,32},{24,40},{32,48},{40,56},{48,64},{56,72},{64,... | collective-permute-start | bytes 196616 | tf_op jit(solution)/shard_map/ppermute | solution.py:12
  60.1 3.7 %fusion.18 = f32[16,256,256]{2,1,0:T(8,128)S(1)} fusion(f32[16,16]{1,0:T(8,128)S(1)} %copy-done.2, f32[16,16]{1,0:T(8,128)S(1)} %get-tuple-element.18, f32[16,16]{1,0:T(8,128)S(1)} %get-tuple-element.17), kind=kOutput, calls=%fused_computation.39 | convolution fusion | flops 201523200 | bytes 4197376 | tf_op jit(solution)/shard_map/grm,gms->grs/dot_general | solution.py:55
  63.8 1.3 %collective-permute-done.3 = f32[16,16,64]{2,1,0:T(8,128)S(1)} collective-permute-done((f32[16,16,64]{2,1,0:T(8,128)S(1)}, f32[16,16,64]{2,1,0:T(8,128)S(1)}, u32[]{:S(2)}, u32[]{:S(2)}) %collective-permute-start.3) | collective-permute-done | bytes 65568 | tf_op jit(solution)/shard_map/ppermute | solution.py:12
  65.1 0.1 multiply_add_fusion.3
  65.2 2.9 %collective-permute-start.4 = (f32[16,16,64]{2,1,0:T(8,128)S(1)}, f32[16,16,64]{2,1,0:T(8,128)S(1)}, u32[]{:S(2)}, u32[]{:S(2)}) collective-permute-start(f32[16,16,64]{2,1,0:T(8,128)S(1)} %multiply_add_fusion.3), channel_id=1, source_target_pairs={{0,32},{8,40},{16,48},{24,56},{32,64},{40,72},{48,80},{56,88},{64,... | collective-permute-start | bytes 196616 | tf_op jit(solution)/shard_map/ppermute | solution.py:12
  68.2 6.9 %collective-permute-done.4 = f32[16,16,64]{2,1,0:T(8,128)S(1)} collective-permute-done((f32[16,16,64]{2,1,0:T(8,128)S(1)}, f32[16,16,64]{2,1,0:T(8,128)S(1)}, u32[]{:S(2)}, u32[]{:S(2)}) %collective-permute-start.4) | collective-permute-done | bytes 65568 | tf_op jit(solution)/shard_map/ppermute | solution.py:12
  75.1 0.1 multiply_add_fusion.2
  75.2 1.9 %collective-permute-start.5 = (f32[16,16,64]{2,1,0:T(8,128)S(1)}, f32[16,16,64]{2,1,0:T(8,128)S(1)}, u32[]{:S(2)}, u32[]{:S(2)}) collective-permute-start(f32[16,16,64]{2,1,0:T(8,128)S(1)} %multiply_add_fusion.2), channel_id=1, source_target_pairs={{0,64},{8,72},{16,80},{24,88},{32,96},{40,104},{48,112},{56,120},{... | collective-permute-start | bytes 196616 | tf_op jit(solution)/shard_map/ppermute | solution.py:12
  77.1 0.8 fusion
  77.9 6.4 %collective-permute-done.5 = f32[16,16,64]{2,1,0:T(8,128)S(1)} collective-permute-done((f32[16,16,64]{2,1,0:T(8,128)S(1)}, f32[16,16,64]{2,1,0:T(8,128)S(1)}, u32[]{:S(2)}, u32[]{:S(2)}) %collective-permute-start.5) | collective-permute-done | bytes 65568 | tf_op jit(solution)/shard_map/ppermute | solution.py:12
  84.2 0.1 multiply_add_fusion.1
  84.3 1.5 %collective-permute-start.6 = (f32[16,16,64]{2,1,0:T(8,128)S(1)}, f32[16,16,64]{2,1,0:T(8,128)S(1)}, u32[]{:S(2)}, u32[]{:S(2)}) collective-permute-start(f32[16,16,64]{2,1,0:T(8,128)S(1)} %multiply_add_fusion.1), channel_id=1, source_target_pairs={{0,128},{8,136},{16,144},{24,152},{32,160},{40,168},{48,176},{56,1... | collective-permute-start | bytes 196616 | tf_op jit(solution)/shard_map/ppermute | solution.py:12
  85.8 0.8 fusion.11
  86.6 8.5 %collective-permute-done.6 = f32[16,16,64]{2,1,0:T(8,128)S(1)} collective-permute-done((f32[16,16,64]{2,1,0:T(8,128)S(1)}, f32[16,16,64]{2,1,0:T(8,128)S(1)}, u32[]{:S(2)}, u32[]{:S(2)}) %collective-permute-start.6) | collective-permute-done | bytes 65568 | tf_op jit(solution)/shard_map/ppermute | solution.py:12
  95.1 1.3 %fusion.13 = bf16[256,16,64]{0,2,1:T(8,128)(2,1)S(1)} fusion(f32[16,64,256]{2,1,0:T(8,128)S(1)} %fusion.11, f32[16,16,64]{2,1,0:T(8,128)S(1)} %multiply_add_fusion.1, f32[16,16,64]{2,1,0:T(8,128)S(1)} %collective-permute-done.6, f32[16,16]{1,0:T(8,128)S(1)} %get-tuple-element.18, f32[16,16]{1,0:T(8,128)S(1)} %get-tuple-element.17, ...), kind=kOutput, calls=%fused_computation.28 | convolution fusion | flops 51019776 | bytes 1707008 | tf_op jit(solution)/shard_map/grm,gmc->rgc/dot_general | solution.py:72
  96.4 1.0 copy.30
  97.3 0.7 convert_element_type.117
  98.1 17.8 %all_to_all.23 = bf16[8,32,1024]{2,1,0:T(8,128)(2,1)S(1)} all-to-all(bf16[8,32,1024]{2,1,0:T(8,128)(2,1)S(1)} %convert_element_type.117), channel_id=1, replica_groups=mesh['ctx'=32,'mp'=8] {'mp'}, dimensions={0} | all-to-all | bytes 1048576 | tf_op jit(solution)/shard_map/all_to_all | solution.py:90
  115.9 0.1 convert_bitcast_fusion
  116.0 0.1 copy.39
  116.1 2.1 %fusion.16 = bf16[32,8192]{1,0:T(8,128)(2,1)} fusion(f32[32,8192]{1,0:T(8,128)S(1)} %bitcast.37, f32[32,3,8192]{2,0,1:T(8,128)} %copy-done), kind=kLoop, calls=%fused_computation.34 | loop fusion | flops 524288 | bytes 2621440 | tf_op jit(solution)/shard_map/convert_element_type | solution.py:91
  (5 shorter events, 0.1 us)
Async XLA Ops:
  0.0 14.6 %copy-start.1 = (bf16[32,3,8192]{2,0,1:T(8,128)(2,1)S(1)}, bf16[32,3,8192]{2,0,1:T(8,128)(2,1)}, u32[]{:S(2)}) copy-start(bf16[32,3,8192]{2,0,1:T(8,128)(2,1)} %param.5) | copy-start | bytes 4718596
  1.2 13.4 %collective-permute-start = (bf16[6,3,8192]{2,0,1:T(8,128)(2,1)S(1)}, bf16[6,3,8192]{2,0,1:T(8,128)(2,1)S(1)}, u32[]{:S(2)}, u32[]{:S(2)}) collective-permute-start(bf16[6,3,8192]{2,0,1:T(8,128)(2,1)S(1)} %slice.97), channel_id=1, source_target_pairs={{0,1},{1,2},{2,3},{3,4},{4,5},{5,6},{6,7},{7,8},{8,9},{9,10},{10,1... | collective-permute-start | bytes 884744 | tf_op jit(solution)/shard_map/ppermute | solution.py:12
  18.6 1.6 %copy-start = (f32[32,3,8192]{2,0,1:T(8,128)}, f32[32,3,8192]{2,0,1:T(8,128)S(1)}, u32[]{:S(2)}) copy-start(f32[32,3,8192]{2,0,1:T(8,128)S(1)} %multiply_add_fusion) | copy-start | bytes 9437188
  20.3 6.1 %copy-start.2 = (f32[16,16]{1,0:T(8,128)S(1)}, f32[16,16]{1,0:T(8,128)}, u32[]{:S(2)}) copy-start(f32[16,16]{1,0:T(8,128)} %param.8) | copy-start | bytes 3076
  20.3 6.2 %copy-start.3 = (f32[16,16]{1,0:T(8,128)S(1)}, f32[16,16]{1,0:T(8,128)}, u32[]{:S(2)}) copy-start(f32[16,16]{1,0:T(8,128)} %param.7) | copy-start | bytes 3076
  21.7 14.5 %all-to-all-start = ((bf16[32,8,1024]{2,0,1:T(8,128)(2,1)}), bf16[32,8,1024]{2,0,1:T(8,128)(2,1)S(1)}, u32[]{:S(2)}, u32[]{:S(2)}) async-start(bf16[32,8,1024]{2,0,1:T(8,128)(2,1)} %copy.25), calls=%async_computation | async-start | bytes 1048576 | tf_op jit(solution)/shard_map/all_to_all | solution.py:88
  38.3 8.7 %collective-permute-start.1 = (f32[16,16,64]{2,1,0:T(8,128)S(1)}, f32[16,16,64]{2,1,0:T(8,128)S(1)}, u32[]{:S(2)}, u32[]{:S(2)}) collective-permute-start(f32[16,16,64]{2,1,0:T(8,128)S(1)} %convolution_add_fusion.1), channel_id=1, source_target_pairs={{0,8},{8,16},{16,24},{24,32},{32,40},{40,48},{48,56},{56,64},{64,7... | collective-permute-start | bytes 196616 | tf_op jit(solution)/shard_map/ppermute | solution.py:12
  47.0 8.7 %collective-permute-start.2 = (f32[16,16,64]{2,1,0:T(8,128)S(1)}, f32[16,16,64]{2,1,0:T(8,128)S(1)}, u32[]{:S(2)}, u32[]{:S(2)}) collective-permute-start(f32[16,16,64]{2,1,0:T(8,128)S(1)} %collective-permute-done.1), channel_id=1, source_target_pairs={{0,8},{8,16},{16,24},{24,32},{32,40},{40,48},{48,56},{56,64},{64,7... | collective-permute-start | bytes 196616 | tf_op jit(solution)/shard_map/ppermute | solution.py:12
  55.8 9.3 %collective-permute-start.3 = (f32[16,16,64]{2,1,0:T(8,128)S(1)}, f32[16,16,64]{2,1,0:T(8,128)S(1)}, u32[]{:S(2)}, u32[]{:S(2)}) collective-permute-start(f32[16,16,64]{2,1,0:T(8,128)S(1)} %multiply_add_fusion.4), channel_id=1, source_target_pairs={{0,16},{8,24},{16,32},{24,40},{32,48},{40,56},{48,64},{56,72},{64,... | collective-permute-start | bytes 196616 | tf_op jit(solution)/shard_map/ppermute | solution.py:12
  65.2 9.9 %collective-permute-start.4 = (f32[16,16,64]{2,1,0:T(8,128)S(1)}, f32[16,16,64]{2,1,0:T(8,128)S(1)}, u32[]{:S(2)}, u32[]{:S(2)}) collective-permute-start(f32[16,16,64]{2,1,0:T(8,128)S(1)} %multiply_add_fusion.3), channel_id=1, source_target_pairs={{0,32},{8,40},{16,48},{24,56},{32,64},{40,72},{48,80},{56,88},{64,... | collective-permute-start | bytes 196616 | tf_op jit(solution)/shard_map/ppermute | solution.py:12
  75.2 9.1 %collective-permute-start.5 = (f32[16,16,64]{2,1,0:T(8,128)S(1)}, f32[16,16,64]{2,1,0:T(8,128)S(1)}, u32[]{:S(2)}, u32[]{:S(2)}) collective-permute-start(f32[16,16,64]{2,1,0:T(8,128)S(1)} %multiply_add_fusion.2), channel_id=1, source_target_pairs={{0,64},{8,72},{16,80},{24,88},{32,96},{40,104},{48,112},{56,120},{... | collective-permute-start | bytes 196616 | tf_op jit(solution)/shard_map/ppermute | solution.py:12
  84.3 10.8 %collective-permute-start.6 = (f32[16,16,64]{2,1,0:T(8,128)S(1)}, f32[16,16,64]{2,1,0:T(8,128)S(1)}, u32[]{:S(2)}, u32[]{:S(2)}) collective-permute-start(f32[16,16,64]{2,1,0:T(8,128)S(1)} %multiply_add_fusion.1), channel_id=1, source_target_pairs={{0,128},{8,136},{16,144},{24,152},{32,160},{40,168},{48,176},{56,1... | collective-permute-start | bytes 196616 | tf_op jit(solution)/shard_map/ppermute | solution.py:12

commit v2 on v1

--- a/solution.py
+++ b/solution.py
@@ -61,13 +61,17 @@
     end_weight = jnp.exp(-decays[:, :, None] * (float(block_len) - offsets)[None, None, :])
     local_state = split_product("gms,sgc->gmc", end_weight, inputs)
 
-    state = shifted(local_state, "ctx", 1)
-    count = lax.axis_size("ctx")
-    distance = 1
-    while distance < count:
-        decay_k = jnp.exp(-decays * float(block_len * distance))
-        state = state + decay_k[:, :, None] * shifted(state, "ctx", distance)
-        distance *= 2
+    gathered = lax.all_gather(local_state, "ctx", axis=0)
+    count = gathered.shape[0]
+    here = lax.axis_index("ctx")
+    earlier = jnp.arange(count, dtype=jnp.int32)
+    gap = (here - 1 - earlier).astype(jnp.float32) * float(block_len)
+    weight = jnp.where(
+        (earlier < here)[:, None, None],
+        jnp.exp(-decays[None] * jnp.maximum(gap, 0.0)[:, None, None]),
+        0.0,
+    )
+    state = jnp.sum(weight[:, :, :, None] * gathered, axis=0)
 
     inter = jnp.einsum("grm,gmc->rgc", left, state, precision=HIGHEST)
     return (intra + inter).reshape(block_len, channels).astype(jnp.bfloat16)

time: 119 us -> 165 us (1.39)
  the two profiles are of different devices: /device:TPU:160 before, /device:TPU:1 now
where the time goes in v2:
time: 165 us; the launch traced here: 164 us
  waiting for transfers between devices  96.9 us (59%)
  local copies, waits for them, and re-layouts  14.9 us (9%)
  between operations  13.7 us (8%)
  blocking collectives  12.5 us (8%)
  other arithmetic  10.6 us (6%)
  matrix products  7.82 us (5%)
  starting transfers between devices  7.74 us (5%)
    all_gather x1, waiting for transfers between devices, long_filter(): gathered = lax.all_gather(local_state, 'ctx', axis=0)  83 us
    all_to_all x1, blocking collectives, shards(): lax.all_to_all(filtered, 'mp', split_axis=0, concat_axis=1, tiled=True)  12.5 us
    all_to_all x1, waiting for transfers between devices, shards(): lax.all_to_all(product, 'mp', split_axis=1, concat_axis=0, tiled=True)  8.91 us
    ppermute x1, waiting for transfers between devices, shifted(): return lax.ppermute(block, axis, route)  4.98 us
    unnamed x17, local copies, waits for them, and re-layouts  4.5 us
    slice x1, local copies, waits for them, and re-layouts, short_convolution(): conv_weight[:, position_shift, :][None] * earlier  4.09 us
    ppermute x1, starting transfers between devices, shifted(): return lax.ppermute(block, axis, route)  4.02 us
    add x1, other arithmetic, short_convolution(): result + conv_weight[:, position_shift, :][None] * earlier * keep_mask.as...  3.98 us
  transfers between devices with their start and end apart: 3, of which 3 were waited for; matrix products, arithmetic and copies ran while one was open for 7% of the time, Pallas kernels for 0%

profile of v2, /device:TPU:1, one launch (start us, length us, event | category | flops | bytes accessed | tf_op | source)
XLA Modules:
  0.0 164.2 jit_solution(4188361015102338891)
XLA Ops:
  6.5 0.0 copy-start.3
  6.5 1.2 slice.97
  7.7 4.0 %collective-permute-start = (bf16[6,3,8192]{2,0,1:T(8,128)(2,1)S(1)}, bf16[6,3,8192]{2,0,1:T(8,128)(2,1)S(1)}, u32[]{:S(2)}, u32[]{:S(2)}) collective-permute-start(bf16[6,3,8192]{2,0,1:T(8,128)(2,1)S(1)} %slice.97), channel_id=1, source_target_pairs={{0,1},{1,2},{2,3},{3,4},{4,5},{5,6},{6,7},{7,8},{8,9},{9,10},{10,1... | collective-permute-start | bytes 884744 | tf_op jit(solution)/shard_map/ppermute | solution.py:12
  11.8 0.7 copy.32
  12.5 0.1 reduce-window.9
  12.6 0.1 reduce
  12.7 0.7 sub.57
  13.4 4.1 %fusion.37 = (f32[3,1,8192]{2,1,0:T(1,128)S(1)}, f32[3,1,8192]{2,1,0:T(1,128)S(1)}, f32[3,1,8192]{2,1,0:T(1,128)S(1)}, f32[3,1,8192]{2,1,0:T(1,128)S(1)}, f32[3,...) fusion(f32[3,7,8192]{2,1,0:T(8,128)} %param.6), kind=kLoop, calls=%fused_computation.81 | loop fusion | bytes 1376256 | tf_op jit(solution)/shard_map/slice | solution.py:33
  17.5 0.2 convert_reduce_fusion
  17.7 0.1 copy_bitcast_fusion.2
  17.8 0.1 copy_bitcast_fusion.4
  18.0 0.1 copy_bitcast_fusion
  18.1 0.1 copy.56
  18.2 0.1 and_convert_fusion.5
  18.3 5.0 %collective-permute-done = bf16[6,3,8192]{2,0,1:T(8,128)(2,1)S(1)} collective-permute-done((bf16[6,3,8192]{2,0,1:T(8,128)(2,1)S(1)}, bf16[6,3,8192]{2,0,1:T(8,128)(2,1)S(1)}, u32[]{:S(2)}, u32[]{:S(2)}) %collective-permute-start) | collective-permute-done | bytes 294944 | tf_op jit(solution)/shard_map/ppermute | solution.py:12
  23.3 0.0 copy-done.3
  23.3 4.0 %multiply_add_fusion = f32[32,3,8192]{2,0,1:T(8,128)S(1)} fusion(bf16[32,3,8192]{2,0,1:T(8,128)(2,1)S(1)} %copy-done.3, bf16[6,3,8192]{2,0,1:T(8,128)(2,1)S(1)} %collective-permute-done, f32[32]{0:T(128)S(1)} %get-tuple-element.15, f32[3,8192]{1,0:T(4,128)S(1)} %get-tuple-element.21, f32[32]{0:T(128)S(1)} %get-tuple-element.16, ...), kind=kLoop, calls=%fused_computation.8 | loop fusion | flops 35389440 | bytes 5702528 | tf_op jit(solution)/shard_map/add | solution.py:32
  27.3 0.0 copy-start.2
  27.3 1.7 %copy-done.2 = f32[32,3,8192]{2,0,1:T(8,128)} copy-done((f32[32,3,8192]{2,0,1:T(8,128)}, f32[32,3,8192]{2,0,1:T(8,128)S(1)}, u32[]{:S(2)}) %copy-start.2) | copy-done | bytes 3145752
  29.0 0.0 copy-start.4
  29.0 0.0 copy-start.5
  29.0 0.1 fusion.15
  29.1 0.3 copy.48
  29.4 1.1 copy.33
  30.5 3.5 %all-to-all-start = ((bf16[32,8,1024]{2,0,1:T(8,128)(2,1)}), bf16[32,8,1024]{2,0,1:T(8,128)(2,1)S(1)}, u32[]{:S(2)}, u32[]{:S(2)}) async-start(bf16[32,8,1024]{2,0,1:T(8,128)(2,1)} %copy.33), calls=%async_computation | async-start | bytes 1048576 | tf_op jit(solution)/shard_map/all_to_all | solution.py:92
  34.0 0.2 all-gather.3.cloned.1.call-start
  34.3 0.0 copy-done.4
  34.3 0.0 copy-done.5
  34.3 8.9 %all-to-all-done = bf16[32,8,1024]{2,0,1:T(8,128)(2,1)S(1)} async-done(((bf16[32,8,1024]{2,0,1:T(8,128)(2,1)}), bf16[32,8,1024]{2,0,1:T(8,128)(2,1)S(1)}, u32[]{:S(2)}, u32[]{:S(2)}) %all-to-all-start) | async-done | bytes 524320 | tf_op jit(solution)/shard_map/all_to_all | solution.py:92
  43.2 0.7 reshape.105
  43.9 0.8 copy.34
  44.7 0.3 fusion.24
  45.0 1.0 convolution_add_fusion
  46.0 0.0 all-gather.3.cloned.1.call-update
  46.1 0.1 exponential_select_fusion
  46.2 3.7 %fusion.19 = f32[16,256,256]{2,1,0:T(8,128)S(1)} fusion(f32[16,16]{1,0:T(8,128)S(1)} %copy-done.4, f32[16,16]{1,0:T(8,128)S(1)} %get-tuple-element.13, f32[16,16]{1,0:T(8,128)S(1)} %get-tuple-element.12), kind=kOutput, calls=%fused_computation.41 | convolution fusion | flops 201523200 | bytes 4197376 | tf_op jit(solution)/shard_map/grm,gms->grs/dot_general | solution.py:55
  50.0 0.0 copy-start
  50.0 2.0 %copy-done = f32[16,256,256]{2,1,0:T(8,128)} copy-done((f32[16,256,256]{2,1,0:T(8,128)}, f32[16,256,256]{2,1,0:T(8,128)S(1)}, u32[]{:S(2)}) %copy-start) | copy-done | bytes 4194328
  51.9 0.8 fusion
  52.7 83.0 %all-gather.3.cloned.1.call-done = f32[512,16,64]{2,1,0:T(8,128)} async-done(((f32[16,16,64]{2,1,0:T(8,128)}), f32[512,16,64]{2,1,0:T(8,128)}) %all-gather.3.cloned.1.call-update) | async-done | bytes 2097168 | tf_op jit(solution)/shard_map/all_gather | solution.py:64
  135.7 0.0 copy-start.1
  135.7 3.0 %multiply_reduce_fusion = f32[16,16,64]{2,1,0:T(8,128)S(1)} fusion(f32[32,16,16,64]{3,2,1,0:T(8,128)} %bitcast.39, f32[32,16,16]{2,1,0:T(8,128)S(1)} %exponential_select_fusion), kind=kLoop, calls=%fused_computation | loop fusion | flops 1032192 | bytes 2195456 | tf_op jit(solution)/shard_map/reduce_sum | solution.py:74
  138.7 1.2 fusion.23
  139.9 0.0 copy-done.1
  140.0 0.8 fusion.14
  140.8 1.0 copy.38
  141.8 0.7 convert_element_type.125
  142.5 12.5 %all_to_all.23 = bf16[8,32,1024]{2,1,0:T(8,128)(2,1)S(1)} all-to-all(bf16[8,32,1024]{2,1,0:T(8,128)(2,1)S(1)} %convert_element_type.125), channel_id=1, replica_groups=mesh['ctx'=32,'mp'=8] {'mp'}, dimensions={0} | all-to-all | bytes 1048576 | tf_op jit(solution)/shard_map/all_to_all | solution.py:94
  155.0 0.1 convert_bitcast_fusion
  155.1 0.1 copy.47
  155.2 2.1 %fusion.17 = bf16[32,8192]{1,0:T(8,128)(2,1)} fusion(f32[32,8192]{1,0:T(8,128)S(1)} %bitcast.40, f32[32,3,8192]{2,0,1:T(8,128)} %copy-done.2), kind=kLoop, calls=%fused_computation.35 | loop fusion | flops 524288 | bytes 2621440 | tf_op jit(solution)/shard_map/convert_element_type | solution.py:95
  (7 shorter events, 0.1 us)
Async XLA Ops:
  6.5 16.8 %copy-start.3 = (bf16[32,3,8192]{2,0,1:T(8,128)(2,1)S(1)}, bf16[32,3,8192]{2,0,1:T(8,128)(2,1)}, u32[]{:S(2)}) copy-start(bf16[32,3,8192]{2,0,1:T(8,128)(2,1)} %param.5) | copy-start | bytes 4718596
  7.7 15.5 %collective-permute-start = (bf16[6,3,8192]{2,0,1:T(8,128)(2,1)S(1)}, bf16[6,3,8192]{2,0,1:T(8,128)(2,1)S(1)}, u32[]{:S(2)}, u32[]{:S(2)}) collective-permute-start(bf16[6,3,8192]{2,0,1:T(8,128)(2,1)S(1)} %slice.97), channel_id=1, source_target_pairs={{0,1},{1,2},{2,3},{3,4},{4,5},{5,6},{6,7},{7,8},{8,9},{9,10},{10,1... | collective-permute-start | bytes 884744 | tf_op jit(solution)/shard_map/ppermute | solution.py:12
  27.3 1.7 %copy-start.2 = (f32[32,3,8192]{2,0,1:T(8,128)}, f32[32,3,8192]{2,0,1:T(8,128)S(1)}, u32[]{:S(2)}) copy-start(f32[32,3,8192]{2,0,1:T(8,128)S(1)} %multiply_add_fusion) | copy-start | bytes 9437188
  29.0 5.2 %copy-start.4 = (f32[16,16]{1,0:T(8,128)S(1)}, f32[16,16]{1,0:T(8,128)}, u32[]{:S(2)}) copy-start(f32[16,16]{1,0:T(8,128)} %param.8) | copy-start | bytes 3076
  29.0 5.2 %copy-start.5 = (f32[16,16]{1,0:T(8,128)S(1)}, f32[16,16]{1,0:T(8,128)}, u32[]{:S(2)}) copy-start(f32[16,16]{1,0:T(8,128)} %param.7) | copy-start | bytes 3076
  30.5 12.7 %all-to-all-start = ((bf16[32,8,1024]{2,0,1:T(8,128)(2,1)}), bf16[32,8,1024]{2,0,1:T(8,128)(2,1)S(1)}, u32[]{:S(2)}, u32[]{:S(2)}) async-start(bf16[32,8,1024]{2,0,1:T(8,128)(2,1)} %copy.33), calls=%async_computation | async-start | bytes 1048576 | tf_op jit(solution)/shard_map/all_to_all | solution.py:92
  34.0 101.7 %all-gather.3.cloned.1.call-start = ((), (), s32[]{:S(2)}) async-start(), calls=%async_computation.2 | async-start | bytes 4325376 | tf_op jit(solution)/shard_map/all_gather | solution.py:64
  50.0 2.0 %copy-start = (f32[16,256,256]{2,1,0:T(8,128)}, f32[16,256,256]{2,1,0:T(8,128)S(1)}, u32[]{:S(2)}) copy-start(f32[16,256,256]{2,1,0:T(8,128)S(1)} %fusion.19) | copy-start | bytes 12582916
  135.7 4.2 %copy-start.1 = (f32[16,256,256]{2,1,0:T(8,128)S(1)}, f32[16,256,256]{2,1,0:T(8,128)}, u32[]{:S(2)}) copy-start(f32[16,256,256]{2,1,0:T(8,128)} %copy-done) | copy-start | bytes 12582916
Sparse Core Ops, SparseCore 0:
  46.1 89.5 all-gather.2

commit v3 on v1

--- a/solution.py
+++ b/solution.py
@@ -44,50 +44,59 @@
     return first + jnp.einsum(form, lower_part, inputs, preferred_element_type=jnp.float32)
 
 
-def long_filter(product, residues, decays):
-    block_len, channels = product.shape
-    group_count = residues.shape[0]
-    group_width = channels // group_count
-    coefficient = residues * jnp.sqrt(decays)
+def long_filter(product, coefficient, decays, block_len):
+    positions, channels = product.shape
+    block_count = positions // block_len
     offsets = jnp.arange(block_len, dtype=jnp.float32)
-    left = coefficient[:, None, :] * jnp.exp(-decays[:, None, :] * offsets[None, :, None])
-    right = jnp.exp(decays[:, :, None] * offsets[None, None, :])
-    tile = jnp.einsum("grm,gms->grs", left, right, precision=HIGHEST)
+    left = coefficient[None, :] * jnp.exp(-decays[None, :] * offsets[:, None])
+    right = jnp.exp(decays[:, None] * offsets[None, :])
+    tile = jnp.dot(left, right, precision=HIGHEST)
     lag = jnp.arange(block_len)[:, None] - jnp.arange(block_len)[None, :]
-    tile = jnp.where((lag >= 0)[None], tile, 0.0)
-    inputs = product.reshape(block_len, group_count, group_width)
-    intra = split_product("grs,sgc->rgc", tile, inputs)
+    tile = jnp.where(lag >= 0, tile, 0.0)
+    inputs = product.reshape(block_count, block_len, channels)
+    intra = split_product("rs,bsc->brc", tile, inputs)
 
-    end_weight = jnp.exp(-decays[:, :, None] * (float(block_len) - offsets)[None, None, :])
-    local_state = split_product("gms,sgc->gmc", end_weight, inputs)
+    end_weight = jnp.exp(-decays[:, None] * (float(block_len) - offsets)[None, :])
+    local_state = split_product("ms,bsc->mbc", end_weight, inputs)
 
-    state = shifted(local_state, "ctx", 1)
-    count = lax.axis_size("ctx")
-    distance = 1
-    while distance < count:
-        decay_k = jnp.exp(-decays * float(block_len * distance))
-        state = state + decay_k[:, :, None] * shifted(state, "ctx", distance)
-        distance *= 2
+    later = jnp.arange(block_count)[:, None]
+    earlier = jnp.arange(block_count)[None, :]
+    gap = jnp.maximum(later - 1 - earlier, 0).astype(jnp.float32) * float(block_len)
+    carry = jnp.where((earlier < later)[None], jnp.exp(-decays[:, None, None] * gap[None]), 0.0)
+    state = jnp.einsum("mab,mbc->mac", carry, local_state, precision=HIGHEST)
 
-    inter = jnp.einsum("grm,gmc->rgc", left, state, precision=HIGHEST)
-    return (intra + inter).reshape(block_len, channels).astype(jnp.bfloat16)
+    inter = jnp.einsum("rm,mbc->brc", left, state, precision=HIGHEST)
+    return (intra + inter).reshape(positions, channels).astype(jnp.bfloat16)
 
 
 def shards(proj, conv_weight, residues, decays, doc_lengths):
     kernel_len = conv_weight.shape[1]
     rows = proj.shape[0]
+    ctx_size = lax.axis_size("ctx")
+    mp_size = lax.axis_size("mp")
     lin_axis = ("ctx", "mp")
     tail_rows = shifted(proj[rows - (kernel_len - 1) :], lin_axis, 1)
-    lin_index = lax.axis_index("ctx") * lax.axis_size("mp") + lax.axis_index("mp")
+    lin_index = lax.axis_index("ctx") * mp_size + lax.axis_index("mp")
     padded_pos = lin_index * rows - (kernel_len - 1) + jnp.arange(rows + kernel_len - 1, dtype=jnp.int32)
     padded_document_ids = document_number_index(doc_lengths, padded_pos)
     padded = jnp.concatenate([tail_rows, proj], axis=0)
     conv = short_convolution(padded, conv_weight, padded_document_ids, padded_pos, rows)
     query_part = conv[:, 0]
     product = (conv[:, 1] * conv[:, 2]).astype(jnp.bfloat16)
-    channel_rows = lax.all_to_all(product, "mp", split_axis=1, concat_axis=0, tiled=True)
-    filtered = long_filter(channel_rows, residues, decays)
-    filtered = lax.all_to_all(filtered, "mp", split_axis=0, concat_axis=1, tiled=True)
+
+    swap_axis = ("mp", "ctx")
+    gathered = lax.all_to_all(product, swap_axis, split_axis=1, concat_axis=0, tiled=True)
+    width = gathered.shape[1]
+    gathered = gathered.reshape(mp_size, ctx_size, rows, width).transpose(1, 0, 2, 3)
+    gathered = gathered.reshape(ctx_size * mp_size * rows, width)
+    groups_here = residues.shape[0]
+    group_span = proj.shape[2] // mp_size // groups_here
+    local_group = lax.axis_index("ctx") * width // group_span
+    coefficient = residues[local_group] * jnp.sqrt(decays[local_group])
+    filtered = long_filter(gathered, coefficient, decays[local_group], 256)
+    filtered = filtered.reshape(ctx_size, mp_size, rows, width).transpose(1, 0, 2, 3)
+    filtered = filtered.reshape(ctx_size * mp_size * rows, width)
+    filtered = lax.all_to_all(filtered, swap_axis, split_axis=0, concat_axis=1, tiled=True)
     return (query_part * filtered.astype(jnp.float32)).astype(jnp.bfloat16)
 
 

time: 119 us -> 122 us (1.025)
  the two profiles are of different devices: /device:TPU:160 before, /device:TPU:1 now
where the time goes in v3:
time: 122 us; the launch traced here: 121 us
  local copies, waits for them, and re-layouts  40.4 us (33%)
  blocking collectives  25.9 us (21%)
  waiting for transfers between devices  24 us (20%)
  starting transfers between devices  17.8 us (15%)
  other arithmetic  9.49 us (8%)
  matrix products  3.69 us (3%)
    all_to_all x1, blocking collectives, shards(): lax.all_to_all(filtered, swap_axis, split_axis=0, concat_axis=1, tiled=True)  25.9 us
    all_to_all x1, waiting for transfers between devices, shards(): lax.all_to_all(product, swap_axis, split_axis=1, concat_axis=0, tiled=True)  19.1 us
    all_to_all x1, starting transfers between devices, shards(): lax.all_to_all(product, swap_axis, split_axis=1, concat_axis=0, tiled=True)  13.8 us
    unnamed x12, local copies, waits for them, and re-layouts  12.1 us
    convert_element_type x2, local copies, waits for them, and re-layouts, shards(): return (query_part * filtered.astype(jnp.float32)).astype(jnp.bfloat16)  7.87 us
    ppermute x1, waiting for transfers between devices, shifted(): return lax.ppermute(block, axis, route)  4.93 us
    convert_element_type x2, local copies, waits for them, and re-layouts, shards(): product = (conv[:, 1] * conv[:, 2]).astype(jnp.bfloat16)  4.33 us
    slice x1, local copies, waits for them, and re-layouts, short_convolution(): conv_weight[:, position_shift, :][None] * earlier  4.07 us
  transfers between devices with their start and end apart: 2, of which 2 were waited for; matrix products, arithmetic and copies ran while one was open for 7% of the time, Pallas kernels for 0%

profile of v3, /device:TPU:1, one launch (start us, length us, event | category | flops | bytes accessed | tf_op | source)
XLA Modules:
  0.0 121.5 jit_solution(13848348024659228065)
XLA Ops:
  0.0 0.0 copy-start.1
  0.0 1.2 slice.97
  1.2 4.0 %collective-permute-start = (bf16[6,3,8192]{2,0,1:T(8,128)(2,1)S(1)}, bf16[6,3,8192]{2,0,1:T(8,128)(2,1)S(1)}, u32[]{:S(2)}, u32[]{:S(2)}) collective-permute-start(bf16[6,3,8192]{2,0,1:T(8,128)(2,1)S(1)} %slice.97), channel_id=1, source_target_pairs={{0,1},{1,2},{2,3},{3,4},{4,5},{5,6},{6,7},{7,8},{8,9},{9,10},{10,1... | collective-permute-start | bytes 884744 | tf_op jit(solution)/shard_map/ppermute | solution.py:12
  5.3 0.1 compare_convert_fusion
  5.3 0.7 copy.21
  6.1 0.1 reduce-window.9
  6.2 0.1 reduce
  6.3 0.7 sub.63
  7.0 0.2 convert_reduce_fusion
  7.1 4.1 %fusion.49 = (f32[3,1,8192]{2,1,0:T(1,128)S(1)}, f32[3,1,8192]{2,1,0:T(1,128)S(1)}, f32[3,1,8192]{2,1,0:T(1,128)S(1)}, f32[3,1,8192]{2,1,0:T(1,128)S(1)}, f32[3,...) fusion(f32[3,7,8192]{2,1,0:T(8,128)} %param.6), kind=kLoop, calls=%fused_computation.94 | loop fusion | bytes 1376256 | tf_op jit(solution)/shard_map/slice | solution.py:33
  11.2 0.1 copy_bitcast_fusion.2
  11.4 0.1 copy_bitcast_fusion.4
  11.5 0.1 copy_bitcast_fusion
  11.7 0.1 copy.53
  11.7 0.1 and_convert_fusion.5
  11.8 4.9 %collective-permute-done = bf16[6,3,8192]{2,0,1:T(8,128)(2,1)S(1)} collective-permute-done((bf16[6,3,8192]{2,0,1:T(8,128)(2,1)S(1)}, bf16[6,3,8192]{2,0,1:T(8,128)(2,1)S(1)}, u32[]{:S(2)}, u32[]{:S(2)}) %collective-permute-start) | collective-permute-done | bytes 294944 | tf_op jit(solution)/shard_map/ppermute | solution.py:12
  16.8 0.0 copy-done.1
  16.8 4.0 %multiply_add_fusion = f32[32,3,8192]{2,0,1:T(8,128)S(1)} fusion(bf16[32,3,8192]{2,0,1:T(8,128)(2,1)S(1)} %copy-done.1, bf16[6,3,8192]{2,0,1:T(8,128)(2,1)S(1)} %collective-permute-done, f32[32]{0:T(128)S(1)} %get-tuple-element.16, f32[3,8192]{1,0:T(4,128)S(1)} %get-tuple-element.21, f32[32]{0:T(128)S(1)} %get-tuple-element.17, ...), kind=kLoop, calls=%fused_computation.6 | loop fusion | flops 35389440 | bytes 5702528 | tf_op jit(solution)/shard_map/add | solution.py:32
  20.7 0.0 copy-start
  20.8 1.7 %copy-done = f32[32,3,8192]{2,0,1:T(8,128)} copy-done((f32[32,3,8192]{2,0,1:T(8,128)}, f32[32,3,8192]{2,0,1:T(8,128)S(1)}, u32[]{:S(2)}) %copy-start) | copy-done | bytes 3145752
  22.4 0.1 fusion.8
  22.5 1.6 %convert_element_type.115 = bf16[32,256,32]{2,1,0:T(8,128)(2,1)S(1)} reshape(bf16[32,1,8192]{2,0,1:T(8,128)(2,1)S(1)} %fusion.8) | data formatting | bytes 1048576 | tf_op jit(solution)/shard_map/convert_element_type | solution.py:85
  24.2 2.7 %copy.54 = bf16[32,256,32]{2,0,1:T(8,128)(2,1)} copy(bf16[32,256,32]{2,1,0:T(8,128)(2,1)S(1)} %convert_element_type.115) | data formatting | bytes 1048576 | tf_op jit(solution)/shard_map/convert_element_type | solution.py:85
  26.9 4.3 %reshape.135 = bf16[256,2,512]{2,1,0:T(2,128)(2,1)} reshape(bf16[256,32,32]{2,1,0:T(8,128)(2,1)} %bitcast.73) | data formatting | bytes 1048576
  31.1 13.8 %all-to-all-start = ((bf16[256,2,512]{2,1,0:T(2,128)(2,1)}), bf16[256,2,512]{2,1,0:T(2,128)(2,1)S(1)}, u32[]{:S(2)}, u32[]{:S(2)}) async-start(bf16[256,2,512]{2,1,0:T(2,128)(2,1)} %reshape.135), calls=%async_computation | async-start | bytes 1048576 | tf_op jit(solution)/shard_map/all_to_all | solution.py:88
  44.9 0.7 bitcast_negate_fusion
  45.6 0.7 fusion.48
  46.4 0.1 convert_multiply_fusion
  46.4 0.5 convolution_select_fusion
  46.9 19.1 %all-to-all-done = bf16[256,2,512]{2,1,0:T(2,128)(2,1)S(1)} async-done(((bf16[256,2,512]{2,1,0:T(2,128)(2,1)}), bf16[256,2,512]{2,1,0:T(2,128)(2,1)S(1)}, u32[]{:S(2)}, u32[]{:S(2)}) %all-to-all-start) | async-done | bytes 524320 | tf_op jit(solution)/shard_map/all_to_all | solution.py:88
  66.0 1.0 reshape.136
  67.1 2.8 %copy.24 = bf16[32,8,32,32]{2,1,3,0:T(8,128)(2,1)} copy(bf16[32,8,32,32]{3,2,0,1:T(8,128)(2,1)S(1)} %bitcast.74) | data formatting | bytes 1048576 | tf_op jit(solution)/shard_map/transpose | solution.py:90
  69.9 3.1 %reshape_reshape.3 = bf16[32,256,32]{1,2,0:T(8,128)(2,1)S(1)} reshape(bf16[32,8,32,32]{2,1,3,0:T(8,128)(2,1)} %copy.24) | data formatting | bytes 1048576 | tf_op jit(solution)/shard_map/reshape;reshape | solution.py:56
  73.0 0.5 fusion.36
  73.5 0.5 convolution_add_fusion.1
  74.0 0.5 fusion.13
  74.5 1.1 fusion.11
  75.6 0.3 fusion.20
  75.9 0.3 fusion.7
  76.2 0.9 convert_element_type.125
  77.2 3.3 %copy.32 = bf16[8,32,32,32]{3,2,1,0:T(8,128)(2,1)} copy(bf16[8,32,32,32]{2,0,3,1:T(8,128)(2,1)S(1)} %bitcast.75) | data formatting | bytes 1048576 | tf_op jit(solution)/shard_map/all_to_all | solution.py:99
  80.4 3.6 %reshape.137 = bf16[256,2,512]{2,1,0:T(2,128)(2,1)S(1)} reshape(bf16[256,32,32]{2,1,0:T(8,128)(2,1)} %bitcast.76) | data formatting | bytes 1048576
  84.0 25.9 %all_to_all.26 = bf16[256,2,512]{2,1,0:T(2,128)(2,1)S(1)} all-to-all(bf16[256,2,512]{2,1,0:T(2,128)(2,1)S(1)} %reshape.137), channel_id=1, replica_groups=mesh['ctx'=32,'mp'=8] {'mp','ctx'}, dimensions={0} | all-to-all | bytes 1048576 | tf_op jit(solution)/shard_map/all_to_all | solution.py:99
  109.8 1.0 reshape.138
  110.9 0.6 convert_bitcast_fusion
  111.5 4.4 %copy.29 = f32[32,256,32]{2,1,0:T(8,128)} copy(f32[32,256,32]{2,0,1:T(8,128)S(1)} %convert_bitcast_fusion) | data formatting | bytes 2097152 | tf_op jit(solution)/shard_map/convert_element_type | solution.py:100
  115.9 3.5 %reshape.128 = f32[32,8192]{1,0:T(8,128)S(1)} reshape(f32[32,256,32]{2,1,0:T(8,128)} %copy.29) | data formatting | bytes 2097152 | tf_op jit(solution)/shard_map/convert_element_type | solution.py:100
  119.4 2.1 %fusion.10 = bf16[32,8192]{1,0:T(8,128)(2,1)} fusion(f32[32,8192]{1,0:T(8,128)S(1)} %reshape.128, f32[32,3,8192]{2,0,1:T(8,128)} %copy-done), kind=kLoop, calls=%fused_computation.28 | loop fusion | flops 524288 | bytes 2621440 | tf_op jit(solution)/shard_map/convert_element_type | solution.py:100
  (5 shorter events, 0.0 us)
Async XLA Ops:
  0.0 16.8 %copy-start.1 = (bf16[32,3,8192]{2,0,1:T(8,128)(2,1)S(1)}, bf16[32,3,8192]{2,0,1:T(8,128)(2,1)}, u32[]{:S(2)}) copy-start(bf16[32,3,8192]{2,0,1:T(8,128)(2,1)} %param.5) | copy-start | bytes 4718596
  1.2 15.5 %collective-permute-start = (bf16[6,3,8192]{2,0,1:T(8,128)(2,1)S(1)}, bf16[6,3,8192]{2,0,1:T(8,128)(2,1)S(1)}, u32[]{:S(2)}, u32[]{:S(2)}) collective-permute-start(bf16[6,3,8192]{2,0,1:T(8,128)(2,1)S(1)} %slice.97), channel_id=1, source_target_pairs={{0,1},{1,2},{2,3},{3,4},{4,5},{5,6},{6,7},{7,8},{8,9},{9,10},{10,1... | collective-permute-start | bytes 884744 | tf_op jit(solution)/shard_map/ppermute | solution.py:12
  20.7 1.7 %copy-start = (f32[32,3,8192]{2,0,1:T(8,128)}, f32[32,3,8192]{2,0,1:T(8,128)S(1)}, u32[]{:S(2)}) copy-start(f32[32,3,8192]{2,0,1:T(8,128)S(1)} %multiply_add_fusion) | copy-start | bytes 9437188
  31.1 34.9 %all-to-all-start = ((bf16[256,2,512]{2,1,0:T(2,128)(2,1)}), bf16[256,2,512]{2,1,0:T(2,128)(2,1)S(1)}, u32[]{:S(2)}, u32[]{:S(2)}) async-start(bf16[256,2,512]{2,1,0:T(2,128)(2,1)} %reshape.135), calls=%async_computation | async-start | bytes 1048576 | tf_op jit(solution)/shard_map/all_to_all | solution.py:88

commit v4 on v1

--- a/solution.py
+++ b/solution.py
@@ -61,13 +61,18 @@
     end_weight = jnp.exp(-decays[:, :, None] * (float(block_len) - offsets)[None, None, :])
     local_state = split_product("gms,sgc->gmc", end_weight, inputs)
 
-    state = shifted(local_state, "ctx", 1)
     count = lax.axis_size("ctx")
-    distance = 1
-    while distance < count:
-        decay_k = jnp.exp(-decays * float(block_len * distance))
-        state = state + decay_k[:, :, None] * shifted(state, "ctx", distance)
-        distance *= 2
+    radix = min(4, count)
+
+    def decay_of(distance):
+        return jnp.exp(-decays * float(block_len * distance))[:, :, None]
+
+    window = shifted(local_state, "ctx", 1)
+    for distance in range(2, radix + 1):
+        window = window + decay_of(distance - 1) * shifted(local_state, "ctx", distance)
+    state = window
+    for distance in range(radix, count, radix):
+        state = state + decay_of(distance) * shifted(window, "ctx", distance)
 
     inter = jnp.einsum("grm,gmc->rgc", left, state, precision=HIGHEST)
     return (intra + inter).reshape(block_len, channels).astype(jnp.bfloat16)

time: 119 us -> 115 us (0.966)
  the two profiles are of different devices: /device:TPU:160 before, /device:TPU:128 now
where the time goes in v4:
time: 115 us; the launch traced here: 114 us
  waiting for transfers between devices  36.5 us (32%)
  starting transfers between devices  32.9 us (29%)
  local copies, waits for them, and re-layouts  12.8 us (11%)
  blocking collectives  12.6 us (11%)
  matrix products  11.2 us (10%)
  other arithmetic  7.67 us (7%)
    ppermute x12, waiting for transfers between devices, shifted(): return lax.ppermute(block, axis, route)  32 us
    ppermute x12, starting transfers between devices, shifted(): return lax.ppermute(block, axis, route)  29.4 us
    all_to_all x1, blocking collectives, shards(): lax.all_to_all(filtered, 'mp', split_axis=0, concat_axis=1, tiled=True)  12.6 us
    dot_general x1, matrix products, long_filter(): tile = jnp.einsum('grm,gms->grs', left, right, precision=HIGHEST)  5.32 us
    all_to_all x1, waiting for transfers between devices, shards(): lax.all_to_all(product, 'mp', split_axis=1, concat_axis=0, tiled=True)  4.51 us
    slice x1, local copies, waits for them, and re-layouts, short_convolution(): conv_weight[:, position_shift, :][None] * earlier  4.06 us
    add x1, other arithmetic, short_convolution(): result + conv_weight[:, position_shift, :][None] * earlier * keep_mask.as...  3.98 us
    all_to_all x1, starting transfers between devices, shards(): lax.all_to_all(product, 'mp', split_axis=1, concat_axis=0, tiled=True)  3.49 us
  transfers between devices with their start and end apart: 13, of which 8 were waited for; matrix products, arithmetic and copies ran while one was open for 14% of the time, Pallas kernels for 0%

profile of v4, /device:TPU:128, one launch (start us, length us, event | category | flops | bytes accessed | tf_op | source)
XLA Modules:
  0.0 114.0 jit_solution(14495584161506968304)
XLA Ops:
  0.0 0.0 copy-start.2
  0.0 1.2 %slice.97 = bf16[6,3,8192]{2,0,1:T(8,128)(2,1)S(1)} slice(bf16[32,3,8192]{2,0,1:T(8,128)(2,1)} %param.5), slice={[26:32], [0:3], [0:8192]} | slice | bytes 589824 | tf_op jit(solution)/shard_map/slice | solution.py:85
  1.2 3.5 %collective-permute-start = (bf16[6,3,8192]{2,0,1:T(8,128)(2,1)S(1)}, bf16[6,3,8192]{2,0,1:T(8,128)(2,1)S(1)}, u32[]{:S(2)}, u32[]{:S(2)}) collective-permute-start(bf16[6,3,8192]{2,0,1:T(8,128)(2,1)S(1)} %slice.97), channel_id=1, source_target_pairs={{0,1},{1,2},{2,3},{3,4},{4,5},{5,6},{6,7},{7,8},{8,9},{9,10},{10,1... | collective-permute-start | bytes 884744 | tf_op jit(solution)/shard_map/ppermute | solution.py:12
  4.7 0.7 copy.24
  5.5 0.1 reduce-window.9
  5.6 0.1 reduce
  5.7 0.7 sub.44
  6.3 4.1 %fusion.56 = (f32[3,1,8192]{2,1,0:T(1,128)S(1)}, f32[3,1,8192]{2,1,0:T(1,128)S(1)}, f32[3,1,8192]{2,1,0:T(1,128)S(1)}, f32[3,1,8192]{2,1,0:T(1,128)S(1)}, f32[3,...) fusion(f32[3,7,8192]{2,1,0:T(8,128)} %param.6), kind=kLoop, calls=%fused_computation.108 | loop fusion | bytes 1376256 | tf_op jit(solution)/shard_map/slice | solution.py:33
  10.4 0.2 convert_reduce_fusion
  10.6 0.1 copy_bitcast_fusion
  10.7 0.1 copy_bitcast_fusion.2
  10.9 0.1 copy_bitcast_fusion.4
  11.0 0.1 copy.48
  11.1 0.1 and_convert_fusion.5
  11.2 4.6 %collective-permute-done = bf16[6,3,8192]{2,0,1:T(8,128)(2,1)S(1)} collective-permute-done((bf16[6,3,8192]{2,0,1:T(8,128)(2,1)S(1)}, bf16[6,3,8192]{2,0,1:T(8,128)(2,1)S(1)}, u32[]{:S(2)}, u32[]{:S(2)}) %collective-permute-start) | collective-permute-done | bytes 294944 | tf_op jit(solution)/shard_map/ppermute | solution.py:12
  15.8 0.0 copy-done.2
  15.8 4.0 %multiply_add_fusion = f32[32,3,8192]{2,0,1:T(8,128)S(1)} fusion(bf16[32,3,8192]{2,0,1:T(8,128)(2,1)S(1)} %copy-done.2, bf16[6,3,8192]{2,0,1:T(8,128)(2,1)S(1)} %collective-permute-done, f32[32]{0:T(128)S(1)} %get-tuple-element.25, f32[3,8192]{1,0:T(4,128)S(1)} %get-tuple-element.31, f32[32]{0:T(128)S(1)} %get-tuple-element.26, ...), kind=kLoop, calls=%fused_computation.7 | loop fusion | flops 35389440 | bytes 5702528 | tf_op jit(solution)/shard_map/add | solution.py:32
  19.8 0.0 copy-start.1
  19.8 1.7 %copy-done.1 = f32[32,3,8192]{2,0,1:T(8,128)} copy-done((f32[32,3,8192]{2,0,1:T(8,128)}, f32[32,3,8192]{2,0,1:T(8,128)S(1)}, u32[]{:S(2)}) %copy-start.1) | copy-done | bytes 3145752
  21.5 0.1 fusion.14
  21.6 0.3 copy.40
  21.9 1.1 copy.25
  23.0 3.5 %all-to-all-start = ((bf16[32,8,1024]{2,0,1:T(8,128)(2,1)}), bf16[32,8,1024]{2,0,1:T(8,128)(2,1)S(1)}, u32[]{:S(2)}, u32[]{:S(2)}) async-start(bf16[32,8,1024]{2,0,1:T(8,128)(2,1)} %copy.25), calls=%async_computation | async-start | bytes 1048576 | tf_op jit(solution)/shard_map/all_to_all | solution.py:93
  26.5 0.0 copy-done.3
  26.5 0.0 copy-done.4
  26.6 5.3 %fusion.18 = f32[16,256,256]{2,1,0:T(8,128)} fusion(f32[16,16]{1,0:T(8,128)S(1)} %copy-done.3, f32[16,16]{1,0:T(8,128)S(1)} %get-tuple-element.23, f32[16,16]{1,0:T(8,128)S(1)} %get-tuple-element.22), kind=kOutput, calls=%fused_computation.39 | convolution fusion | flops 201523200 | bytes 4197376 | tf_op jit(solution)/shard_map/grm,gms->grs/dot_general | solution.py:55
  31.9 4.5 %all-to-all-done = bf16[32,8,1024]{2,0,1:T(8,128)(2,1)S(1)} async-done(((bf16[32,8,1024]{2,0,1:T(8,128)(2,1)}), bf16[32,8,1024]{2,0,1:T(8,128)(2,1)S(1)}, u32[]{:S(2)}, u32[]{:S(2)}) %all-to-all-start) | async-done | bytes 524320 | tf_op jit(solution)/shard_map/all_to_all | solution.py:93
  36.4 0.7 reshape.99
  37.1 0.8 copy.26
  37.9 0.3 fusion.22
  38.2 0.3 convolution_add_fusion.1
  38.5 2.8 %collective-permute-start.4 = (f32[16,16,64]{2,1,0:T(8,128)S(1)}, f32[16,16,64]{2,1,0:T(8,128)S(1)}, u32[]{:S(2)}, u32[]{:S(2)}) collective-permute-start(f32[16,16,64]{2,1,0:T(8,128)S(1)} %convolution_add_fusion.1), channel_id=1, source_target_pairs={{0,32},{8,40},{16,48},{24,56},{32,64},{40,72},{48,80},{56,88},{64,... | collective-permute-start | bytes 196616 | tf_op jit(solution)/shard_map/ppermute | solution.py:12
  41.3 5.2 %collective-permute-start.3 = (f32[16,16,64]{2,1,0:T(8,128)S(1)}, f32[16,16,64]{2,1,0:T(8,128)S(1)}, u32[]{:S(2)}, u32[]{:S(2)}) collective-permute-start(f32[16,16,64]{2,1,0:T(8,128)S(1)} %convolution_add_fusion.1), channel_id=1, source_target_pairs={{0,24},{8,32},{16,40},{24,48},{32,56},{40,64},{48,72},{56,80},{64,... | collective-permute-start | bytes 196616 | tf_op jit(solution)/shard_map/ppermute | solution.py:12
  46.6 1.9 %collective-permute-start.1 = (f32[16,16,64]{2,1,0:T(8,128)S(1)}, f32[16,16,64]{2,1,0:T(8,128)S(1)}, u32[]{:S(2)}, u32[]{:S(2)}) collective-permute-start(f32[16,16,64]{2,1,0:T(8,128)S(1)} %convolution_add_fusion.1), channel_id=1, source_target_pairs={{0,8},{8,16},{16,24},{24,32},{32,40},{40,48},{48,56},{56,64},{64,7... | collective-permute-start | bytes 196616 | tf_op jit(solution)/shard_map/ppermute | solution.py:12
  48.5 3.8 %collective-permute-start.2 = (f32[16,16,64]{2,1,0:T(8,128)S(1)}, f32[16,16,64]{2,1,0:T(8,128)S(1)}, u32[]{:S(2)}, u32[]{:S(2)}) collective-permute-start(f32[16,16,64]{2,1,0:T(8,128)S(1)} %convolution_add_fusion.1), channel_id=1, source_target_pairs={{0,16},{8,24},{16,32},{24,40},{32,48},{40,56},{48,64},{56,72},{64,... | collective-permute-start | bytes 196616 | tf_op jit(solution)/shard_map/ppermute | solution.py:12
  52.4 0.0 collective-permute-done.4
  52.4 0.0 collective-permute-done.3
  52.4 4.1 %collective-permute-done.1 = f32[16,16,64]{2,1,0:T(8,128)S(1)} collective-permute-done((f32[16,16,64]{2,1,0:T(8,128)S(1)}, f32[16,16,64]{2,1,0:T(8,128)S(1)}, u32[]{:S(2)}, u32[]{:S(2)}) %collective-permute-start.1) | collective-permute-done | bytes 65568 | tf_op jit(solution)/shard_map/ppermute | solution.py:12
  56.5 3.9 %collective-permute-done.2 = f32[16,16,64]{2,1,0:T(8,128)S(1)} collective-permute-done((f32[16,16,64]{2,1,0:T(8,128)S(1)}, f32[16,16,64]{2,1,0:T(8,128)S(1)}, u32[]{:S(2)}, u32[]{:S(2)}) %collective-permute-start.2) | collective-permute-done | bytes 65568 | tf_op jit(solution)/shard_map/ppermute | solution.py:12
  60.4 0.2 multiply_add_fusion.1
  60.5 0.8 collective-permute-start.11
  61.3 0.8 collective-permute-start.10
  62.1 2.9 %fusion = f32[16,64,256]{2,1,0:T(8,128)S(1)} fusion(bf16[256,16,64]{0,2,1:T(8,128)(2,1)S(1)} %copy.26, f32[16,256,256]{2,1,0:T(8,128)} %fusion.18, pred[256,256]{1,0:T(8,128)(4,1)S(1)} %subtract_compare_fusion), kind=kOutput, calls=%fused_computation.8 | convolution fusion | flops 135266304 | bytes 5832704 | tf_op jit(solution)/shard_map/grs,sgc->rgc/dot_general | solution.py:43
  65.1 0.7 collective-permute-start.9
  65.8 1.3 %collective-permute-start.8 = (f32[16,16,64]{2,1,0:T(8,128)S(1)}, f32[16,16,64]{2,1,0:T(8,128)S(1)}, u32[]{:S(2)}, u32[]{:S(2)}) collective-permute-start(f32[16,16,64]{2,1,0:T(8,128)S(1)} %multiply_add_fusion.1), channel_id=1, source_target_pairs={{0,128},{8,136},{16,144},{24,152},{32,160},{40,168},{48,176},{56,1... | collective-permute-start | bytes 196616 | tf_op jit(solution)/shard_map/ppermute | solution.py:12
  67.1 2.6 %collective-permute-start.7 = (f32[16,16,64]{2,1,0:T(8,128)S(1)}, f32[16,16,64]{2,1,0:T(8,128)S(1)}, u32[]{:S(2)}, u32[]{:S(2)}) collective-permute-start(f32[16,16,64]{2,1,0:T(8,128)S(1)} %multiply_add_fusion.1), channel_id=1, source_target_pairs={{0,96},{8,104},{16,112},{24,120},{32,128},{40,136},{48,144},{56,15... | collective-permute-start | bytes 196616 | tf_op jit(solution)/shard_map/ppermute | solution.py:12
  69.7 0.0 collective-permute-done.11
  69.7 2.1 %collective-permute-start.6 = (f32[16,16,64]{2,1,0:T(8,128)S(1)}, f32[16,16,64]{2,1,0:T(8,128)S(1)}, u32[]{:S(2)}, u32[]{:S(2)}) collective-permute-start(f32[16,16,64]{2,1,0:T(8,128)S(1)} %multiply_add_fusion.1), channel_id=1, source_target_pairs={{0,64},{8,72},{16,80},{24,88},{32,96},{40,104},{48,112},{56,120},{... | collective-permute-start | bytes 196616 | tf_op jit(solution)/shard_map/ppermute | solution.py:12
  71.8 0.0 collective-permute-done.10
  71.8 3.8 %collective-permute-start.5 = (f32[16,16,64]{2,1,0:T(8,128)S(1)}, f32[16,16,64]{2,1,0:T(8,128)S(1)}, u32[]{:S(2)}, u32[]{:S(2)}) collective-permute-start(f32[16,16,64]{2,1,0:T(8,128)S(1)} %multiply_add_fusion.1), channel_id=1, source_target_pairs={{0,32},{8,40},{16,48},{24,56},{32,64},{40,72},{48,80},{56,88},{64,... | collective-permute-start | bytes 196616 | tf_op jit(solution)/shard_map/ppermute | solution.py:12
  75.6 0.0 copy-done
  75.6 0.8 fusion.11
  76.4 0.0 collective-permute-done.9
  76.4 1.7 %collective-permute-done.8 = f32[16,16,64]{2,1,0:T(8,128)S(1)} collective-permute-done((f32[16,16,64]{2,1,0:T(8,128)S(1)}, f32[16,16,64]{2,1,0:T(8,128)S(1)}, u32[]{:S(2)}, u32[]{:S(2)}) %collective-permute-start.8) | collective-permute-done | bytes 65568 | tf_op jit(solution)/shard_map/ppermute | solution.py:12
  78.2 7.5 %collective-permute-done.7 = f32[16,16,64]{2,1,0:T(8,128)S(1)} collective-permute-done((f32[16,16,64]{2,1,0:T(8,128)S(1)}, f32[16,16,64]{2,1,0:T(8,128)S(1)}, u32[]{:S(2)}, u32[]{:S(2)}) %collective-permute-start.7) | collective-permute-done | bytes 65568 | tf_op jit(solution)/shard_map/ppermute | solution.py:12
  85.7 8.3 %collective-permute-done.6 = f32[16,16,64]{2,1,0:T(8,128)S(1)} collective-permute-done((f32[16,16,64]{2,1,0:T(8,128)S(1)}, f32[16,16,64]{2,1,0:T(8,128)S(1)}, u32[]{:S(2)}, u32[]{:S(2)}) %collective-permute-start.6) | collective-permute-done | bytes 65568 | tf_op jit(solution)/shard_map/ppermute | solution.py:12
  94.1 1.8 %collective-permute-done.5 = f32[16,16,64]{2,1,0:T(8,128)S(1)} collective-permute-done((f32[16,16,64]{2,1,0:T(8,128)S(1)}, f32[16,16,64]{2,1,0:T(8,128)S(1)}, u32[]{:S(2)}, u32[]{:S(2)}) %collective-permute-start.5) | collective-permute-done | bytes 65568 | tf_op jit(solution)/shard_map/ppermute | solution.py:12
  95.8 1.5 %fusion.13 = bf16[256,16,64]{0,2,1:T(8,128)(2,1)S(1)} fusion(f32[16,64,256]{2,1,0:T(8,128)S(1)} %fusion.11, f32[16,16,64]{2,1,0:T(8,128)S(1)} %collective-permute-done.11, f32[16,16,64]{2,1,0:T(8,128)S(1)} %collective-permute-done.10, f32[16,16,64]{2,1,0:T(8,128)S(1)} %collective-permute-done.9, f32[16,16,64]{2,1,0:T(8,128)S(1)} %collective-permute-done.8, ...), kind=kOutput, calls=%fused_computation.28 | convolution fusion | flops 51216384 | bytes 2106368 | tf_op jit(solution)/shard_map/grm,gmc->rgc/dot_general | solution.py:77
  97.4 1.0 copy.30
  98.3 0.7 convert_element_type.117
  99.0 12.6 %all_to_all.23 = bf16[8,32,1024]{2,1,0:T(8,128)(2,1)S(1)} all-to-all(bf16[8,32,1024]{2,1,0:T(8,128)(2,1)S(1)} %convert_element_type.117), channel_id=1, replica_groups=mesh['ctx'=32,'mp'=8] {'mp'}, dimensions={0} | all-to-all | bytes 1048576 | tf_op jit(solution)/shard_map/all_to_all | solution.py:95
  111.7 0.1 convert_bitcast_fusion
  111.8 0.1 copy.39
  111.8 2.1 %fusion.16 = bf16[32,8192]{1,0:T(8,128)(2,1)} fusion(f32[32,8192]{1,0:T(8,128)S(1)} %bitcast.37, f32[32,3,8192]{2,0,1:T(8,128)} %copy-done.1), kind=kLoop, calls=%fused_computation.34 | loop fusion | flops 524288 | bytes 2621440 | tf_op jit(solution)/shard_map/convert_element_type | solution.py:96
  (8 shorter events, 0.1 us)
Async XLA Ops:
  0.0 15.8 %copy-start.2 = (bf16[32,3,8192]{2,0,1:T(8,128)(2,1)S(1)}, bf16[32,3,8192]{2,0,1:T(8,128)(2,1)}, u32[]{:S(2)}) copy-start(bf16[32,3,8192]{2,0,1:T(8,128)(2,1)} %param.5) | copy-start | bytes 4718596
  1.2 14.6 %collective-permute-start = (bf16[6,3,8192]{2,0,1:T(8,128)(2,1)S(1)}, bf16[6,3,8192]{2,0,1:T(8,128)(2,1)S(1)}, u32[]{:S(2)}, u32[]{:S(2)}) collective-permute-start(bf16[6,3,8192]{2,0,1:T(8,128)(2,1)S(1)} %slice.97), channel_id=1, source_target_pairs={{0,1},{1,2},{2,3},{3,4},{4,5},{5,6},{6,7},{7,8},{8,9},{9,10},{10,1... | collective-permute-start | bytes 884744 | tf_op jit(solution)/shard_map/ppermute | solution.py:12
  19.8 1.7 %copy-start.1 = (f32[32,3,8192]{2,0,1:T(8,128)}, f32[32,3,8192]{2,0,1:T(8,128)S(1)}, u32[]{:S(2)}) copy-start(f32[32,3,8192]{2,0,1:T(8,128)S(1)} %multiply_add_fusion) | copy-start | bytes 9437188
  21.5 5.0 %copy-start.3 = (f32[16,16]{1,0:T(8,128)S(1)}, f32[16,16]{1,0:T(8,128)}, u32[]{:S(2)}) copy-start(f32[16,16]{1,0:T(8,128)} %param.8) | copy-start | bytes 3076
  21.5 5.0 %copy-start.4 = (f32[16,16]{1,0:T(8,128)S(1)}, f32[16,16]{1,0:T(8,128)}, u32[]{:S(2)}) copy-start(f32[16,16]{1,0:T(8,128)} %param.7) | copy-start | bytes 3076
  23.0 13.4 %all-to-all-start = ((bf16[32,8,1024]{2,0,1:T(8,128)(2,1)}), bf16[32,8,1024]{2,0,1:T(8,128)(2,1)S(1)}, u32[]{:S(2)}, u32[]{:S(2)}) async-start(bf16[32,8,1024]{2,0,1:T(8,128)(2,1)} %copy.25), calls=%async_computation | async-start | bytes 1048576 | tf_op jit(solution)/shard_map/all_to_all | solution.py:93
  38.5 13.9 %collective-permute-start.4 = (f32[16,16,64]{2,1,0:T(8,128)S(1)}, f32[16,16,64]{2,1,0:T(8,128)S(1)}, u32[]{:S(2)}, u32[]{:S(2)}) collective-permute-start(f32[16,16,64]{2,1,0:T(8,128)S(1)} %convolution_add_fusion.1), channel_id=1, source_target_pairs={{0,32},{8,40},{16,48},{24,56},{32,64},{40,72},{48,80},{56,88},{64,... | collective-permute-start | bytes 196616 | tf_op jit(solution)/shard_map/ppermute | solution.py:12
  41.3 11.1 %collective-permute-start.3 = (f32[16,16,64]{2,1,0:T(8,128)S(1)}, f32[16,16,64]{2,1,0:T(8,128)S(1)}, u32[]{:S(2)}, u32[]{:S(2)}) collective-permute-start(f32[16,16,64]{2,1,0:T(8,128)S(1)} %convolution_add_fusion.1), channel_id=1, source_target_pairs={{0,24},{8,32},{16,40},{24,48},{32,56},{40,64},{48,72},{56,80},{64,... | collective-permute-start | bytes 196616 | tf_op jit(solution)/shard_map/ppermute | solution.py:12
  46.6 9.9 %collective-permute-start.1 = (f32[16,16,64]{2,1,0:T(8,128)S(1)}, f32[16,16,64]{2,1,0:T(8,128)S(1)}, u32[]{:S(2)}, u32[]{:S(2)}) collective-permute-start(f32[16,16,64]{2,1,0:T(8,128)S(1)} %convolution_add_fusion.1), channel_id=1, source_target_pairs={{0,8},{8,16},{16,24},{24,32},{32,40},{40,48},{48,56},{56,64},{64,7... | collective-permute-start | bytes 196616 | tf_op jit(solution)/shard_map/ppermute | solution.py:12
  48.5 11.8 %collective-permute-start.2 = (f32[16,16,64]{2,1,0:T(8,128)S(1)}, f32[16,16,64]{2,1,0:T(8,128)S(1)}, u32[]{:S(2)}, u32[]{:S(2)}) collective-permute-start(f32[16,16,64]{2,1,0:T(8,128)S(1)} %convolution_add_fusion.1), channel_id=1, source_target_pairs={{0,16},{8,24},{16,32},{24,40},{32,48},{40,56},{48,64},{56,72},{64,... | collective-permute-start | bytes 196616 | tf_op jit(solution)/shard_map/ppermute | solution.py:12
  60.3 15.3 %copy-start = (f32[16,256,256]{2,1,0:T(8,128)S(1)}, f32[16,256,256]{2,1,0:T(8,128)}, u32[]{:S(2)}) copy-start(f32[16,256,256]{2,1,0:T(8,128)} %fusion.18) | copy-start | bytes 12582916
  60.5 9.2 %collective-permute-start.11 = (f32[16,16,64]{2,1,0:T(8,128)S(1)}, f32[16,16,64]{2,1,0:T(8,128)S(1)}, u32[]{:S(2)}, u32[]{:S(2)}) collective-permute-start(f32[16,16,64]{2,1,0:T(8,128)S(1)} %multiply_add_fusion.1), channel_id=1, source_target_pairs={{0,224},{8,232},{16,240},{24,248},{1,225},{9,233},{17,241},{25,249... | collective-permute-start | bytes 196616 | tf_op jit(solution)/shard_map/ppermute | solution.py:12
  61.3 10.5 %collective-permute-start.10 = (f32[16,16,64]{2,1,0:T(8,128)S(1)}, f32[16,16,64]{2,1,0:T(8,128)S(1)}, u32[]{:S(2)}, u32[]{:S(2)}) collective-permute-start(f32[16,16,64]{2,1,0:T(8,128)S(1)} %multiply_add_fusion.1), channel_id=1, source_target_pairs={{0,192},{8,200},{16,208},{24,216},{32,224},{40,232},{48,240},{56,2... | collective-permute-start | bytes 196616 | tf_op jit(solution)/shard_map/ppermute | solution.py:12
  65.1 11.3 %collective-permute-start.9 = (f32[16,16,64]{2,1,0:T(8,128)S(1)}, f32[16,16,64]{2,1,0:T(8,128)S(1)}, u32[]{:S(2)}, u32[]{:S(2)}) collective-permute-start(f32[16,16,64]{2,1,0:T(8,128)S(1)} %multiply_add_fusion.1), channel_id=1, source_target_pairs={{0,160},{8,168},{16,176},{24,184},{32,192},{40,200},{48,208},{56,2... | collective-permute-start | bytes 196616 | tf_op jit(solution)/shard_map/ppermute | solution.py:12
  65.8 12.4 %collective-permute-start.8 = (f32[16,16,64]{2,1,0:T(8,128)S(1)}, f32[16,16,64]{2,1,0:T(8,128)S(1)}, u32[]{:S(2)}, u32[]{:S(2)}) collective-permute-start(f32[16,16,64]{2,1,0:T(8,128)S(1)} %multiply_add_fusion.1), channel_id=1, source_target_pairs={{0,128},{8,136},{16,144},{24,152},{32,160},{40,168},{48,176},{56,1... | collective-permute-start | bytes 196616 | tf_op jit(solution)/shard_map/ppermute | solution.py:12
  67.1 18.7 %collective-permute-start.7 = (f32[16,16,64]{2,1,0:T(8,128)S(1)}, f32[16,16,64]{2,1,0:T(8,128)S(1)}, u32[]{:S(2)}, u32[]{:S(2)}) collective-permute-start(f32[16,16,64]{2,1,0:T(8,128)S(1)} %multiply_add_fusion.1), channel_id=1, source_target_pairs={{0,96},{8,104},{16,112},{24,120},{32,128},{40,136},{48,144},{56,15... | collective-permute-start | bytes 196616 | tf_op jit(solution)/shard_map/ppermute | solution.py:12
  69.7 24.4 %collective-permute-start.6 = (f32[16,16,64]{2,1,0:T(8,128)S(1)}, f32[16,16,64]{2,1,0:T(8,128)S(1)}, u32[]{:S(2)}, u32[]{:S(2)}) collective-permute-start(f32[16,16,64]{2,1,0:T(8,128)S(1)} %multiply_add_fusion.1), channel_id=1, source_target_pairs={{0,64},{8,72},{16,80},{24,88},{32,96},{40,104},{48,112},{56,120},{... | collective-permute-start | bytes 196616 | tf_op jit(solution)/shard_map/ppermute | solution.py:12
  71.8 24.0 %collective-permute-start.5 = (f32[16,16,64]{2,1,0:T(8,128)S(1)}, f32[16,16,64]{2,1,0:T(8,128)S(1)}, u32[]{:S(2)}, u32[]{:S(2)}) collective-permute-start(f32[16,16,64]{2,1,0:T(8,128)S(1)} %multiply_add_fusion.1), channel_id=1, source_target_pairs={{0,32},{8,40},{16,48},{24,56},{32,64},{40,72},{48,80},{56,88},{64,... | collective-permute-start | bytes 196616 | tf_op jit(solution)/shard_map/ppermute | solution.py:12

commit v5 on v2

--- a/solution.py
+++ b/solution.py
@@ -61,8 +61,11 @@
     end_weight = jnp.exp(-decays[:, :, None] * (float(block_len) - offsets)[None, None, :])
     local_state = split_product("gms,sgc->gmc", end_weight, inputs)
 
-    gathered = lax.all_gather(local_state, "ctx", axis=0)
-    count = gathered.shape[0]
+    count = lax.axis_size("ctx")
+    flat = local_state.reshape(1, -1)
+    sent = jnp.broadcast_to(flat, (count, flat.shape[1]))
+    gathered = lax.all_to_all(sent, "ctx", split_axis=0, concat_axis=0, tiled=True)
+    gathered = gathered.reshape((count,) + local_state.shape)
     here = lax.axis_index("ctx")
     earlier = jnp.arange(count, dtype=jnp.int32)
     gap = (here - 1 - earlier).astype(jnp.float32) * float(block_len)

time: 165 us -> 132 us (0.80)
  waiting for transfers between devices: 96.9 us -> 48.9 us
  between operations: 13.7 us -> 0.28 us
  starting transfers between devices: 7.74 us -> 20.9 us
  local copies, waits for them, and re-layouts: 14.9 us -> 25.8 us
  matrix products: 7.82 us -> 10.6 us
  other arithmetic: 10.6 us -> 12.9 us
    all_gather x1 -> x0, waiting for transfers between devices: 83 us -> none  [long_filter(): gathered = lax.all_gather(local_state, 'ctx', axis=0)]
    all_to_all x0 -> x1, waiting for transfers between devices: none -> 35.2 us  [long_filter(): lax.all_to_all(sent, 'ctx', split_axis=0, concat_axis=0, tiled=True)]
    all_to_all x0 -> x1, starting transfers between devices: none -> 13.4 us  [long_filter(): lax.all_to_all(sent, 'ctx', split_axis=0, concat_axis=0, tiled=True)]
    mul x0 -> x2, local copies, waits for them, and re-layouts: none -> 7.26 us  [long_filter(): state = jnp.sum(weight[:, :, :, None] * gathered, axis=0)]
    broadcast_in_dim x0 -> x2, local copies, waits for them, and re-layouts: none -> 3.29 us  [long_filter(): sent = jnp.broadcast_to(flat, (count, flat.shape[1]))]
    reduce_sum x1, other arithmetic: 3.01 us -> 5.27 us  [long_filter(): state = jnp.sum(weight[:, :, :, None] * gathered, axis=0)]
    dot_general x2, matrix products: 1.83 us -> 3.62 us  [split_product(): jnp.einsum(form, lower_part, inputs, preferred_element_type=jnp.float32)]
    unnamed x17 -> x15, local copies, waits for them, and re-layouts: 4.5 us -> 4.4 us
  transfers between devices with their start and end apart: 3 -> 3, of which waited for: 3 -> 3; matrix products, arithmetic and copies ran while one was open for 7% -> 15% of each run, Pallas kernels for 0% -> 0%
where the time goes in v5:
time: 132 us; the launch traced here: 131 us
  waiting for transfers between devices  48.9 us (37%)
  local copies, waits for them, and re-layouts  25.8 us (20%)
  starting transfers between devices  20.9 us (16%)
  other arithmetic  12.9 us (10%)
  blocking collectives  11.2 us (8%)
  matrix products  10.6 us (8%)
    all_to_all x1, waiting for transfers between devices, long_filter(): lax.all_to_all(sent, 'ctx', split_axis=0, concat_axis=0, tiled=True)  35.2 us
    all_to_all x1, starting transfers between devices, long_filter(): lax.all_to_all(sent, 'ctx', split_axis=0, concat_axis=0, tiled=True)  13.4 us
    all_to_all x1, blocking collectives, shards(): lax.all_to_all(filtered, 'mp', split_axis=0, concat_axis=1, tiled=True)  11.2 us
    all_to_all x1, waiting for transfers between devices, shards(): lax.all_to_all(product, 'mp', split_axis=1, concat_axis=0, tiled=True)  9.14 us
    mul x2, local copies, waits for them, and re-layouts, long_filter(): state = jnp.sum(weight[:, :, :, None] * gathered, axis=0)  7.26 us
    reduce_sum x1, other arithmetic, long_filter(): state = jnp.sum(weight[:, :, :, None] * gathered, axis=0)  5.27 us
    slice x1, local copies, waits for them, and re-layouts, short_convolution(): conv_weight[:, position_shift, :][None] * earlier  4.54 us
    ppermute x1, waiting for transfers between devices, shifted(): return lax.ppermute(block, axis, route)  4.53 us
  transfers between devices with their start and end apart: 3, of which 3 were waited for; matrix products, arithmetic and copies ran while one was open for 15% of the time, Pallas kernels for 0%

profile of v5, /device:TPU:1, one launch (start us, length us, event | category | flops | bytes accessed | tf_op | source)
XLA Modules:
  0.0 130.6 jit_solution(4303315855973390787)
XLA Ops:
  0.0 0.0 copy-start.2
  0.0 1.2 slice.97
  1.2 4.0 %collective-permute-start = (bf16[6,3,8192]{2,0,1:T(8,128)(2,1)S(1)}, bf16[6,3,8192]{2,0,1:T(8,128)(2,1)S(1)}, u32[]{:S(2)}, u32[]{:S(2)}) collective-permute-start(bf16[6,3,8192]{2,0,1:T(8,128)(2,1)S(1)} %slice.97), channel_id=1, source_target_pairs={{0,1},{1,2},{2,3},{3,4},{4,5},{5,6},{6,7},{7,8},{8,9},{9,10},{10,1... | collective-permute-start | bytes 884744 | tf_op jit(solution)/shard_map/ppermute | solution.py:12
  5.3 0.7 copy.32
  6.0 0.1 reduce-window.9
  6.1 0.1 reduce.3
  6.2 0.7 sub.57
  6.9 4.5 %fusion.37 = (f32[3,1,8192]{2,1,0:T(1,128)S(1)}, f32[3,1,8192]{2,1,0:T(1,128)S(1)}, f32[3,1,8192]{2,1,0:T(1,128)S(1)}, f32[3,1,8192]{2,1,0:T(1,128)S(1)}, f32[3,...) fusion(f32[3,7,8192]{2,1,0:T(8,128)} %param.6), kind=kLoop, calls=%fused_computation.81 | loop fusion | bytes 1376256 | tf_op jit(solution)/shard_map/slice | solution.py:33
  11.4 0.2 convert_reduce_fusion
  11.6 0.1 copy_bitcast_fusion
  11.8 0.1 copy_bitcast_fusion.2
  11.9 0.1 copy_bitcast_fusion.4
  12.1 0.1 copy.56
  12.1 0.1 and_convert_fusion.5
  12.2 4.5 %collective-permute-done = bf16[6,3,8192]{2,0,1:T(8,128)(2,1)S(1)} collective-permute-done((bf16[6,3,8192]{2,0,1:T(8,128)(2,1)S(1)}, bf16[6,3,8192]{2,0,1:T(8,128)(2,1)S(1)}, u32[]{:S(2)}, u32[]{:S(2)}) %collective-permute-start) | collective-permute-done | bytes 294944 | tf_op jit(solution)/shard_map/ppermute | solution.py:12
  16.8 0.0 copy-done.2
  16.8 4.0 %multiply_add_fusion = f32[32,3,8192]{2,0,1:T(8,128)S(1)} fusion(bf16[32,3,8192]{2,0,1:T(8,128)(2,1)S(1)} %copy-done.2, bf16[6,3,8192]{2,0,1:T(8,128)(2,1)S(1)} %collective-permute-done, f32[32]{0:T(128)S(1)} %get-tuple-element.15, f32[3,8192]{1,0:T(4,128)S(1)} %get-tuple-element.21, f32[32]{0:T(128)S(1)} %get-tuple-element.16, ...), kind=kLoop, calls=%fused_computation.7 | loop fusion | flops 35389440 | bytes 5702528 | tf_op jit(solution)/shard_map/add | solution.py:32
  20.7 0.0 copy-start.1
  20.8 1.7 %copy-done.1 = f32[32,3,8192]{2,0,1:T(8,128)} copy-done((f32[32,3,8192]{2,0,1:T(8,128)}, f32[32,3,8192]{2,0,1:T(8,128)S(1)}, u32[]{:S(2)}) %copy-start.1) | copy-done | bytes 3145752
  22.4 0.0 copy-start.3
  22.4 0.0 copy-start.4
  22.4 0.1 fusion.15
  22.5 0.3 copy.48
  22.8 1.1 copy.33
  23.9 3.5 %all-to-all-start = ((bf16[32,8,1024]{2,0,1:T(8,128)(2,1)}), bf16[32,8,1024]{2,0,1:T(8,128)(2,1)S(1)}, u32[]{:S(2)}, u32[]{:S(2)}) async-start(bf16[32,8,1024]{2,0,1:T(8,128)(2,1)} %copy.33), calls=%async_computation | async-start | bytes 1048576 | tf_op jit(solution)/shard_map/all_to_all | solution.py:95
  27.4 0.0 copy-done.3
  27.4 0.0 copy-done.4
  27.5 9.1 %all-to-all-done = bf16[32,8,1024]{2,0,1:T(8,128)(2,1)S(1)} async-done(((bf16[32,8,1024]{2,0,1:T(8,128)(2,1)}), bf16[32,8,1024]{2,0,1:T(8,128)(2,1)S(1)}, u32[]{:S(2)}, u32[]{:S(2)}) %all-to-all-start) | async-done | bytes 524320 | tf_op jit(solution)/shard_map/all_to_all | solution.py:95
  36.6 0.7 reshape.124
  37.3 0.8 copy.34
  38.1 0.3 fusion.24
  38.4 0.3 convolution_add_fusion
  38.7 0.1 broadcast_in_dim.28
  38.8 3.2 %broadcast_in_dim.29 = f32[32,1,16384]{2,1,0:T(1,128)} broadcast(f32[16384]{0:T(1024)S(1)} %broadcast_in_dim.28), dimensions={2} | broadcast | bytes 2162688 | tf_op jit(solution)/shard_map/broadcast_in_dim | solution.py:66
  42.0 13.4 %all-to-all-start.1 = ((f32[32,1,16384]{2,1,0:T(1,128)}), f32[32,1,16384]{2,1,0:T(1,128)}, u32[]{:S(2)}, u32[]{:S(2)}) async-start(f32[32,1,16384]{2,1,0:T(1,128)} %broadcast_in_dim.29), calls=%async_computation.1 | async-start | bytes 4194304 | tf_op jit(solution)/shard_map/all_to_all | solution.py:67
  55.5 0.1 exponential_select_fusion
  55.6 2.6 %mul.282 = f32[32,16,16,64]{3,2,1,0:T(8,128)} broadcast(f32[32,16,16]{2,1,0:T(8,128)S(1)} %exponential_select_fusion), dimensions={0,1,2} | broadcast | bytes 2129920 | tf_op jit(solution)/shard_map/mul | solution.py:77
  58.2 4.7 %mul.283 = f32[32,1,16384]{2,1,0:T(1,128)S(1)} reshape(f32[32,16,16,64]{3,2,1,0:T(8,128)} %mul.282) | data formatting | bytes 4194304 | tf_op jit(solution)/shard_map/mul | solution.py:77
  62.9 3.7 %fusion.19 = f32[16,256,256]{2,1,0:T(8,128)S(1)} fusion(f32[16,16]{1,0:T(8,128)S(1)} %copy-done.3, f32[16,16]{1,0:T(8,128)S(1)} %get-tuple-element.13, f32[16,16]{1,0:T(8,128)S(1)} %get-tuple-element.12), kind=kOutput, calls=%fused_computation.41 | convolution fusion | flops 201523200 | bytes 4197376 | tf_op jit(solution)/shard_map/grm,gms->grs/dot_general | solution.py:55
  66.7 0.0 copy-start
  66.7 1.9 %copy-done = f32[16,256,256]{2,1,0:T(8,128)} copy-done((f32[16,256,256]{2,1,0:T(8,128)}, f32[16,256,256]{2,1,0:T(8,128)S(1)}, u32[]{:S(2)}) %copy-start) | copy-done | bytes 4194328
  68.6 1.7 %fusion = f32[16,64,256]{2,1,0:T(8,128)} fusion(bf16[256,16,64]{0,2,1:T(8,128)(2,1)S(1)} %copy.34, f32[16,256,256]{2,1,0:T(8,128)S(1)} %fusion.19, pred[256,256]{1,0:T(8,128)(4,1)S(1)} %subtract_compare_fusion), kind=kOutput, calls=%fused_computation.8 | convolution fusion | flops 135266304 | bytes 5832704 | tf_op jit(solution)/shard_map/grs,sgc->rgc/dot_general | solution.py:43
  70.4 35.2 %all-to-all-done.1 = f32[32,1,16384]{2,1,0:T(1,128)} async-done(((f32[32,1,16384]{2,1,0:T(1,128)}), f32[32,1,16384]{2,1,0:T(1,128)}, u32[]{:S(2)}, u32[]{:S(2)}) %all-to-all-start.1) | async-done | bytes 2097184 | tf_op jit(solution)/shard_map/all_to_all | solution.py:67
  105.6 5.3 %multiply_reduce_fusion = f32[16384]{0:T(1024)S(1)} fusion(f32[32,1,16384]{2,1,0:T(1,128)S(1)} %mul.283, f32[32,1,16384]{2,1,0:T(1,128)} %all-to-all-done.1), kind=kLoop, calls=%fused_computation.10 | loop fusion | flops 1032192 | bytes 4259840 | tf_op jit(solution)/shard_map/reduce_sum | solution.py:77
  110.8 0.1 reduce_sum.22
  110.9 1.2 fusion.23
  112.1 3.3 %fusion.14 = bf16[256,16,64]{0,2,1:T(8,128)(2,1)S(1)} fusion(f32[16,64,256]{2,1,0:T(8,128)S(1)} %fusion.23, f32[16,64,256]{2,1,0:T(8,128)} %fusion, bf16[256,16,64]{0,2,1:T(8,128)(2,1)S(1)} %copy.34, f32[16,256,256]{2,1,0:T(8,128)} %copy-done, pred[256,256]{1,0:T(8,128)(4,1)S(1)} %subtract_compare_fusion), kind=kOutput, calls=%fused_computation.29 | convolution fusion | flops 140247040 | bytes 7405568 | tf_op jit(solution)/shard_map/grs,sgc->rgc/dot_general | solution.py:44
  115.4 1.0 copy.38
  116.4 0.7 convert_element_type.125
  117.1 11.2 %all_to_all.29 = bf16[8,32,1024]{2,1,0:T(8,128)(2,1)S(1)} all-to-all(bf16[8,32,1024]{2,1,0:T(8,128)(2,1)S(1)} %convert_element_type.125), channel_id=1, replica_groups=mesh['ctx'=32,'mp'=8] {'mp'}, dimensions={0} | all-to-all | bytes 1048576 | tf_op jit(solution)/shard_map/all_to_all | solution.py:97
  128.3 0.1 convert_bitcast_fusion
  128.4 0.1 copy.47
  128.5 2.1 %fusion.17 = bf16[32,8192]{1,0:T(8,128)(2,1)} fusion(f32[32,8192]{1,0:T(8,128)S(1)} %bitcast.40, f32[32,3,8192]{2,0,1:T(8,128)} %copy-done.1), kind=kLoop, calls=%fused_computation.35 | loop fusion | flops 524288 | bytes 2621440 | tf_op jit(solution)/shard_map/convert_element_type | solution.py:98
  (7 shorter events, 0.1 us)
Async XLA Ops:
  0.0 16.8 %copy-start.2 = (bf16[32,3,8192]{2,0,1:T(8,128)(2,1)S(1)}, bf16[32,3,8192]{2,0,1:T(8,128)(2,1)}, u32[]{:S(2)}) copy-start(bf16[32,3,8192]{2,0,1:T(8,128)(2,1)} %param.5) | copy-start | bytes 4718596
  1.2 15.5 %collective-permute-start = (bf16[6,3,8192]{2,0,1:T(8,128)(2,1)S(1)}, bf16[6,3,8192]{2,0,1:T(8,128)(2,1)S(1)}, u32[]{:S(2)}, u32[]{:S(2)}) collective-permute-start(bf16[6,3,8192]{2,0,1:T(8,128)(2,1)S(1)} %slice.97), channel_id=1, source_target_pairs={{0,1},{1,2},{2,3},{3,4},{4,5},{5,6},{6,7},{7,8},{8,9},{9,10},{10,1... | collective-permute-start | bytes 884744 | tf_op jit(solution)/shard_map/ppermute | solution.py:12
  20.7 1.7 %copy-start.1 = (f32[32,3,8192]{2,0,1:T(8,128)}, f32[32,3,8192]{2,0,1:T(8,128)S(1)}, u32[]{:S(2)}) copy-start(f32[32,3,8192]{2,0,1:T(8,128)S(1)} %multiply_add_fusion) | copy-start | bytes 9437188
  22.4 5.0 %copy-start.3 = (f32[16,16]{1,0:T(8,128)S(1)}, f32[16,16]{1,0:T(8,128)}, u32[]{:S(2)}) copy-start(f32[16,16]{1,0:T(8,128)} %param.8) | copy-start | bytes 3076
  22.4 5.0 %copy-start.4 = (f32[16,16]{1,0:T(8,128)S(1)}, f32[16,16]{1,0:T(8,128)}, u32[]{:S(2)}) copy-start(f32[16,16]{1,0:T(8,128)} %param.7) | copy-start | bytes 3076
  23.9 12.7 %all-to-all-start = ((bf16[32,8,1024]{2,0,1:T(8,128)(2,1)}), bf16[32,8,1024]{2,0,1:T(8,128)(2,1)S(1)}, u32[]{:S(2)}, u32[]{:S(2)}) async-start(bf16[32,8,1024]{2,0,1:T(8,128)(2,1)} %copy.33), calls=%async_computation | async-start | bytes 1048576 | tf_op jit(solution)/shard_map/all_to_all | solution.py:95
  42.0 63.5 %all-to-all-start.1 = ((f32[32,1,16384]{2,1,0:T(1,128)}), f32[32,1,16384]{2,1,0:T(1,128)}, u32[]{:S(2)}, u32[]{:S(2)}) async-start(f32[32,1,16384]{2,1,0:T(1,128)} %broadcast_in_dim.29), calls=%async_computation.1 | async-start | bytes 4194304 | tf_op jit(solution)/shard_map/all_to_all | solution.py:67
  66.7 1.9 %copy-start = (f32[16,256,256]{2,1,0:T(8,128)}, f32[16,256,256]{2,1,0:T(8,128)S(1)}, u32[]{:S(2)}) copy-start(f32[16,256,256]{2,1,0:T(8,128)S(1)} %fusion.19) | copy-start | bytes 12582916

commit v6 on v2

--- a/solution.py
+++ b/solution.py
@@ -1,7 +1,7 @@
 import jax
 import jax.numpy as jnp
 from jax import lax
-from jax.sharding import PartitionSpec as P
+from jax.sharding import Mesh, NamedSharding, PartitionSpec as P
 
 HIGHEST = lax.Precision.HIGHEST
 
@@ -44,10 +44,11 @@
     return first + jnp.einsum(form, lower_part, inputs, preferred_element_type=jnp.float32)
 
 
-def long_filter(product, residues, decays):
-    block_len, channels = product.shape
+def long_filter(product, residues, decays, block_len, outer_axis):
+    positions, channels = product.shape
     group_count = residues.shape[0]
     group_width = channels // group_count
+    block_count = positions // block_len
     coefficient = residues * jnp.sqrt(decays)
     offsets = jnp.arange(block_len, dtype=jnp.float32)
     left = coefficient[:, None, :] * jnp.exp(-decays[:, None, :] * offsets[None, :, None])
@@ -55,51 +56,89 @@
     tile = jnp.einsum("grm,gms->grs", left, right, precision=HIGHEST)
     lag = jnp.arange(block_len)[:, None] - jnp.arange(block_len)[None, :]
     tile = jnp.where((lag >= 0)[None], tile, 0.0)
-    inputs = product.reshape(block_len, group_count, group_width)
-    intra = split_product("grs,sgc->rgc", tile, inputs)
+    inputs = product.reshape(block_count, block_len, group_count, group_width)
+    intra = split_product("grs,bsgc->brgc", tile, inputs)
 
     end_weight = jnp.exp(-decays[:, :, None] * (float(block_len) - offsets)[None, None, :])
-    local_state = split_product("gms,sgc->gmc", end_weight, inputs)
+    block_state = split_product("gms,bsgc->gmbc", end_weight, inputs)
 
-    gathered = lax.all_gather(local_state, "ctx", axis=0)
-    count = gathered.shape[0]
-    here = lax.axis_index("ctx")
+    blocks = jnp.arange(block_count, dtype=jnp.float32)
+    to_end = jnp.exp(-decays[:, :, None] * (float(block_len) * (block_count - 1 - blocks))[None, None, :])
+    run_state = jnp.einsum("gmb,gmbc->gmc", to_end, block_state, precision=HIGHEST)
+    count = lax.axis_size(outer_axis)
+    flat = run_state.reshape(1, -1)
+    sent = jnp.broadcast_to(flat, (count, flat.shape[1]))
+    gathered = lax.all_to_all(sent, outer_axis, split_axis=0, concat_axis=0, tiled=True)
+    gathered = gathered.reshape((count,) + run_state.shape)
+    here = lax.axis_index(outer_axis)
     earlier = jnp.arange(count, dtype=jnp.int32)
-    gap = (here - 1 - earlier).astype(jnp.float32) * float(block_len)
+    gap = (here - 1 - earlier).astype(jnp.float32) * float(positions)
     weight = jnp.where(
         (earlier < here)[:, None, None],
         jnp.exp(-decays[None] * jnp.maximum(gap, 0.0)[:, None, None]),
         0.0,
     )
-    state = jnp.sum(weight[:, :, :, None] * gathered, axis=0)
+    incoming = jnp.sum(weight[:, :, :, None] * gathered, axis=0)
 
-    inter = jnp.einsum("grm,gmc->rgc", left, state, precision=HIGHEST)
-    return (intra + inter).reshape(block_len, channels).astype(jnp.bfloat16)
+    later = jnp.arange(block_count)[:, None]
+    before = jnp.arange(block_count)[None, :]
+    block_gap = jnp.maximum(later - 1 - before, 0).astype(jnp.float32) * float(block_len)
+    carry = jnp.where((before < later)[None, None], jnp.exp(-decays[:, :, None, None] * block_gap[None, None]), 0.0)
+    start_decay = jnp.exp(-decays[:, :, None] * (float(block_len) * blocks)[None, None, :])
+    state = jnp.einsum("gmab,gmbc->gmac", carry, block_state, precision=HIGHEST)
+    state = state + start_decay[:, :, :, None] * incoming[:, :, None, :]
+
+    inter = jnp.einsum("grm,gmbc->brgc", left, state, precision=HIGHEST)
+    return (intra + inter).reshape(positions, channels).astype(jnp.bfloat16)
 
 
 def shards(proj, conv_weight, residues, decays, doc_lengths):
     kernel_len = conv_weight.shape[1]
     rows = proj.shape[0]
-    lin_axis = ("ctx", "mp")
+    outer_size = lax.axis_size("zo")
+    inner_size = lax.axis_size("zi")
+    mp_size = lax.axis_size("mp")
+    lin_axis = ("zo", "zi", "mp")
     tail_rows = shifted(proj[rows - (kernel_len - 1) :], lin_axis, 1)
-    lin_index = lax.axis_index("ctx") * lax.axis_size("mp") + lax.axis_index("mp")
+    lin_index = (lax.axis_index("zo") * inner_size + lax.axis_index("zi")) * mp_size + lax.axis_index("mp")
     padded_pos = lin_index * rows - (kernel_len - 1) + jnp.arange(rows + kernel_len - 1, dtype=jnp.int32)
     padded_document_ids = document_number_index(doc_lengths, padded_pos)
     padded = jnp.concatenate([tail_rows, proj], axis=0)
     conv = short_convolution(padded, conv_weight, padded_document_ids, padded_pos, rows)
     query_part = conv[:, 0]
     product = (conv[:, 1] * conv[:, 2]).astype(jnp.bfloat16)
-    channel_rows = lax.all_to_all(product, "mp", split_axis=1, concat_axis=0, tiled=True)
-    filtered = long_filter(channel_rows, residues, decays)
-    filtered = lax.all_to_all(filtered, "mp", split_axis=0, concat_axis=1, tiled=True)
+
+    swap_axis = ("mp", "zi")
+    gathered = lax.all_to_all(product, swap_axis, split_axis=1, concat_axis=0, tiled=True)
+    width = gathered.shape[1]
+    gathered = gathered.reshape(mp_size, inner_size, rows, width).transpose(1, 0, 2, 3)
+    gathered = gathered.reshape(inner_size * mp_size * rows, width)
+    groups_here = residues.shape[0] // inner_size
+    first_group = lax.axis_index("zi") * groups_here
+    local_residues = lax.dynamic_slice_in_dim(residues, first_group, groups_here, 0)
+    local_decays = lax.dynamic_slice_in_dim(decays, first_group, groups_here, 0)
+    block_len = min(256, gathered.shape[0])
+    filtered = long_filter(gathered, local_residues, local_decays, block_len, "zo")
+    filtered = filtered.reshape(inner_size, mp_size, rows, width).transpose(1, 0, 2, 3)
+    filtered = filtered.reshape(inner_size * mp_size * rows, width)
+    filtered = lax.all_to_all(filtered, swap_axis, split_axis=0, concat_axis=1, tiled=True)
     return (query_part * filtered.astype(jnp.float32)).astype(jnp.bfloat16)
 
 
 def solution(mesh):
-    return jax.shard_map(
+    ctx_size, mp_size = mesh.devices.shape
+    inner = 4 if ctx_size % 4 == 0 else 1
+    split_mesh = Mesh(mesh.devices.reshape(ctx_size // inner, inner, mp_size), ("zo", "zi", "mp"))
+    mapped = jax.shard_map(
         shards,
-        mesh=mesh,
-        in_specs=(P(("ctx", "mp"), None, None), P(), P("mp", None), P("mp", None), P()),
-        out_specs=P(("ctx", "mp"), None),
+        mesh=split_mesh,
+        in_specs=(P(("zo", "zi", "mp"), None, None), P(), P("mp", None), P("mp", None), P()),
+        out_specs=P(("zo", "zi", "mp"), None),
         check_vma=False,
     )
+    placed = NamedSharding(mesh, P(("ctx", "mp"), None))
+
+    def run(*args):
+        return lax.with_sharding_constraint(mapped(*args), placed)
+
+    return run

time: 165 us -> 85.6 us (0.52)
  waiting for transfers between devices: 96.9 us -> 20.4 us
  between operations: 13.7 us -> 0.3 us
  starting transfers between devices: 7.74 us -> 18.9 us
  blocking collectives: 12.5 us -> 16.6 us
  other arithmetic: 10.6 us -> 8.71 us
  local copies, waits for them, and re-layouts: 14.9 us -> 13.2 us
    all_gather x1 -> x0, waiting for transfers between devices: 83 us -> none  [long_filter(): gathered = lax.all_gather(local_state, 'ctx', axis=0)]
    all_to_all x1 -> x2, starting transfers between devices: 3.49 us -> 14.9 us  [the longest x1 8.18 us: long_filter(): lax.all_to_all(sent, outer_axis, split_axis=0, concat_axis=0, tiled=True)]
    all_to_all x1 -> x2, waiting for transfers between devices: 8.91 us -> 16.6 us  [the longest x1 9.64 us: shards(): lax.all_to_all(product, swap_axis, split_axis=1, concat_axis=0, tiled=True)]
    all_to_all x1, blocking collectives: 12.5 us -> 16.6 us  [shards(): lax.all_to_all(filtered, swap_axis, split_axis=0, concat_axis=1, tiled=True)]
    reduce_sum x1, other arithmetic: 3.01 us -> 0.16 us  [long_filter(): incoming = jnp.sum(weight[:, :, :, None] * gathered, axis=0)]
    dot_general x1, matrix products: 3.74 us -> 1.18 us  [long_filter(): tile = jnp.einsum('grm,gms->grs', left, right, precision=HIGHEST)]
    dot_general x1 -> x3, matrix products: 1.2 us -> 3.58 us  [the longest x1 2.35 us: long_filter(): inter = jnp.einsum('grm,gmbc->brgc', left, state, precision=HIGHEST)]
    unnamed x17 -> x9, local copies, waits for them, and re-layouts: 4.5 us -> 2.24 us
  transfers between devices with their start and end apart: 3 -> 3, of which waited for: 3 -> 3; matrix products, arithmetic and copies ran while one was open for 7% -> 12% of each run, Pallas kernels for 0% -> 0%
where the time goes in v6:
time: 85.6 us; the launch traced here: 85.1 us
  waiting for transfers between devices  20.4 us (24%)
  starting transfers between devices  18.9 us (22%)
  blocking collectives  16.6 us (19%)
  local copies, waits for them, and re-layouts  13.2 us (15%)
  other arithmetic  8.71 us (10%)
  matrix products  7.09 us (8%)
    all_to_all x1, blocking collectives, shards(): lax.all_to_all(filtered, swap_axis, split_axis=0, concat_axis=1, tiled=True)  16.6 us
    all_to_all x1, waiting for transfers between devices, shards(): lax.all_to_all(product, swap_axis, split_axis=1, concat_axis=0, tiled=True)  9.64 us
    all_to_all x1, starting transfers between devices, long_filter(): lax.all_to_all(sent, outer_axis, split_axis=0, concat_axis=0, tiled=True)  8.18 us
    all_to_all x1, waiting for transfers between devices, long_filter(): lax.all_to_all(sent, outer_axis, split_axis=0, concat_axis=0, tiled=True)  6.99 us
    all_to_all x1, starting transfers between devices, shards(): lax.all_to_all(product, swap_axis, split_axis=1, concat_axis=0, tiled=True)  6.68 us
    slice x1, local copies, waits for them, and re-layouts, short_convolution(): conv_weight[:, position_shift, :][None] * earlier  4.22 us
    ppermute x1, starting transfers between devices, shifted(): return lax.ppermute(block, axis, route)  4.02 us
    add x1, other arithmetic, short_convolution(): result + conv_weight[:, position_shift, :][None] * earlier * keep_mask.as...  3.98 us
  transfers between devices with their start and end apart: 3, of which 3 were waited for; matrix products, arithmetic and copies ran while one was open for 12% of the time, Pallas kernels for 0%

profile of v6, /device:TPU:1, one launch (start us, length us, event | category | flops | bytes accessed | tf_op | source)
XLA Modules:
  0.0 85.1 jit_solution(10614986577789238527)
XLA Ops:
  0.0 0.0 copy-start.1
  0.0 1.2 %slice.97 = bf16[6,3,8192]{2,0,1:T(8,128)(2,1)S(1)} slice(bf16[32,3,8192]{2,0,1:T(8,128)(2,1)} %param.5), slice={[26:32], [0:3], [0:8192]} | slice | bytes 589824 | tf_op jit(solution)/shard_map/slice | solution.py:102
  1.2 4.0 %collective-permute-start = (bf16[6,3,8192]{2,0,1:T(8,128)(2,1)S(1)}, bf16[6,3,8192]{2,0,1:T(8,128)(2,1)S(1)}, u32[]{:S(2)}, u32[]{:S(2)}) collective-permute-start(bf16[6,3,8192]{2,0,1:T(8,128)(2,1)S(1)} %slice.97), channel_id=1, source_target_pairs={{0,1},{1,2},{2,3},{3,4},{4,5},{5,6},{6,7},{7,8},{8,9},{9,10},{10,1... | collective-permute-start | bytes 884744 | tf_op jit(solution)/shard_map/ppermute | solution.py:12
  5.4 0.7 copy.47
  6.1 0.1 reduce-window.9
  6.2 0.1 reduce.3
  6.3 0.7 sub.82
  7.0 0.1 compare_convert_fusion
  7.1 0.2 convert_reduce_fusion
  7.2 0.1 and_convert_fusion.5
  7.3 4.2 %fusion.47 = (f32[3,1,8192]{2,1,0:T(1,128)S(1)}, f32[3,1,8192]{2,1,0:T(1,128)S(1)}, f32[3,1,8192]{2,1,0:T(1,128)S(1)}, f32[3,1,8192]{2,1,0:T(1,128)S(1)}, f32[3,...) fusion(f32[3,7,8192]{2,1,0:T(8,128)} %param.6), kind=kLoop, calls=%fused_computation.100 | loop fusion | bytes 1376256 | tf_op jit(solution)/shard_map/slice | solution.py:33
  11.6 0.1 copy.88
  11.6 0.7 sqrt_multiply_fusion
  12.4 0.1 convert_multiply_fusion
  12.4 0.1 copy_bitcast_fusion
  12.6 0.1 copy_bitcast_fusion.2
  12.7 0.1 copy_bitcast_fusion.4
  12.9 0.1 exponential_select_fusion
  13.0 3.8 %collective-permute-done = bf16[6,3,8192]{2,0,1:T(8,128)(2,1)S(1)} collective-permute-done((bf16[6,3,8192]{2,0,1:T(8,128)(2,1)S(1)}, bf16[6,3,8192]{2,0,1:T(8,128)(2,1)S(1)}, u32[]{:S(2)}, u32[]{:S(2)}) %collective-permute-start) | collective-permute-done | bytes 294944 | tf_op jit(solution)/shard_map/ppermute | solution.py:12
  16.8 0.0 copy-done.1
  16.8 4.0 %multiply_add_fusion = f32[32,3,8192]{2,0,1:T(8,128)S(1)} fusion(bf16[32,3,8192]{2,0,1:T(8,128)(2,1)S(1)} %copy-done.1, bf16[6,3,8192]{2,0,1:T(8,128)(2,1)S(1)} %collective-permute-done, f32[32]{0:T(128)S(1)} %get-tuple-element.17, f32[3,8192]{1,0:T(4,128)S(1)} %get-tuple-element.22, f32[32]{0:T(128)S(1)} %get-tuple-element.18, ...), kind=kLoop, calls=%fused_computation.5 | loop fusion | flops 35389440 | bytes 5702528 | tf_op jit(solution)/shard_map/add | solution.py:32
  20.7 0.0 copy-start
  20.8 1.6 %copy-done = f32[32,3,8192]{2,0,1:T(8,128)} copy-done((f32[32,3,8192]{2,0,1:T(8,128)}, f32[32,3,8192]{2,0,1:T(8,128)S(1)}, u32[]{:S(2)}) %copy-start) | copy-done | bytes 3145752
  22.4 0.1 fusion.7
  22.5 0.1 copy.74
  22.6 1.1 %copy.48 = bf16[32,32,256]{2,0,1:T(8,128)(2,1)} copy(bf16[32,32,256]{2,1,0:T(8,128)(2,1)S(1)} %bitcast.82) | data formatting | bytes 1048576 | tf_op jit(solution)/shard_map/convert_element_type | solution.py:109
  23.7 6.7 %all-to-all-start = ((bf16[32,32,256]{2,0,1:T(8,128)(2,1)}), bf16[32,32,256]{2,0,1:T(8,128)(2,1)S(1)}, u32[]{:S(2)}, u32[]{:S(2)}) async-start(bf16[32,32,256]{2,0,1:T(8,128)(2,1)} %copy.48), calls=%async_computation | async-start | bytes 1048576 | tf_op jit(solution)/shard_map/all_to_all | solution.py:112
  30.4 0.1 mul.373
  30.5 0.2 mul.374
  30.7 0.1 multiply_exponential_fusion.2
  30.8 1.2 %convolution_select_fusion = f32[4,256,256]{2,1,0:T(8,128)S(1)} fusion(pred[256,256]{1,0:T(8,128)(4,1)S(1)} %subtract_compare_fusion, f32[4,16]{1,0:T(4,128)S(1)} %get-tuple-element.6, f32[4,16]{1,0:T(4,128)S(1)} %neg.12, f32[4,16]{1,0:T(4,128)S(1)} %get-tuple-element.5), kind=kOutput, calls=%fused_computation.19 | convolution fusion | flops 50642944 | bytes 1114880 | tf_op jit(solution)/shard_map/grm,gms->grs/dot_general | solution.py:56
  32.0 9.6 %all-to-all-done = bf16[32,32,256]{2,0,1:T(8,128)(2,1)S(1)} async-done(((bf16[32,32,256]{2,0,1:T(8,128)(2,1)}), bf16[32,32,256]{2,0,1:T(8,128)(2,1)S(1)}, u32[]{:S(2)}, u32[]{:S(2)}) %all-to-all-start) | async-done | bytes 524320 | tf_op jit(solution)/shard_map/all_to_all | solution.py:112
  41.7 0.4 reshape_reshape.3
  42.1 0.6 copy.50
  42.7 0.3 fusion.12
  43.1 0.3 fusion.35
  43.4 0.4 convolution_add_fusion.2
  43.8 0.6 fusion.20
  44.3 0.1 broadcast_in_dim.38
  44.4 0.7 broadcast_in_dim.43
  45.1 8.2 %all-to-all-start.1 = ((f32[8,1,4096]{2,1,0:T(1,128)}), f32[8,1,4096]{2,1,0:T(1,128)S(1)}, u32[]{:S(2)}, u32[]{:S(2)}) async-start(f32[8,1,4096]{2,1,0:T(1,128)} %broadcast_in_dim.43), calls=%async_computation.1 | async-start | bytes 262144 | tf_op jit(solution)/shard_map/all_to_all | solution.py:71
  53.3 1.3 %convolution_add_fusion.1 = f32[4,4,64,256]{3,2,1,0:T(8,128)} fusion(f32[4,4,64,256]{3,2,1,0:T(8,128)S(1)} %fusion.12, bf16[4,256,4,64]{1,3,0,2:T(8,128)(2,1)S(1)} %copy.50, f32[4,256,256]{2,1,0:T(8,128)S(1)} %convolution_select_fusion), kind=kOutput, calls=%fused_computation.18 | convolution fusion | flops 135528448 | bytes 3670016 | tf_op jit(solution)/shard_map/grs,bsgc->brgc/dot_general | solution.py:44
  54.7 7.0 %all-to-all-done.1 = f32[8,1,4096]{2,1,0:T(1,128)S(1)} async-done(((f32[8,1,4096]{2,1,0:T(1,128)}), f32[8,1,4096]{2,1,0:T(1,128)S(1)}, u32[]{:S(2)}, u32[]{:S(2)}) %all-to-all-start.1) | async-done | bytes 131104 | tf_op jit(solution)/shard_map/all_to_all | solution.py:71
  61.6 0.2 multiply_reduce_fusion
  61.8 0.1 reduce_sum.22
  61.9 0.6 convolution_add_fusion.3
  62.5 2.3 %fusion.6 = bf16[4,256,4,64]{1,3,0,2:T(8,128)(2,1)S(1)} fusion(f32[4,4,64,256]{3,2,1,0:T(8,128)} %convolution_add_fusion.1, f32[4,16,4,64]{3,2,1,0:T(4,128)S(1)} %convolution_add_fusion.3, f32[4,16]{1,0:T(4,128)S(1)} %neg.12, f32[4,16]{1,0:T(4,128)S(1)} %get-tuple-element.5), kind=kOutput, calls=%fused_computation.21 | convolution fusion | flops 50888704 | bytes 1638912 | tf_op jit(solution)/shard_map/grm,gmbc->brgc/dot_general | solution.py:91
  64.9 0.7 copy.56
  65.5 0.7 convert_element_type.133
  66.2 16.6 %all_to_all.32 = bf16[32,32,256]{2,1,0:T(8,128)(2,1)S(1)} all-to-all(bf16[32,32,256]{2,1,0:T(8,128)(2,1)S(1)} %bitcast.83), channel_id=1, replica_groups=mesh['zo'=8,'zi'=4,'mp'=8] {'mp','zi'}, dimensions={0} | all-to-all | bytes 1048576 | tf_op jit(solution)/shard_map/all_to_all | solution.py:124
  82.8 0.1 convert_bitcast_fusion
  82.9 0.1 copy.73
  83.0 2.1 %fusion.9 = bf16[32,8192]{1,0:T(8,128)(2,1)} fusion(f32[32,8192]{1,0:T(8,128)S(1)} %bitcast.78, f32[32,3,8192]{2,0,1:T(8,128)} %copy-done), kind=kLoop, calls=%fused_computation.28 | loop fusion | flops 524288 | bytes 2621440 | tf_op jit(solution)/shard_map/convert_element_type | solution.py:125
  (12 shorter events, 0.2 us)
Async XLA Ops:
  0.0 16.8 %copy-start.1 = (bf16[32,3,8192]{2,0,1:T(8,128)(2,1)S(1)}, bf16[32,3,8192]{2,0,1:T(8,128)(2,1)}, u32[]{:S(2)}) copy-start(bf16[32,3,8192]{2,0,1:T(8,128)(2,1)} %param.5) | copy-start | bytes 4718596
  1.2 15.5 %collective-permute-start = (bf16[6,3,8192]{2,0,1:T(8,128)(2,1)S(1)}, bf16[6,3,8192]{2,0,1:T(8,128)(2,1)S(1)}, u32[]{:S(2)}, u32[]{:S(2)}) collective-permute-start(bf16[6,3,8192]{2,0,1:T(8,128)(2,1)S(1)} %slice.97), channel_id=1, source_target_pairs={{0,1},{1,2},{2,3},{3,4},{4,5},{5,6},{6,7},{7,8},{8,9},{9,10},{10,1... | collective-permute-start | bytes 884744 | tf_op jit(solution)/shard_map/ppermute | solution.py:12
  20.7 1.6 %copy-start = (f32[32,3,8192]{2,0,1:T(8,128)}, f32[32,3,8192]{2,0,1:T(8,128)S(1)}, u32[]{:S(2)}) copy-start(f32[32,3,8192]{2,0,1:T(8,128)S(1)} %multiply_add_fusion) | copy-start | bytes 9437188
  23.7 17.9 %all-to-all-start = ((bf16[32,32,256]{2,0,1:T(8,128)(2,1)}), bf16[32,32,256]{2,0,1:T(8,128)(2,1)S(1)}, u32[]{:S(2)}, u32[]{:S(2)}) async-start(bf16[32,32,256]{2,0,1:T(8,128)(2,1)} %copy.48), calls=%async_computation | async-start | bytes 1048576 | tf_op jit(solution)/shard_map/all_to_all | solution.py:112
  45.1 16.5 %all-to-all-start.1 = ((f32[8,1,4096]{2,1,0:T(1,128)}), f32[8,1,4096]{2,1,0:T(1,128)S(1)}, u32[]{:S(2)}, u32[]{:S(2)}) async-start(f32[8,1,4096]{2,1,0:T(1,128)} %broadcast_in_dim.43), calls=%async_computation.1 | async-start | bytes 262144 | tf_op jit(solution)/shard_map/all_to_all | solution.py:71

commit v7 on v6

--- a/solution.py
+++ b/solution.py
@@ -18,22 +18,14 @@
     return jnp.sum(inside, axis=1) - 1
 
 
-def short_convolution(padded, conv_weight, padded_document_ids, padded_pos, out_rows):
-    kernel_len = conv_weight.shape[1]
-    result = jnp.zeros((out_rows,) + padded.shape[1:], jnp.float32)
-    own_docs = padded_document_ids[kernel_len - 1 :]
+def short_convolution(padded, weight_rows, keep, out_rows, feature, kernel_len):
+    result = None
     for position_shift in range(kernel_len):
         begin_row = kernel_len - 1 - position_shift
-        earlier = padded[begin_row : begin_row + out_rows].astype(jnp.float32)
-        keep_mask = (padded_document_ids[begin_row : begin_row + out_rows] == own_docs) & (
-            padded_pos[begin_row : begin_row + out_rows] >= 0
-        )
-        result = (
-            result
-            + conv_weight[:, position_shift, :][None]
-            * earlier
-            * keep_mask.astype(jnp.float32)[:, None, None]
-        )
+        earlier = padded[begin_row : begin_row + out_rows, feature].astype(jnp.float32)
+        tap = weight_rows[feature * kernel_len + position_shift][None, :]
+        term = (tap * earlier) * keep[:, position_shift : position_shift + 1]
+        result = term if result is None else result + term
     return result
 
 
@@ -104,9 +96,20 @@
     padded_pos = lin_index * rows - (kernel_len - 1) + jnp.arange(rows + kernel_len - 1, dtype=jnp.int32)
     padded_document_ids = document_number_index(doc_lengths, padded_pos)
     padded = jnp.concatenate([tail_rows, proj], axis=0)
-    conv = short_convolution(padded, conv_weight, padded_document_ids, padded_pos, rows)
-    query_part = conv[:, 0]
-    product = (conv[:, 1] * conv[:, 2]).astype(jnp.bfloat16)
+    own_docs = padded_document_ids[kernel_len - 1 :]
+    keep = jnp.stack(
+        [
+            (padded_document_ids[kernel_len - 1 - k : kernel_len - 1 - k + rows] == own_docs)
+            & (padded_pos[kernel_len - 1 - k : kernel_len - 1 - k + rows] >= 0)
+            for k in range(kernel_len)
+        ],
+        axis=1,
+    ).astype(jnp.float32)
+    weight_rows = conv_weight.reshape(-1, conv_weight.shape[2])
+    query_part = short_convolution(padded, weight_rows, keep, rows, 0, kernel_len)
+    keys = short_convolution(padded, weight_rows, keep, rows, 1, kernel_len)
+    values = short_convolution(padded, weight_rows, keep, rows, 2, kernel_len)
+    product = (keys * values).astype(jnp.bfloat16)
 
     swap_axis = ("mp", "zi")
     gathered = lax.all_to_all(product, swap_axis, split_axis=1, concat_axis=0, tiled=True)

time: 85.6 us -> 108 us (1.26); the launches traced: 85.1 us -> 106 us
  local copies, waits for them, and re-layouts: 13.2 us -> 30.5 us
  blocking collectives: 16.6 us -> 0 us
  other arithmetic: 8.71 us -> 16.5 us
  starting transfers between devices: 18.9 us -> 25.5 us
  waiting for transfers between devices: 20.4 us -> 23.6 us
  matrix products: 7.09 us -> 9.57 us
    all_to_all x1 -> x0, blocking collectives: 16.6 us -> none  [shards(): lax.all_to_all(filtered, swap_axis, split_axis=0, concat_axis=1, tiled=True)]
    all_to_all x0 -> x1, waiting for transfers between devices: none -> 9.88 us  [shards(): lax.all_to_all(filtered, swap_axis, split_axis=0, concat_axis=1, tiled=True)]
    mul x0 -> x15, local copies, waits for them, and re-layouts: none -> 6.93 us  [short_convolution(): term = tap * earlier * keep[:, position_shift:position_shift + 1]]
    all_to_all x0 -> x1, starting transfers between devices: none -> 5.49 us  [shards(): lax.all_to_all(filtered, swap_axis, split_axis=0, concat_axis=1, tiled=True)]
    convert_element_type x3 -> x4, other arithmetic: 0.25 us -> 4.86 us  [the longest x1 2.85 us: shards(): product = (keys * values).astype(jnp.bfloat16)]
    add x1 -> x0, other arithmetic: 3.98 us -> none  [short_convolution(): result + conv_weight[:, position_shift, :][None] * earlier * keep_mask.as...]
    ppermute x1, waiting for transfers between devices: 3.77 us -> 0.01 us  [shifted(): return lax.ppermute(block, axis, route)]
    unnamed x9 -> x76, local copies, waits for them, and re-layouts: 2.24 us -> 5.72 us
  transfers between devices with their start and end apart: 3 -> 4, of which waited for: 3 -> 3; matrix products, arithmetic and copies ran while one was open for 12% -> 24% of each run, Pallas kernels for 0% -> 0%
where the time goes in v7:
time: 108 us; the launch traced here: 106 us
  local copies, waits for them, and re-layouts  30.5 us (28%)
  starting transfers between devices  25.5 us (24%)
  waiting for transfers between devices  23.6 us (22%)
  other arithmetic  16.5 us (15%)
  matrix products  9.57 us (9%)
    all_to_all x1, waiting for transfers between devices, shards(): lax.all_to_all(filtered, swap_axis, split_axis=0, concat_axis=1, tiled=True)  9.88 us
    all_to_all x1, starting transfers between devices, long_filter(): lax.all_to_all(sent, outer_axis, split_axis=0, concat_axis=0, tiled=True)  8.19 us
    all_to_all x1, waiting for transfers between devices, shards(): lax.all_to_all(product, swap_axis, split_axis=1, concat_axis=0, tiled=True)  7.84 us
    all_to_all x1, starting transfers between devices, shards(): lax.all_to_all(product, swap_axis, split_axis=1, concat_axis=0, tiled=True)  7.81 us
    mul x15, local copies, waits for them, and re-layouts, short_convolution(): term = tap * earlier * keep[:, position_shift:position_shift + 1]  6.93 us
    all_to_all x1, waiting for transfers between devices, long_filter(): lax.all_to_all(sent, outer_axis, split_axis=0, concat_axis=0, tiled=True)  5.86 us
    unnamed x76, local copies, waits for them, and re-layouts  5.72 us
    all_to_all x1, starting transfers between devices, shards(): lax.all_to_all(filtered, swap_axis, split_axis=0, concat_axis=1, tiled=True)  5.49 us
  transfers between devices with their start and end apart: 4, of which 3 were waited for; matrix products, arithmetic and copies ran while one was open for 24% of the time, Pallas kernels for 0%

profile of v7, /device:TPU:1, one launch (start us, length us, event | category | flops | bytes accessed | tf_op | source)
XLA Modules:
  0.0 106.4 jit_solution(496304347752965021)
XLA Ops:
  0.0 1.1 %slice.225 = bf16[6,3,8192]{2,0,1:T(8,128)(2,1)S(1)} slice(bf16[32,3,8192]{2,0,1:T(8,128)(2,1)} %param.5), slice={[26:32], [0:3], [0:8192]} | slice | bytes 589824 | tf_op jit(solution)/shard_map/slice | solution.py:94
  1.1 4.0 %collective-permute-start = (bf16[6,3,8192]{2,0,1:T(8,128)(2,1)S(1)}, bf16[6,3,8192]{2,0,1:T(8,128)(2,1)S(1)}, u32[]{:S(2)}, u32[]{:S(2)}) collective-permute-start(bf16[6,3,8192]{2,0,1:T(8,128)(2,1)S(1)} %slice.225), channel_id=1, source_target_pairs={{0,1},{1,2},{2,3},{3,4},{4,5},{5,6},{6,7},{7,8},{8,9},{9,10},{10,1... | collective-permute-start | bytes 884744 | tf_op jit(solution)/shard_map/ppermute | solution.py:12
  5.2 0.6 iota_subtract_fusion
  5.7 0.5 subtract_multiply_fusion
  6.2 0.6 iota_add_fusion
  6.8 1.2 %reshape.360 = f32[21,8192]{1,0:T(8,128)S(1)} reshape(f32[3,7,8192]{2,1,0:T(8,128)} %param.6) | data formatting | bytes 1376256 | tf_op jit(solution)/shard_map/reshape | solution.py:108
  8.1 2.3 %slice_reduce_fusion.13 = (f32[8192]{0:T(1024)}, f32[8192]{0:T(1024)S(1)}, f32[8192]{0:T(1024)S(1)}, f32[8192]{0:T(1024)S(1)}, f32[8192]{0:T(1024)S(1)}, /*index...) fusion(f32[21,8192]{1,0:T(8,128)S(1)} %reshape.360), kind=kLoop, calls=%fused_computation.187 | loop fusion | bytes 1179648 | tf_op jit(solution)/shard_map/slice | solution.py:26
  10.5 0.6 iota_compare_fusion.1
  11.2 0.7 copy.47
  11.9 0.9 reduce-window.9
  13.2 0.6 slice_bitcast_fusion.6
  13.8 0.8 mul.652
  14.6 1.4 %mul.647 = f32[32,256]{1,0:T(8,128)} reshape(f32[8192]{0:T(1024)} %get-tuple-element.16) | data formatting | bytes 65536 | tf_op jit(solution)/shard_map/mul | solution.py:27
  16.0 1.4 %mul.642 = f32[32,256]{1,0:T(8,128)} reshape(f32[8192]{0:T(1024)} %get-tuple-element.17) | data formatting | bytes 65536 | tf_op jit(solution)/shard_map/mul | solution.py:27
  17.3 1.4 %mul.637 = f32[32,256]{1,0:T(8,128)} reshape(f32[8192]{0:T(1024)} %get-tuple-element.18) | data formatting | bytes 65536 | tf_op jit(solution)/shard_map/mul | solution.py:27
  18.7 1.4 %mul.632 = f32[32,256]{1,0:T(8,128)} reshape(f32[8192]{0:T(1024)} %get-tuple-element.5) | data formatting | bytes 65536 | tf_op jit(solution)/shard_map/mul | solution.py:27
  20.1 0.7 sqrt_multiply_fusion
  20.8 1.3 %convert_multiply_fusion.7 = f32[4,4]{1,0:T(4,128)} fusion(s32[4]{0:T(128)} %iota_add_fusion), kind=kLoop, calls=%fused_computation.201 | loop fusion | flops 64 | bytes 80 | tf_op jit(solution)/shard_map/mul | solution.py:77
  22.1 1.3 %exponential_select_fusion = f32[8,4,16]{2,1,0:T(4,128)} fusion(f32[8]{0:T(128)S(1)} %multiply_maximum_fusion, f32[4,16]{1,0:T(4,128)S(1)} %neg.12, pred[8]{0:T(512)(128)(4,1)} %iota_compare_fusion.1), kind=kLoop, calls=%fused_computation.200 | loop fusion | flops 1024 | bytes 2344 | tf_op jit(solution)/shard_map/jit(_where)/select_n | solution.py:68
  23.5 0.4 fusion.80
  23.9 0.3 copy.80
  24.3 0.3 copy.79
  24.6 0.3 copy.78
  24.9 1.6 %fusion.62 = (f32[32,1,8192]{2,0,1:T(8,128)S(1)}, f32[32,1,8192]{2,0,1:T(8,128)S(1)}, f32[32,1,8192]{2,0,1:T(8,128)S(1)}, f32[32,1,8192]{2,0,1:T(8,128)S(1)}, f3...) fusion(bf16[32,3,8192]{2,0,1:T(8,128)(2,1)S(1)} %copy-done, ...), kind=kLoop, calls=%fused_computation.123 | loop fusion | flops 9699328 | bytes 12976128 | tf_op jit(solution)/shard_map/convert_element_type | solution.py:25
  26.5 0.3 copy.77
  26.8 0.3 copy.76
  27.1 0.3 copy.75
  27.5 0.3 copy.74
  27.8 0.3 copy.73
  28.1 0.3 copy.72
  28.5 0.3 copy.71
  29.1 0.3 copy.69
  29.5 0.3 copy.68
  30.2 0.3 copy-done.7
  30.6 2.9 %fusion.5 = bf16[32,32,256]{2,1,0:T(8,128)(2,1)S(1)} fusion(f32[4,8,32,256]{3,2,1,0:T(8,128)S(1)} %copy.80, f32[4,8,32,256]{3,2,1,0:T(8,128)S(1)} %copy.79, f32[4,8,32,256]{3,2,1,0:T(8,128)S(1)} %copy.78, f32[4,8,32,256]{3,2,1,0:T(8,128)S(1)} %copy.77, f32[4,8,32,256]{3,2,1,0:T(8,128)S(1)} %copy.76, f32[4,8,32,256]{3,2,1,0:T(8,128)S(1)} %copy.75, ...), kind=kLoop, calls=%fused_computation.45 | loop fusion | flops 11010048 | bytes 15664000 | tf_op jit(solution)/shard_map/convert_element_type | solution.py:112
  33.5 1.1 %copy.48 = bf16[32,32,256]{2,0,1:T(8,128)(2,1)} copy(bf16[32,32,256]{2,1,0:T(8,128)(2,1)S(1)} %fusion.5) | data formatting | bytes 1048576 | tf_op jit(solution)/shard_map/convert_element_type | solution.py:112
  34.6 7.8 %all-to-all-start = ((bf16[32,32,256]{2,0,1:T(8,128)(2,1)}), bf16[32,32,256]{2,0,1:T(8,128)(2,1)}, u32[]{:S(2)}, u32[]{:S(2)}) async-start(bf16[32,32,256]{2,0,1:T(8,128)(2,1)} %copy.48), calls=%async_computation | async-start | bytes 1048576 | tf_op jit(solution)/shard_map/all_to_all | solution.py:115
  42.4 0.6 iota_compare_fusion
  43.2 0.8 mul.723
  44.0 0.7 multiply_exponential_fusion.2
  44.7 1.2 %convolution_select_fusion = f32[4,256,256]{2,1,0:T(8,128)S(1)} fusion(pred[256,256]{1,0:T(8,128)(4,1)S(1)} %subtract_compare_fusion, f32[4,16]{1,0:T(4,128)S(1)} %get-tuple-element.20, f32[4,16]{1,0:T(4,128)S(1)} %neg.12, f32[4,16]{1,0:T(4,128)S(1)} %get-tuple-element.19), kind=kOutput, calls=%fused_computation.36 | convolution fusion | flops 50642944 | bytes 1114880 | tf_op jit(solution)/shard_map/grm,gms->grs/dot_general | solution.py:48
  45.9 7.8 %all-to-all-done = bf16[32,32,256]{2,0,1:T(8,128)(2,1)} async-done(((bf16[32,32,256]{2,0,1:T(8,128)(2,1)}), bf16[32,32,256]{2,0,1:T(8,128)(2,1)}, u32[]{:S(2)}, u32[]{:S(2)}) %all-to-all-start) | async-done | bytes 524320 | tf_op jit(solution)/shard_map/all_to_all | solution.py:115
  53.7 1.1 %copy.49 = bf16[4,8,32,256]{3,2,1,0:T(8,128)(2,1)S(1)} copy(bf16[4,8,32,256]{3,2,0,1:T(8,128)(2,1)} %bitcast.31) | data formatting | bytes 1048576 | tf_op jit(solution)/shard_map/transpose | solution.py:117
  54.8 1.4 %reshape_reshape.3 = bf16[4,256,4,64]{3,2,1,0:T(4,128)(2,1)} reshape(bf16[4,8,32,256]{3,2,1,0:T(8,128)(2,1)S(1)} %copy.49) | data formatting | bytes 1048576 | tf_op jit(solution)/shard_map/reshape;reshape | solution.py:51
  56.2 1.6 %copy.50 = bf16[4,256,4,64]{1,3,0,2:T(8,128)(2,1)S(1)} copy(bf16[4,256,4,64]{3,2,1,0:T(4,128)(2,1)} %reshape_reshape.3) | data formatting | bytes 1048576 | tf_op jit(solution)/shard_map/reshape;reshape | solution.py:51
  57.8 1.3 %fusion.82 = f32[4,4,64,256]{3,2,1,0:T(8,128)} fusion(bf16[4,256,4,64]{1,3,0,2:T(8,128)(2,1)S(1)} %copy.50, f32[4,256,256]{2,1,0:T(8,128)S(1)} %convolution_select_fusion), kind=kOutput, calls=%fused_computation.144 | convolution fusion | flops 134479872 | bytes 2621440 | tf_op jit(solution)/shard_map/grs,bsgc->brgc/dot_general | solution.py:35
  59.5 0.4 convolution_add_fusion.2
  59.8 0.7 copy-done.11
  60.5 1.2 %fusion.90 = f32[4,16,1,64]{3,2,1,0:T(1,128)} fusion(f32[4,16,4,1]{2,3,1,0:T(1,128)S(1)} %bitcast.297, f32[4,16,4,64]{3,1,2,0:T(8,128)S(1)} %convolution_add_fusion.2), kind=kOutput, calls=%fused_computation.156 | convolution fusion | flops 196608 | bytes 82944 | tf_op jit(solution)/shard_map/gmb,gmbc->gmc/dot_general | solution.py:59
  61.7 1.4 %broadcast_in_dim.42 = f32[4096]{0:T(1024)} reshape(f32[4,16,64]{2,1,0:T(8,128)} %bitcast.296) | data formatting | bytes 32768 | tf_op jit(solution)/shard_map/broadcast_in_dim | solution.py:62
  63.1 1.4 %broadcast_in_dim.43 = f32[8,1,4096]{2,1,0:T(1,128)} broadcast(f32[4096]{0:T(1024)} %broadcast_in_dim.42), dimensions={2} | broadcast | bytes 147456 | tf_op jit(solution)/shard_map/broadcast_in_dim | solution.py:62
  64.5 8.2 %all-to-all-start.1 = ((f32[8,1,4096]{2,1,0:T(1,128)}), f32[8,1,4096]{2,1,0:T(1,128)}, u32[]{:S(2)}, u32[]{:S(2)}) async-start(f32[8,1,4096]{2,1,0:T(1,128)} %broadcast_in_dim.43), calls=%async_computation.1 | async-start | bytes 262144 | tf_op jit(solution)/shard_map/all_to_all | solution.py:63
  72.7 2.6 %convolution_add_fusion.1 = f32[4,4,64,256]{3,2,1,0:T(8,128)} fusion(f32[4,4,64,256]{3,2,1,0:T(8,128)} %fusion.82, bf16[4,256,4,64]{1,3,0,2:T(8,128)(2,1)S(1)} %copy.50, f32[4,256,256]{2,1,0:T(8,128)S(1)} %convolution_select_fusion), kind=kOutput, calls=%fused_computation.35 | convolution fusion | flops 135528448 | bytes 3670016 | tf_op jit(solution)/shard_map/grs,bsgc->brgc/dot_general | solution.py:36
  75.3 5.9 %all-to-all-done.1 = f32[8,1,4096]{2,1,0:T(1,128)} async-done(((f32[8,1,4096]{2,1,0:T(1,128)}), f32[8,1,4096]{2,1,0:T(1,128)}, u32[]{:S(2)}, u32[]{:S(2)}) %all-to-all-start.1) | async-done | bytes 131104 | tf_op jit(solution)/shard_map/all_to_all | solution.py:63
  81.2 1.1 %multiply_reduce_fusion = f32[4096]{0:T(1024)S(1)} fusion(f32[8,1,4096]{2,1,0:T(1,128)} %mul.723, f32[8,1,4096]{2,1,0:T(1,128)} %all-to-all-done.1), kind=kLoop, calls=%fused_computation.152 | loop fusion | flops 61440 | bytes 278528 | tf_op jit(solution)/shard_map/reduce_sum | solution.py:73
  82.4 1.5 %convolution_add_fusion.3 = f32[4,16,4,64]{3,2,1,0:T(4,128)S(1)} fusion(f32[4,16,4,64]{3,1,2,0:T(8,128)} %copy-done.11, f32[4,16,64]{2,1,0:T(8,128)S(1)} %reduce_sum.22, f32[4,16,4]{2,1,0:T(8,128)} %get-tuple-element.49, f32[4,4]{1,0:T(4,128)S(1)} %copy-done.27, f32[4,16]{1,0:T(4,128)S(1)} %neg.12, pred[4,4]{1,0:T(4,128)(4,1)} %iota_compare_fusion), kind=kOutput, calls=%fused_computation.40 | convolution fusion | flops 821248 | bytes 148816 | tf_op jit(solution)/shard_map/gmab,gmbc->gmac/dot_general | solution.py:80
  83.9 1.1 %fusion.1 = bf16[4,256,4,64]{1,3,0,2:T(8,128)(2,1)S(1)} fusion(f32[4,4,64,256]{3,2,1,0:T(8,128)S(1)} %copy-done.1, f32[4,16,4,64]{3,2,1,0:T(4,128)S(1)} %convolution_add_fusion.3, f32[4,16]{1,0:T(4,128)S(1)} %neg.12, f32[4,16]{1,0:T(4,128)S(1)} %get-tuple-element.19), kind=kOutput, calls=%fused_computation.38 | convolution fusion | flops 50888704 | bytes 1638912 | tf_op jit(solution)/shard_map/grm,gmbc->brgc/dot_general | solution.py:83
  85.0 0.7 copy.56
  85.7 0.7 convert_element_type.259
  86.4 0.8 copy.57
  87.2 5.5 %all-to-all-start.2 = ((bf16[32,32,256]{2,1,0:T(8,128)(2,1)}), bf16[32,32,256]{2,1,0:T(8,128)(2,1)S(1)}, u32[]{:S(2)}, u32[]{:S(2)}) async-start(bf16[32,32,256]{2,1,0:T(8,128)(2,1)} %bitcast.48), calls=%async_computation.2 | async-start | bytes 1048576 | tf_op jit(solution)/shard_map/all_to_all | solution.py:127
  92.7 1.3 %fusion.117 = (f32[1,8192]{1,0:T(1,128)S(1)}, f32[1,8192]{1,0:T(1,128)S(1)}, f32[1,8192]{1,0:T(1,128)S(1)}) fusion(f32[21,8192]{1,0:T(8,128)} %copy-done.2), kind=kLoop, calls=%fused_computation.228 | loop fusion | bytes 196608 | tf_op jit(solution)/shard_map/slice | solution.py:26
  94.1 9.9 %all-to-all-done.2 = bf16[32,32,256]{2,1,0:T(8,128)(2,1)S(1)} async-done(((bf16[32,32,256]{2,1,0:T(8,128)(2,1)}), bf16[32,32,256]{2,1,0:T(8,128)(2,1)S(1)}, u32[]{:S(2)}, u32[]{:S(2)}) %all-to-all-start.2) | async-done | bytes 524320 | tf_op jit(solution)/shard_map/all_to_all | solution.py:127
  104.3 2.1 %fusion.33 = bf16[32,8192]{1,0:T(8,128)(2,1)} fusion(f32[32,8192]{1,0:T(8,128)S(1)} %bitcast.279, bf16[32,3,8192]{2,0,1:T(8,128)(2,1)S(1)} %copy-done, bf16[6,3,8192]{2,0,1:T(8,128)(2,1)S(1)} %collective-permute-done, f32[32]{0:T(128)S(1)} %copy-done.15, f32[8192]{0:T(1024)S(1)} %bitcast.294, f32[32]{0:T(128)S(1)} %copy-done.17, f32[8192]{0:T(1024)S(1)} %bitcast.295, ...), kind=kLoop, calls=%fused_computation.87 | loop fusion | flops 13893632 | bytes 4296192 | tf_op jit(solution)/shard_map/convert_element_type | solution.py:128
  (89 shorter events, 2.2 us)
Async XLA Ops:
  1.1 22.4 %collective-permute-start = (bf16[6,3,8192]{2,0,1:T(8,128)(2,1)S(1)}, bf16[6,3,8192]{2,0,1:T(8,128)(2,1)S(1)}, u32[]{:S(2)}, u32[]{:S(2)}) collective-permute-start(bf16[6,3,8192]{2,0,1:T(8,128)(2,1)S(1)} %slice.225), channel_id=1, source_target_pairs={{0,1},{1,2},{2,3},{3,4},{4,5},{5,6},{6,7},{7,8},{8,9},{9,10},{10,1... | collective-permute-start | bytes 884744 | tf_op jit(solution)/shard_map/ppermute | solution.py:12
  6.8 4.4 %copy-start.28 = (s32[64]{0:T(128)S(1)}, s32[64]{0:T(128)}, u32[]{:S(2)}) copy-start(s32[64]{0:T(128)} %param.9) | copy-start | bytes 772
  8.1 15.8 %copy-start.2 = (f32[21,8192]{1,0:T(8,128)}, f32[21,8192]{1,0:T(8,128)S(1)}, u32[]{:S(2)}) copy-start(f32[21,8192]{1,0:T(8,128)S(1)} %reshape.360) | copy-start | bytes 2064388
  8.1 15.4 %copy-start = (bf16[32,3,8192]{2,0,1:T(8,128)(2,1)S(1)}, bf16[32,3,8192]{2,0,1:T(8,128)(2,1)}, u32[]{:S(2)}) copy-start(bf16[32,3,8192]{2,0,1:T(8,128)(2,1)} %param.5) | copy-start | bytes 4718596
  29.8 0.8 copy-start.7
  29.8 0.8 copy-start.8
  29.8 0.8 copy-start.9
  29.8 0.8 copy-start.10
  29.8 0.8 copy-start.14
  29.8 0.8 copy-start.16
  29.9 0.8 copy-start.18
  29.9 0.8 copy-start.20
  29.9 0.7 copy-start.22
  29.9 0.7 copy-start.24
  33.5 9.5 %copy-start.12 = (f32[8,4,16]{2,1,0:T(4,128)S(1)}, f32[8,4,16]{2,1,0:T(4,128)}, u32[]{:S(2)}) copy-start(f32[8,4,16]{2,1,0:T(4,128)} %exponential_select_fusion) | copy-start | bytes 6148
  33.5 10.5 %copy-start.29 = (f32[4]{0:T(128)S(1)}, f32[4]{0:T(128)}, u32[]{:S(2)}) copy-start(f32[4]{0:T(128)} %get-tuple-element.57) | copy-start | bytes 52
  33.5 10.5 %copy-start.30 = (f32[4]{0:T(128)S(1)}, f32[4]{0:T(128)}, u32[]{:S(2)}) copy-start(f32[4]{0:T(128)} %get-tuple-element.58) | copy-start | bytes 52
  34.6 19.1 %all-to-all-start = ((bf16[32,32,256]{2,0,1:T(8,128)(2,1)}), bf16[32,32,256]{2,0,1:T(8,128)(2,1)}, u32[]{:S(2)}, u32[]{:S(2)}) async-start(bf16[32,32,256]{2,0,1:T(8,128)(2,1)} %copy.48), calls=%async_computation | async-start | bytes 1048576 | tf_op jit(solution)/shard_map/all_to_all | solution.py:115
  57.8 1.3 %copy-start.26 = (f32[256]{0:T(256)S(1)}, f32[256]{0:T(256)}, u32[]{:S(2)}) copy-start(f32[256]{0:T(256)} %iota_subtract_fusion) | copy-start | bytes 3076
  57.8 2.7 %copy-start.13 = (f32[4,16,4]{2,1,0:T(8,128)S(1)}, f32[4,16,4]{2,1,0:T(8,128)}, u32[]{:S(2)}) copy-start(f32[4,16,4]{2,1,0:T(8,128)} %get-tuple-element.50) | copy-start | bytes 3076
  59.8 0.7 copy-start.11
  64.5 16.6 %all-to-all-start.1 = ((f32[8,1,4096]{2,1,0:T(1,128)}), f32[8,1,4096]{2,1,0:T(1,128)}, u32[]{:S(2)}, u32[]{:S(2)}) async-start(f32[8,1,4096]{2,1,0:T(1,128)} %broadcast_in_dim.43), calls=%async_computation.1 | async-start | bytes 262144 | tf_op jit(solution)/shard_map/all_to_all | solution.py:63
  72.7 9.6 %copy-start.27 = (f32[4,4]{1,0:T(4,128)S(1)}, f32[4,4]{1,0:T(4,128)}, u32[]{:S(2)}) copy-start(f32[4,4]{1,0:T(4,128)} %convert_multiply_fusion.7) | copy-start | bytes 196
  75.3 8.6 %copy-start.1 = (f32[4,4,64,256]{3,2,1,0:T(8,128)S(1)}, f32[4,4,64,256]{3,2,1,0:T(8,128)}, u32[]{:S(2)}) copy-start(f32[4,4,64,256]{3,2,1,0:T(8,128)} %convolution_add_fusion.1) | copy-start | bytes 3145732
  87.2 16.7 %all-to-all-start.2 = ((bf16[32,32,256]{2,1,0:T(8,128)(2,1)}), bf16[32,32,256]{2,1,0:T(8,128)(2,1)S(1)}, u32[]{:S(2)}, u32[]{:S(2)}) async-start(bf16[32,32,256]{2,1,0:T(8,128)(2,1)} %bitcast.48), calls=%async_computation.2 | async-start | bytes 1048576 | tf_op jit(solution)/shard_map/all_to_all | solution.py:127
  94.0 10.2 %copy-start.3 = (f32[1,8192]{1,0:T(1,128)S(1)}, f32[1,8192]{1,0:T(1,128)}, u32[]{:S(2)}) copy-start(f32[1,8192]{1,0:T(1,128)} %get-tuple-element.35) | copy-start | bytes 98308
  94.0 10.2 %copy-start.4 = (f32[1,8192]{1,0:T(1,128)S(1)}, f32[1,8192]{1,0:T(1,128)}, u32[]{:S(2)}) copy-start(f32[1,8192]{1,0:T(1,128)} %get-tuple-element.36) | copy-start | bytes 98308
  94.0 10.2 %copy-start.5 = (f32[1,8192]{1,0:T(1,128)S(1)}, f32[1,8192]{1,0:T(1,128)}, u32[]{:S(2)}) copy-start(f32[1,8192]{1,0:T(1,128)} %get-tuple-element.37) | copy-start | bytes 98308
  94.0 10.2 %copy-start.6 = (f32[1,8192]{1,0:T(1,128)S(1)}, f32[1,8192]{1,0:T(1,128)}, u32[]{:S(2)}) copy-start(f32[1,8192]{1,0:T(1,128)} %get-tuple-element.38) | copy-start | bytes 98308
  94.0 10.2 %copy-start.15 = (f32[32]{0:T(128)S(1)}, f32[32]{0:T(128)}, u32[]{:S(2)}) copy-start(f32[32]{0:T(128)} %get-tuple-element.43) | copy-start | bytes 388
  94.0 10.2 %copy-start.17 = (f32[32]{0:T(128)S(1)}, f32[32]{0:T(128)}, u32[]{:S(2)}) copy-start(f32[32]{0:T(128)} %get-tuple-element.44) | copy-start | bytes 388
  94.0 10.2 %copy-start.19 = (f32[32]{0:T(128)S(1)}, f32[32]{0:T(128)}, u32[]{:S(2)}) copy-start(f32[32]{0:T(128)} %get-tuple-element.45) | copy-start | bytes 388
  94.0 10.2 %copy-start.21 = (f32[32]{0:T(128)S(1)}, f32[32]{0:T(128)}, u32[]{:S(2)}) copy-start(f32[32]{0:T(128)} %get-tuple-element.46) | copy-start | bytes 388
  94.1 10.2 %copy-start.23 = (f32[32]{0:T(128)S(1)}, f32[32]{0:T(128)}, u32[]{:S(2)}) copy-start(f32[32]{0:T(128)} %get-tuple-element.47) | copy-start | bytes 388
  94.1 10.2 %copy-start.25 = (f32[32]{0:T(128)S(1)}, f32[32]{0:T(128)}, u32[]{:S(2)}) copy-start(f32[32]{0:T(128)} %get-tuple-element.48) | copy-start | bytes 388

commit v8 on v7

--- a/solution.py
+++ b/solution.py
@@ -1,6 +1,8 @@
 import jax
 import jax.numpy as jnp
 from jax import lax
+from jax.experimental import pallas as pl
+from jax.experimental.pallas import tpu as pltpu
 from jax.sharding import Mesh, NamedSharding, PartitionSpec as P
 
 HIGHEST = lax.Precision.HIGHEST
@@ -18,15 +20,47 @@
     return jnp.sum(inside, axis=1) - 1
 
 
-def short_convolution(padded, weight_rows, keep, out_rows, feature, kernel_len):
-    result = None
-    for position_shift in range(kernel_len):
-        begin_row = kernel_len - 1 - position_shift
-        earlier = padded[begin_row : begin_row + out_rows, feature].astype(jnp.float32)
-        tap = weight_rows[feature * kernel_len + position_shift][None, :]
-        term = (tap * earlier) * keep[:, position_shift : position_shift + 1]
-        result = term if result is None else result + term
-    return result
+def conv_kernel(x_ref, w_ref, keep_ref, q_ref, u_ref, scratch):
+    kernel_len = w_ref.shape[1]
+    out_rows = q_ref.shape[0]
+    keep = keep_ref[...]
+    results = []
+    for feature in range(x_ref.shape[0]):
+        scratch[0 : out_rows + kernel_len - 1, :] = x_ref[feature].astype(jnp.float32)
+        weights = w_ref[feature]
+        total = None
+        for position_shift in range(kernel_len):
+            begin_row = kernel_len - 1 - position_shift
+            earlier = scratch[begin_row : begin_row + out_rows, :]
+            term = earlier * weights[position_shift : position_shift + 1, :] * keep[:, position_shift : position_shift + 1]
+            total = term if total is None else total + term
+        results.append(total)
+    q_ref[...] = results[0]
+    u_ref[...] = (results[1] * results[2]).astype(u_ref.dtype)
+
+
+def short_convolution(padded, conv_weight, keep, out_rows):
+    features, padded_rows, channels = padded.shape
+    kernel_len = conv_weight.shape[1]
+    tile = 1024 if channels % 1024 == 0 else channels
+    return pl.pallas_call(
+        conv_kernel,
+        grid=(channels // tile,),
+        in_specs=[
+            pl.BlockSpec((features, padded_rows, tile), lambda j: (0, 0, j)),
+            pl.BlockSpec((features, kernel_len, tile), lambda j: (0, 0, j)),
+            pl.BlockSpec(keep.shape, lambda j: (0, 0)),
+        ],
+        out_specs=[
+            pl.BlockSpec((out_rows, tile), lambda j: (0, j)),
+            pl.BlockSpec((out_rows, tile), lambda j: (0, j)),
+        ],
+        out_shape=[
+            jax.ShapeDtypeStruct((out_rows, channels), jnp.float32),
+            jax.ShapeDtypeStruct((out_rows, channels), jnp.bfloat16),
+        ],
+        scratch_shapes=[pltpu.VMEM((padded_rows + 8 - padded_rows % 8, tile), jnp.float32)],
+    )(padded, conv_weight, keep)
 
 
 def split_product(form, weights, inputs):
@@ -95,21 +129,18 @@
     lin_index = (lax.axis_index("zo") * inner_size + lax.axis_index("zi")) * mp_size + lax.axis_index("mp")
     padded_pos = lin_index * rows - (kernel_len - 1) + jnp.arange(rows + kernel_len - 1, dtype=jnp.int32)
     padded_document_ids = document_number_index(doc_lengths, padded_pos)
-    padded = jnp.concatenate([tail_rows, proj], axis=0)
+    padded = jnp.concatenate([tail_rows, proj], axis=0).transpose(1, 0, 2)
     own_docs = padded_document_ids[kernel_len - 1 :]
     keep = jnp.stack(
         [
             (padded_document_ids[kernel_len - 1 - k : kernel_len - 1 - k + rows] == own_docs)
             & (padded_pos[kernel_len - 1 - k : kernel_len - 1 - k + rows] >= 0)
             for k in range(kernel_len)
-        ],
+        ]
+        + [jnp.zeros((rows,), bool)] * (8 - kernel_len % 8),
         axis=1,
     ).astype(jnp.float32)
-    weight_rows = conv_weight.reshape(-1, conv_weight.shape[2])
-    query_part = short_convolution(padded, weight_rows, keep, rows, 0, kernel_len)
-    keys = short_convolution(padded, weight_rows, keep, rows, 1, kernel_len)
-    values = short_convolution(padded, weight_rows, keep, rows, 2, kernel_len)
-    product = (keys * values).astype(jnp.bfloat16)
+    query_part, product = short_convolution(padded, conv_weight, keep, rows)
 
     swap_axis = ("mp", "zi")
     gathered = lax.all_to_all(product, swap_axis, split_axis=1, concat_axis=0, tiled=True)

time: 108 us -> 92.4 us (0.86)
  local copies, waits for them, and re-layouts: 30.5 us -> 9.14 us
  blocking collectives: 0 us -> 16.5 us
  other arithmetic: 16.5 us -> 6.64 us
  Pallas kernels: 0 us -> 8.66 us
  starting transfers between devices: 25.5 us -> 18.9 us
  matrix products: 9.57 us -> 7.09 us
    all_to_all x0 -> x1, blocking collectives: none -> 16.5 us  [shards(): lax.all_to_all(filtered, swap_axis, split_axis=0, concat_axis=1, tiled=True)]
    all_to_all x1 -> x0, waiting for transfers between devices: 9.88 us -> none  [shards(): lax.all_to_all(filtered, swap_axis, split_axis=0, concat_axis=1, tiled=True)]
    pallas_call x0 -> x1, Pallas kernels: none -> 8.66 us  [short_convolution(): pl.pallas_call(conv_kernel, grid=(channels // tile,), in_specs=[pl.BlockS...]
    ppermute x1, waiting for transfers between devices: 0.01 us -> 7.79 us  [shifted(): return lax.ppermute(block, axis, route)]
    mul x15 -> x0, local copies, waits for them, and re-layouts: 6.93 us -> none  [short_convolution(): term = tap * earlier * keep[:, position_shift:position_shift + 1]]
    all_to_all x1 -> x0, starting transfers between devices: 5.49 us -> none  [shards(): lax.all_to_all(filtered, swap_axis, split_axis=0, concat_axis=1, tiled=True)]
    convert_element_type x3 -> x0, other arithmetic: 4.85 us -> none  [the longest x1 2.85 us: shards(): product = (keys * values).astype(jnp.bfloat16)]
    unnamed x76 -> x2, local copies, waits for them, and re-layouts: 5.72 us -> 1.01 us
  transfers between devices with their start and end apart: 4 -> 3, of which waited for: 3 -> 3; matrix products, arithmetic and copies ran while one was open for 24% -> 7% of each run, Pallas kernels for 0% -> 0%
where the time goes in v8:
time: 92.4 us; the launch traced here: 91.6 us
  waiting for transfers between devices  24.4 us (26%)
  starting transfers between devices  18.9 us (20%)
  blocking collectives  16.5 us (18%)
  local copies, waits for them, and re-layouts  9.14 us (10%)
  Pallas kernels  8.66 us (9%)
  matrix products  7.09 us (8%)
  other arithmetic  6.64 us (7%)
    all_to_all x1, blocking collectives, shards(): lax.all_to_all(filtered, swap_axis, split_axis=0, concat_axis=1, tiled=True)  16.5 us
    all_to_all x1, waiting for transfers between devices, shards(): lax.all_to_all(product, swap_axis, split_axis=1, concat_axis=0, tiled=True)  9.64 us
    pallas_call x1, Pallas kernels, short_convolution(): pl.pallas_call(conv_kernel, grid=(channels // tile,), in_specs=[pl.BlockS...  8.66 us
    all_to_all x1, starting transfers between devices, long_filter(): lax.all_to_all(sent, outer_axis, split_axis=0, concat_axis=0, tiled=True)  8.19 us
    ppermute x1, waiting for transfers between devices, shifted(): return lax.ppermute(block, axis, route)  7.79 us
    all_to_all x1, waiting for transfers between devices, long_filter(): lax.all_to_all(sent, outer_axis, split_axis=0, concat_axis=0, tiled=True)  7 us
    all_to_all x1, starting transfers between devices, shards(): lax.all_to_all(product, swap_axis, split_axis=1, concat_axis=0, tiled=True)  6.68 us
    ppermute x1, starting transfers between devices, shifted(): return lax.ppermute(block, axis, route)  4.02 us
  transfers between devices with their start and end apart: 3, of which 3 were waited for; matrix products, arithmetic and copies ran while one was open for 7% of the time, Pallas kernels for 0%

profile of v8, /device:TPU:1, one launch (start us, length us, event | category | flops | bytes accessed | tf_op | source)
XLA Modules:
  0.0 91.6 jit_solution(15335326277309455737)
XLA Ops:
  0.0 1.1 %slice.46 = bf16[6,3,8192]{2,0,1:T(8,128)(2,1)S(1)} slice(bf16[32,3,8192]{2,0,1:T(8,128)(2,1)} %param.5), slice={[26:32], [0:3], [0:8192]} | slice | bytes 589824 | tf_op jit(solution)/shard_map/slice | solution.py:128
  1.1 4.0 %collective-permute-start = (bf16[6,3,8192]{2,0,1:T(8,128)(2,1)S(1)}, bf16[6,3,8192]{2,0,1:T(8,128)(2,1)S(1)}, u32[]{:S(2)}, u32[]{:S(2)}) collective-permute-start(bf16[6,3,8192]{2,0,1:T(8,128)(2,1)S(1)} %slice.46), channel_id=1, source_target_pairs={{0,1},{1,2},{2,3},{3,4},{4,5},{5,6},{6,7},{7,8},{8,9},{9,10},{10,1... | collective-permute-start | bytes 884744 | tf_op jit(solution)/shard_map/ppermute | solution.py:14
  5.2 0.1 compare_bitcast_fusion
  5.3 0.7 copy.72
  6.1 0.1 reduce-window.9
  6.2 0.1 reduce.3
  6.3 0.7 sub.82
  6.9 0.2 convert_reduce_fusion
  7.1 0.1 and_bitcast_fusion
  7.3 0.7 copy.73.keep_ref
  7.9 0.7 sqrt_multiply_fusion
  8.7 0.1 convert_multiply_fusion
  8.7 0.1 exponential_select_fusion
  8.8 7.8 %collective-permute-done = bf16[6,3,8192]{2,0,1:T(8,128)(2,1)S(1)} collective-permute-done((bf16[6,3,8192]{2,0,1:T(8,128)(2,1)S(1)}, bf16[6,3,8192]{2,0,1:T(8,128)(2,1)S(1)}, u32[]{:S(2)}, u32[]{:S(2)}) %collective-permute-start) | collective-permute-done | bytes 294944 | tf_op jit(solution)/shard_map/ppermute | solution.py:14
  16.6 3.2 %maximum_bitcast_fusion.x_ref = bf16[3,38,8192]{2,1,0:T(8,128)(2,1)} fusion(bf16[32,3,8192]{2,0,1:T(8,128)(2,1)} %param.5, bf16[6,3,8192]{2,0,1:T(8,128)(2,1)S(1)} %collective-permute-done), kind=kLoop, calls=%fused_computation | loop fusion | flops 3735552 | bytes 3735552 | tf_op jit(solution)/shard_map/transpose | solution.py:132
  19.9 8.7 %shard_map.55 = (f32[32,8192]{1,0:T(8,128)}, bf16[32,8192]{1,0:T(8,128)(2,1)}) custom-call(bf16[3,38,8192]{2,1,0:T(8,128)(2,1)} %maximum_bitcast_fusion.x_ref, f32[3,7,8192]{2,1,0:T(8,128)} %w_ref.1, f32[32,8]{1,0:T(8,128)} %copy.73.keep_ref), custom_call_target="tpu_custom_call" | custom-call | tf_op jit(solution)/shard_map/pallas_call | solution.py:46
  28.5 1.9 %copy.101 = bf16[4,32,8,256]{3,2,0,1:T(8,128)(2,1)} copy(bf16[4,32,8,256]{3,2,1,0:T(8,128)(2,1)} %bitcast.77) | data formatting | bytes 1048576 | tf_op jit(solution)/shard_map/all_to_all | solution.py:146
  30.4 6.7 %all-to-all-start = ((bf16[32,32,256]{2,0,1:T(8,128)(2,1)}), bf16[32,32,256]{2,0,1:T(8,128)(2,1)S(1)}, u32[]{:S(2)}, u32[]{:S(2)}) async-start(bf16[32,32,256]{2,0,1:T(8,128)(2,1)} %bitcast.72), calls=%async_computation | async-start | bytes 1048576 | tf_op jit(solution)/shard_map/all_to_all | solution.py:146
  37.1 0.1 mul.206
  37.3 0.2 mul.207
  37.4 0.1 multiply_exponential_fusion.2
  37.5 1.2 %convolution_select_fusion = f32[4,256,256]{2,1,0:T(8,128)S(1)} fusion(pred[256,256]{1,0:T(8,128)(4,1)S(1)} %subtract_compare_fusion, f32[4,16]{1,0:T(4,128)S(1)} %get-tuple-element.10, f32[4,16]{1,0:T(4,128)S(1)} %neg.12, f32[4,16]{1,0:T(4,128)S(1)} %get-tuple-element.9), kind=kOutput, calls=%fused_computation.3 | convolution fusion | flops 50642944 | bytes 1114880 | tf_op jit(solution)/shard_map/grm,gms->grs/dot_general | solution.py:82
  38.7 9.6 %all-to-all-done = bf16[32,32,256]{2,0,1:T(8,128)(2,1)S(1)} async-done(((bf16[32,32,256]{2,0,1:T(8,128)(2,1)}), bf16[32,32,256]{2,0,1:T(8,128)(2,1)S(1)}, u32[]{:S(2)}, u32[]{:S(2)}) %all-to-all-start) | async-done | bytes 524320 | tf_op jit(solution)/shard_map/all_to_all | solution.py:146
  48.4 0.4 reshape_reshape.3
  48.8 0.6 copy.76
  49.5 0.3 fusion.4
  49.8 0.3 fusion.27
  50.1 0.4 convolution_add_fusion.2
  50.5 0.6 fusion.12
  51.1 0.1 broadcast_in_dim.42
  51.1 0.7 broadcast_in_dim.43
  51.9 8.2 %all-to-all-start.1 = ((f32[8,1,4096]{2,1,0:T(1,128)}), f32[8,1,4096]{2,1,0:T(1,128)S(1)}, u32[]{:S(2)}, u32[]{:S(2)}) async-start(f32[8,1,4096]{2,1,0:T(1,128)} %broadcast_in_dim.43), calls=%async_computation.1 | async-start | bytes 262144 | tf_op jit(solution)/shard_map/all_to_all | solution.py:97
  60.1 1.3 %convolution_add_fusion.1 = f32[4,4,64,256]{3,2,1,0:T(8,128)} fusion(f32[4,4,64,256]{3,2,1,0:T(8,128)S(1)} %fusion.4, bf16[4,256,4,64]{1,3,0,2:T(8,128)(2,1)S(1)} %copy.76, f32[4,256,256]{2,1,0:T(8,128)S(1)} %convolution_select_fusion), kind=kOutput, calls=%fused_computation.2 | convolution fusion | flops 135528448 | bytes 3670016 | tf_op jit(solution)/shard_map/grs,bsgc->brgc/dot_general | solution.py:70
  61.4 7.0 %all-to-all-done.1 = f32[8,1,4096]{2,1,0:T(1,128)S(1)} async-done(((f32[8,1,4096]{2,1,0:T(1,128)}), f32[8,1,4096]{2,1,0:T(1,128)S(1)}, u32[]{:S(2)}, u32[]{:S(2)}) %all-to-all-start.1) | async-done | bytes 131104 | tf_op jit(solution)/shard_map/all_to_all | solution.py:97
  68.4 0.2 multiply_reduce_fusion
  68.5 0.1 reduce_sum.22
  68.6 0.6 convolution_add_fusion.3
  69.3 2.3 %fusion.1 = bf16[4,256,4,64]{1,3,0,2:T(8,128)(2,1)S(1)} fusion(f32[4,4,64,256]{3,2,1,0:T(8,128)} %convolution_add_fusion.1, f32[4,16,4,64]{3,2,1,0:T(4,128)S(1)} %convolution_add_fusion.3, f32[4,16]{1,0:T(4,128)S(1)} %neg.12, f32[4,16]{1,0:T(4,128)S(1)} %get-tuple-element.9), kind=kOutput, calls=%fused_computation.5 | convolution fusion | flops 50888704 | bytes 1638912 | tf_op jit(solution)/shard_map/grm,gmbc->brgc/dot_general | solution.py:117
  71.6 0.7 copy.82
  72.3 0.7 convert_element_type.72
  73.0 16.5 %all_to_all.35 = bf16[32,32,256]{2,1,0:T(8,128)(2,1)S(1)} all-to-all(bf16[32,32,256]{2,1,0:T(8,128)(2,1)S(1)} %bitcast.76), channel_id=1, replica_groups=mesh['zo'=8,'zi'=4,'mp'=8] {'mp','zi'}, dimensions={0} | all-to-all | bytes 1048576 | tf_op jit(solution)/shard_map/all_to_all | solution.py:158
  89.5 0.0 copy-start
  89.5 0.1 convert_bitcast_fusion
  89.6 0.1 copy.93
  89.7 1.0 %copy-done = f32[32,8192]{1,0:T(8,128)S(1)} copy-done((f32[32,8192]{1,0:T(8,128)S(1)}, f32[32,8192]{1,0:T(8,128)}, u32[]{:S(2)}) %copy-start) | copy-done | bytes 1048600
  90.8 0.9 multiply_convert_fusion
  (15 shorter events, 0.2 us)
Async XLA Ops:
  1.1 15.5 %collective-permute-start = (bf16[6,3,8192]{2,0,1:T(8,128)(2,1)S(1)}, bf16[6,3,8192]{2,0,1:T(8,128)(2,1)S(1)}, u32[]{:S(2)}, u32[]{:S(2)}) collective-permute-start(bf16[6,3,8192]{2,0,1:T(8,128)(2,1)S(1)} %slice.46), channel_id=1, source_target_pairs={{0,1},{1,2},{2,3},{3,4},{4,5},{5,6},{6,7},{7,8},{8,9},{9,10},{10,1... | collective-permute-start | bytes 884744 | tf_op jit(solution)/shard_map/ppermute | solution.py:14
  30.4 17.9 %all-to-all-start = ((bf16[32,32,256]{2,0,1:T(8,128)(2,1)}), bf16[32,32,256]{2,0,1:T(8,128)(2,1)S(1)}, u32[]{:S(2)}, u32[]{:S(2)}) async-start(bf16[32,32,256]{2,0,1:T(8,128)(2,1)} %bitcast.72), calls=%async_computation | async-start | bytes 1048576 | tf_op jit(solution)/shard_map/all_to_all | solution.py:146
  51.9 16.5 %all-to-all-start.1 = ((f32[8,1,4096]{2,1,0:T(1,128)}), f32[8,1,4096]{2,1,0:T(1,128)S(1)}, u32[]{:S(2)}, u32[]{:S(2)}) async-start(f32[8,1,4096]{2,1,0:T(1,128)} %broadcast_in_dim.43), calls=%async_computation.1 | async-start | bytes 262144 | tf_op jit(solution)/shard_map/all_to_all | solution.py:97
  89.5 1.2 %copy-start = (f32[32,8192]{1,0:T(8,128)S(1)}, f32[32,8192]{1,0:T(8,128)}, u32[]{:S(2)}) copy-start(f32[32,8192]{1,0:T(8,128)} %get-tuple-element.7) | copy-start | bytes 3145732

commit v9 on v6

--- a/solution.py
+++ b/solution.py
@@ -103,8 +103,15 @@
     lin_index = (lax.axis_index("zo") * inner_size + lax.axis_index("zi")) * mp_size + lax.axis_index("mp")
     padded_pos = lin_index * rows - (kernel_len - 1) + jnp.arange(rows + kernel_len - 1, dtype=jnp.int32)
     padded_document_ids = document_number_index(doc_lengths, padded_pos)
-    padded = jnp.concatenate([tail_rows, proj], axis=0)
-    conv = short_convolution(padded, conv_weight, padded_document_ids, padded_pos, rows)
+    head_rows = kernel_len - 1
+    body = short_convolution(
+        proj, conv_weight, padded_document_ids[head_rows:], padded_pos[head_rows:], rows - head_rows
+    )
+    head_input = jnp.concatenate([tail_rows, proj[:head_rows]], axis=0)
+    head = short_convolution(
+        head_input, conv_weight, padded_document_ids[: 2 * head_rows], padded_pos[: 2 * head_rows], head_rows
+    )
+    conv = jnp.concatenate([head, body], axis=0)
     query_part = conv[:, 0]
     product = (conv[:, 1] * conv[:, 2]).astype(jnp.bfloat16)
 

time: 85.6 us -> 89.7 us (1.048)
  waiting for transfers between devices: 20.4 us -> 15.6 us
  other arithmetic: 8.71 us -> 12.4 us
  matrix products: 7.09 us -> 10.2 us
  starting transfers between devices: 18.9 us -> 20 us
    ppermute x1, waiting for transfers between devices: 3.77 us -> 0.01 us  [shifted(): return lax.ppermute(block, axis, route)]
    broadcast_in_dim x2, local copies, waits for them, and re-layouts: 0.8 us -> 2.86 us  [long_filter(): sent = jnp.broadcast_to(flat, (count, flat.shape[1]))]
    unnamed x9 -> x21, local copies, waits for them, and re-layouts: 2.24 us -> 0.63 us
    dot_general x1, matrix products: 0.59 us -> 2.07 us  [long_filter(): jnp.einsum('gmb,gmbc->gmc', to_end, block_state, precision=HIGHEST)]
    convert_element_type x1, other arithmetic: 2.11 us -> 0.95 us  [shards(): return (query_part * filtered.astype(jnp.float32)).astype(jnp.bfloat16)]
    all_to_all x1, waiting for transfers between devices: 9.64 us -> 8.51 us  [shards(): lax.all_to_all(product, swap_axis, split_axis=1, concat_axis=0, tiled=True)]
    all_to_all x1, starting transfers between devices: 6.68 us -> 7.74 us  [shards(): lax.all_to_all(product, swap_axis, split_axis=1, concat_axis=0, tiled=True)]
    dot_general x1, matrix products: 0.64 us -> 1.55 us  [long_filter(): state = jnp.einsum('gmab,gmbc->gmac', carry, block_state, precision=HIGHEST)]
  transfers between devices with their start and end apart: 3 -> 3, of which waited for: 3 -> 2; matrix products, arithmetic and copies ran while one was open for 12% -> 19% of each run, Pallas kernels for 0% -> 0%
where the time goes in v9:
time: 89.7 us; the launch traced here: 89 us
  starting transfers between devices  20 us (22%)
  blocking collectives  16.8 us (19%)
  waiting for transfers between devices  15.6 us (17%)
  local copies, waits for them, and re-layouts  13.8 us (15%)
  other arithmetic  12.4 us (14%)
  matrix products  10.2 us (11%)
    all_to_all x1, blocking collectives, shards(): lax.all_to_all(filtered, swap_axis, split_axis=0, concat_axis=1, tiled=True)  16.8 us
    all_to_all x1, waiting for transfers between devices, shards(): lax.all_to_all(product, swap_axis, split_axis=1, concat_axis=0, tiled=True)  8.51 us
    all_to_all x1, starting transfers between devices, long_filter(): lax.all_to_all(sent, outer_axis, split_axis=0, concat_axis=0, tiled=True)  8.18 us
    all_to_all x1, starting transfers between devices, shards(): lax.all_to_all(product, swap_axis, split_axis=1, concat_axis=0, tiled=True)  7.74 us
    all_to_all x1, waiting for transfers between devices, long_filter(): lax.all_to_all(sent, outer_axis, split_axis=0, concat_axis=0, tiled=True)  7.08 us
    add x2, other arithmetic, short_convolution(): result + conv_weight[:, position_shift, :][None] * earlier * keep_mask.as...  4.71 us
    slice x1, local copies, waits for them, and re-layouts, short_convolution(): conv_weight[:, position_shift, :][None] * earlier  4.24 us
    ppermute x1, starting transfers between devices, shifted(): return lax.ppermute(block, axis, route)  4.02 us
  transfers between devices with their start and end apart: 3, of which 2 were waited for; matrix products, arithmetic and copies ran while one was open for 19% of the time, Pallas kernels for 0%

profile of v9, /device:TPU:1, one launch (start us, length us, event | category | flops | bytes accessed | tf_op | source)
XLA Modules:
  0.0 89.0 jit_solution(6416172480708571469)
XLA Ops:
  0.0 1.3 %fusion.50 = (bf16[6,3,8192]{2,0,1:T(8,128)(2,1)S(1)}, bf16[6,3,8192]{2,0,1:T(8,128)(2,1)S(1)}) fusion(bf16[32,3,8192]{2,0,1:T(8,128)(2,1)} %param.5), kind=kLoop, calls=%fused_computation.112 | loop fusion | bytes 1179648 | tf_op jit(solution)/shard_map/slice | solution.py:110
  1.3 4.0 %collective-permute-start = (bf16[6,3,8192]{2,0,1:T(8,128)(2,1)S(1)}, bf16[6,3,8192]{2,0,1:T(8,128)(2,1)S(1)}, u32[]{:S(2)}, u32[]{:S(2)}) collective-permute-start(bf16[6,3,8192]{2,0,1:T(8,128)(2,1)S(1)} %get-tuple-element.8), channel_id=1, source_target_pairs={{0,1},{1,2},{2,3},{3,4},{4,5},{5,6},{6,7},{7,8},{8,9},{9,10},{10,1... | collective-permute-start | bytes 884744 | tf_op jit(solution)/shard_map/ppermute | solution.py:12
  5.4 0.7 copy.47
  6.1 0.1 reduce-window.9
  6.2 0.1 reduce.3
  6.3 0.7 sub.82
  7.0 0.1 compare_convert_fusion
  7.1 0.2 convert_reduce_fusion
  7.3 0.1 and_convert_fusion.5
  7.4 0.1 and_convert_fusion.11
  7.4 0.1 compare_convert_fusion.1
  7.5 0.6 subtract_compare_fusion
  8.2 0.6 subtract_multiply_fusion
  8.8 4.2 %fusion.51 = (f32[3,1,8192]{2,1,0:T(1,128)S(1)}, f32[3,1,8192]{2,1,0:T(1,128)S(1)}, f32[3,1,8192]{2,1,0:T(1,128)S(1)}, f32[3,1,8192]{2,1,0:T(1,128)S(1)}, f32[3,...) fusion(f32[3,7,8192]{2,1,0:T(8,128)} %param.6), kind=kLoop, calls=%fused_computation.113 | loop fusion | bytes 1376256 | tf_op jit(solution)/shard_map/slice | solution.py:33
  13.0 0.1 copy.88
  13.1 0.7 sqrt_multiply_fusion
  13.8 0.7 convert_multiply_fusion
  14.5 0.1 copy_bitcast_fusion
  14.6 0.1 copy_bitcast_fusion.2
  14.8 0.1 copy_bitcast_fusion.4
  14.9 0.0 copy-done
  14.9 3.4 %multiply_add_fusion = f32[26,3,8192]{2,0,1:T(8,128)S(1)} fusion(f32[26]{0:T(128)S(1)} %get-tuple-element.25, bf16[32,3,8192]{2,0,1:T(8,128)(2,1)S(1)} %copy-done, f32[3,8192]{1,0:T(4,128)S(1)} %get-tuple-element.30, f32[26]{0:T(128)S(1)} %get-tuple-element.26, f32[3,8192]{1,0:T(4,128)S(1)} %get-tuple-element.31, f32[26]{0:T(128)S(1)} %get-tuple-element.27, ...), kind=kLoop, calls=%fused_computation.2 | loop fusion | flops 17252352 | bytes 12190424 | tf_op jit(solution)/shard_map/add | solution.py:32
  18.4 0.0 copy-start.1
  18.4 0.1 exponential_select_fusion
  18.5 0.0 collective-permute-done
  18.5 1.3 %multiply_add_fusion.1 = f32[6,3,8192]{2,0,1:T(8,128)S(1)} fusion(bf16[6,3,8192]{2,0,1:T(8,128)(2,1)S(1)} %collective-permute-done, bf16[6,3,8192]{2,0,1:T(8,128)(2,1)S(1)} %get-tuple-element.7, f32[6]{0:T(128)S(1)} %get-tuple-element.19, f32[3,8192]{1,0:T(4,128)S(1)} %get-tuple-element.30, f32[6]{0:T(128)S(1)} %get-tuple-element.20, ...), kind=kLoop, calls=%fused_computation.30 | loop fusion | flops 6193152 | bytes 1867944 | tf_op jit(solution)/shard_map/add | solution.py:32
  19.8 0.0 copy-start.6
  19.8 0.0 copy-start.7
  19.8 0.0 copy-start.3
  19.8 0.2 fusion.4
  20.1 0.0 copy-done.1
  20.1 0.1 copy.74
  20.2 1.1 %copy.48 = bf16[32,32,256]{2,0,1:T(8,128)(2,1)} copy(bf16[32,32,256]{2,1,0:T(8,128)(2,1)S(1)} %bitcast.82) | data formatting | bytes 1048576 | tf_op jit(solution)/shard_map/convert_element_type | solution.py:116
  21.3 7.7 %all-to-all-start = ((bf16[32,32,256]{2,0,1:T(8,128)(2,1)}), bf16[32,32,256]{2,0,1:T(8,128)(2,1)S(1)}, u32[]{:S(2)}, u32[]{:S(2)}) async-start(bf16[32,32,256]{2,0,1:T(8,128)(2,1)} %copy.48), calls=%async_computation | async-start | bytes 1048576 | tf_op jit(solution)/shard_map/all_to_all | solution.py:119
  29.0 0.5 iota_compare_fusion
  29.6 0.1 mul.513
  29.7 0.2 mul.514
  29.9 0.0 copy-done.6
  29.9 0.0 copy-done.7
  29.9 0.7 multiply_exponential_fusion.2
  30.6 1.2 %convolution_select_fusion = f32[4,256,256]{2,1,0:T(8,128)S(1)} fusion(pred[256,256]{1,0:T(8,128)(4,1)S(1)} %copy-done.3, f32[4,16]{1,0:T(4,128)S(1)} %get-tuple-element.6, f32[4,16]{1,0:T(4,128)S(1)} %neg.12, f32[4,16]{1,0:T(4,128)S(1)} %get-tuple-element.5), kind=kOutput, calls=%fused_computation.7 | convolution fusion | flops 50642944 | bytes 1114880 | tf_op jit(solution)/shard_map/grm,gms->grs/dot_general | solution.py:56
  31.8 8.5 %all-to-all-done = bf16[32,32,256]{2,0,1:T(8,128)(2,1)S(1)} async-done(((bf16[32,32,256]{2,0,1:T(8,128)(2,1)}), bf16[32,32,256]{2,0,1:T(8,128)(2,1)S(1)}, u32[]{:S(2)}, u32[]{:S(2)}) %all-to-all-start) | async-done | bytes 524320 | tf_op jit(solution)/shard_map/all_to_all | solution.py:119
  40.3 0.4 reshape_reshape.3
  40.8 0.6 copy.50
  41.4 0.3 fusion.11
  41.8 0.3 fusion.38
  42.1 1.0 %convolution_add_fusion.2 = f32[4,16,4,64]{3,1,2,0:T(8,128)} fusion(f32[4,16,4,64]{3,1,2,0:T(8,128)S(1)} %fusion.38, bf16[4,256,4,64]{1,3,0,2:T(8,128)(2,1)S(1)} %copy.50, f32[256]{0:T(256)S(1)} %iota_subtract_fusion, f32[4,16]{1,0:T(4,128)S(1)} %neg.12), kind=kOutput, calls=%fused_computation.10 | convolution fusion | flops 8486912 | bytes 656640 | tf_op jit(solution)/shard_map/gms,bsgc->gmbc/dot_general | solution.py:44
  43.1 2.1 %fusion.23 = f32[4,16,1,64]{3,2,1,0:T(1,128)} fusion(f32[4,16,4,1]{2,3,1,0:T(1,128)S(1)} %bitcast.87, f32[4,16,4,64]{3,1,2,0:T(8,128)} %convolution_add_fusion.2), kind=kOutput, calls=%fused_computation.54 | convolution fusion | flops 196608 | bytes 82944 | tf_op jit(solution)/shard_map/gmb,gmbc->gmc/dot_general | solution.py:67
  45.2 1.4 %broadcast_in_dim.38 = f32[4096]{0:T(1024)} reshape(f32[4,16,64]{2,1,0:T(8,128)} %bitcast.86) | data formatting | bytes 32768 | tf_op jit(solution)/shard_map/broadcast_in_dim | solution.py:70
  46.6 1.4 %broadcast_in_dim.39 = f32[8,1,4096]{2,1,0:T(1,128)} broadcast(f32[4096]{0:T(1024)} %broadcast_in_dim.38), dimensions={2} | broadcast | bytes 147456 | tf_op jit(solution)/shard_map/broadcast_in_dim | solution.py:70
  48.0 8.2 %all-to-all-start.1 = ((f32[8,1,4096]{2,1,0:T(1,128)}), f32[8,1,4096]{2,1,0:T(1,128)}, u32[]{:S(2)}, u32[]{:S(2)}) async-start(f32[8,1,4096]{2,1,0:T(1,128)} %broadcast_in_dim.39), calls=%async_computation.1 | async-start | bytes 262144 | tf_op jit(solution)/shard_map/all_to_all | solution.py:71
  56.2 1.3 %convolution_add_fusion.1 = f32[4,4,64,256]{3,2,1,0:T(8,128)} fusion(f32[4,4,64,256]{3,2,1,0:T(8,128)S(1)} %fusion.11, bf16[4,256,4,64]{1,3,0,2:T(8,128)(2,1)S(1)} %copy.50, f32[4,256,256]{2,1,0:T(8,128)S(1)} %convolution_select_fusion), kind=kOutput, calls=%fused_computation.6 | convolution fusion | flops 135528448 | bytes 3670016 | tf_op jit(solution)/shard_map/grs,bsgc->brgc/dot_general | solution.py:44
  57.6 7.1 %all-to-all-done.1 = f32[8,1,4096]{2,1,0:T(1,128)} async-done(((f32[8,1,4096]{2,1,0:T(1,128)}), f32[8,1,4096]{2,1,0:T(1,128)}, u32[]{:S(2)}, u32[]{:S(2)}) %all-to-all-start.1) | async-done | bytes 131104 | tf_op jit(solution)/shard_map/all_to_all | solution.py:71
  64.6 1.1 %multiply_reduce_fusion = f32[4096]{0:T(1024)S(1)} fusion(f32[8,1,4096]{2,1,0:T(1,128)S(1)} %mul.514, f32[8,1,4096]{2,1,0:T(1,128)} %all-to-all-done.1), kind=kLoop, calls=%fused_computation.50 | loop fusion | flops 61440 | bytes 278528 | tf_op jit(solution)/shard_map/reduce_sum | solution.py:81
  65.7 0.1 reduce_sum.22
  65.8 1.5 %convolution_add_fusion.3 = f32[4,16,4,64]{3,2,1,0:T(4,128)S(1)} fusion(f32[4,16,4,64]{3,1,2,0:T(8,128)} %convolution_add_fusion.2, f32[4,16,64]{2,1,0:T(8,128)S(1)} %reduce_sum.22, f32[4,16,4]{2,1,0:T(8,128)} %get-tuple-element.16, f32[4,4]{1,0:T(4,128)S(1)} %copy-done.5, f32[4,16]{1,0:T(4,128)S(1)} %neg.12, pred[4,4]{1,0:T(4,128)(4,1)} %iota_compare_fusion), kind=kOutput, calls=%fused_computation.11 | convolution fusion | flops 821248 | bytes 148816 | tf_op jit(solution)/shard_map/gmab,gmbc->gmac/dot_general | solution.py:88
  67.3 2.3 %fusion.1 = bf16[4,256,4,64]{1,3,0,2:T(8,128)(2,1)S(1)} fusion(f32[4,4,64,256]{3,2,1,0:T(8,128)} %convolution_add_fusion.1, f32[4,16,4,64]{3,2,1,0:T(4,128)S(1)} %convolution_add_fusion.3, f32[4,16]{1,0:T(4,128)S(1)} %neg.12, f32[4,16]{1,0:T(4,128)S(1)} %get-tuple-element.5), kind=kOutput, calls=%fused_computation.9 | convolution fusion | flops 50888704 | bytes 1638912 | tf_op jit(solution)/shard_map/grm,gmbc->brgc/dot_general | solution.py:91
  69.7 0.7 copy.56
  70.3 0.7 convert_element_type.189
  71.1 16.8 %all_to_all.32 = bf16[32,32,256]{2,1,0:T(8,128)(2,1)S(1)} all-to-all(bf16[32,32,256]{2,1,0:T(8,128)(2,1)S(1)} %bitcast.83), channel_id=1, replica_groups=mesh['zo'=8,'zi'=4,'mp'=8] {'mp','zi'}, dimensions={0} | all-to-all | bytes 1048576 | tf_op jit(solution)/shard_map/all_to_all | solution.py:131
  87.9 0.1 convert_bitcast_fusion
  88.0 0.1 copy.73
  88.1 0.0 copy-done.2
  88.1 0.9 %fusion.8 = bf16[32,8192]{1,0:T(8,128)(2,1)} fusion(f32[32,8192]{1,0:T(8,128)S(1)} %bitcast.78, f32[26,3,8192]{2,0,1:T(8,128)S(1)} %copy-done.2, f32[6,3,8192]{2,0,1:T(8,128)S(1)} %multiply_add_fusion.1), kind=kLoop, calls=%fused_computation.26 | loop fusion | flops 786432 | bytes 4718592 | tf_op jit(solution)/shard_map/convert_element_type | solution.py:132
  (16 shorter events, 0.1 us)
Async XLA Ops:
  0.0 14.9 %copy-start = (bf16[32,3,8192]{2,0,1:T(8,128)(2,1)S(1)}, bf16[32,3,8192]{2,0,1:T(8,128)(2,1)}, u32[]{:S(2)}) copy-start(bf16[32,3,8192]{2,0,1:T(8,128)(2,1)} %param.5) | copy-start | bytes 4718596
  1.3 17.1 %collective-permute-start = (bf16[6,3,8192]{2,0,1:T(8,128)(2,1)S(1)}, bf16[6,3,8192]{2,0,1:T(8,128)(2,1)S(1)}, u32[]{:S(2)}, u32[]{:S(2)}) collective-permute-start(bf16[6,3,8192]{2,0,1:T(8,128)(2,1)S(1)} %get-tuple-element.8), channel_id=1, source_target_pairs={{0,1},{1,2},{2,3},{3,4},{4,5},{5,6},{6,7},{7,8},{8,9},{9,10},{10,1... | collective-permute-start | bytes 884744 | tf_op jit(solution)/shard_map/ppermute | solution.py:12
  18.4 1.7 %copy-start.1 = (f32[26,3,8192]{2,0,1:T(8,128)}, f32[26,3,8192]{2,0,1:T(8,128)S(1)}, u32[]{:S(2)}) copy-start(f32[26,3,8192]{2,0,1:T(8,128)S(1)} %multiply_add_fusion) | copy-start | bytes 7667716
  19.8 10.1 %copy-start.6 = (f32[4]{0:T(128)S(1)}, f32[4]{0:T(128)}, u32[]{:S(2)}) copy-start(f32[4]{0:T(128)} %get-tuple-element.36) | copy-start | bytes 52
  19.8 10.1 %copy-start.7 = (f32[4]{0:T(128)S(1)}, f32[4]{0:T(128)}, u32[]{:S(2)}) copy-start(f32[4]{0:T(128)} %get-tuple-element.37) | copy-start | bytes 52
  19.8 10.8 %copy-start.3 = (pred[256,256]{1,0:T(8,128)(4,1)S(1)}, pred[256,256]{1,0:T(8,128)(4,1)}, u32[]{:S(2)}) copy-start(pred[256,256]{1,0:T(8,128)(4,1)} %subtract_compare_fusion) | copy-start | bytes 196612
  21.3 19.0 %all-to-all-start = ((bf16[32,32,256]{2,0,1:T(8,128)(2,1)}), bf16[32,32,256]{2,0,1:T(8,128)(2,1)S(1)}, u32[]{:S(2)}, u32[]{:S(2)}) async-start(bf16[32,32,256]{2,0,1:T(8,128)(2,1)} %copy.48), calls=%async_computation | async-start | bytes 1048576 | tf_op jit(solution)/shard_map/all_to_all | solution.py:119
  41.4 1.7 %copy-start.4 = (f32[4,16,4]{2,1,0:T(8,128)S(1)}, f32[4,16,4]{2,1,0:T(8,128)}, u32[]{:S(2)}) copy-start(f32[4,16,4]{2,1,0:T(8,128)} %get-tuple-element.17) | copy-start | bytes 3076
  41.7 24.0 %copy-start.5 = (f32[4,4]{1,0:T(4,128)S(1)}, f32[4,4]{1,0:T(4,128)}, u32[]{:S(2)}) copy-start(f32[4,4]{1,0:T(4,128)} %convert_multiply_fusion) | copy-start | bytes 196
  48.0 16.6 %all-to-all-start.1 = ((f32[8,1,4096]{2,1,0:T(1,128)}), f32[8,1,4096]{2,1,0:T(1,128)}, u32[]{:S(2)}, u32[]{:S(2)}) async-start(f32[8,1,4096]{2,1,0:T(1,128)} %broadcast_in_dim.39), calls=%async_computation.1 | async-start | bytes 262144 | tf_op jit(solution)/shard_map/all_to_all | solution.py:71
  71.0 17.1 %copy-start.2 = (f32[26,3,8192]{2,0,1:T(8,128)S(1)}, f32[26,3,8192]{2,0,1:T(8,128)}, u32[]{:S(2)}) copy-start(f32[26,3,8192]{2,0,1:T(8,128)} %copy-done.1) | copy-start | bytes 7667716

commit v10 on v6

--- a/solution.py
+++ b/solution.py
@@ -66,10 +66,7 @@
     to_end = jnp.exp(-decays[:, :, None] * (float(block_len) * (block_count - 1 - blocks))[None, None, :])
     run_state = jnp.einsum("gmb,gmbc->gmc", to_end, block_state, precision=HIGHEST)
     count = lax.axis_size(outer_axis)
-    flat = run_state.reshape(1, -1)
-    sent = jnp.broadcast_to(flat, (count, flat.shape[1]))
-    gathered = lax.all_to_all(sent, outer_axis, split_axis=0, concat_axis=0, tiled=True)
-    gathered = gathered.reshape((count,) + run_state.shape)
+    gathered = lax.all_gather(run_state, outer_axis, axis=0)
     here = lax.axis_index(outer_axis)
     earlier = jnp.arange(count, dtype=jnp.int32)
     gap = (here - 1 - earlier).astype(jnp.float32) * float(positions)

time: 85.6 us -> 94.5 us (1.10)
  blocking collectives: 16.6 us -> 43.8 us
  starting transfers between devices: 18.9 us -> 10.7 us
  waiting for transfers between devices: 20.4 us -> 13.7 us
  matrix products: 7.09 us -> 4.88 us
  local copies, waits for them, and re-layouts: 13.2 us -> 12 us
    all_gather x0 -> x1, blocking collectives: none -> 22.3 us  [long_filter(): gathered = lax.all_gather(run_state, outer_axis, axis=0)]
    all_to_all x1 -> x0, starting transfers between devices: 8.18 us -> none  [long_filter(): lax.all_to_all(sent, outer_axis, split_axis=0, concat_axis=0, tiled=True)]
    all_to_all x1 -> x0, waiting for transfers between devices: 6.99 us -> none  [long_filter(): lax.all_to_all(sent, outer_axis, split_axis=0, concat_axis=0, tiled=True)]
    all_to_all x1, blocking collectives: 16.6 us -> 21.5 us  [shards(): lax.all_to_all(filtered, swap_axis, split_axis=0, concat_axis=1, tiled=True)]
    dot_general x1, matrix products: 2.35 us -> 1.12 us  [long_filter(): inter = jnp.einsum('grm,gmbc->brgc', left, state, precision=HIGHEST)]
    dot_general x2, matrix products: 1.68 us -> 0.7 us  [split_product(): jnp.einsum(form, lower_part, inputs, preferred_element_type=jnp.float32)]
  transfers between devices with their start and end apart: 3 -> 2, of which waited for: 3 -> 2; matrix products, arithmetic and copies ran while one was open for 12% -> 9% of each run, Pallas kernels for 0% -> 0%
where the time goes in v10:
time: 94.5 us; the launch traced here: 94.1 us
  blocking collectives  43.8 us (46%)
  waiting for transfers between devices  13.7 us (14%)
  local copies, waits for them, and re-layouts  12 us (13%)
  starting transfers between devices  10.7 us (11%)
  other arithmetic  8.69 us (9%)
  matrix products  4.88 us (5%)
    all_gather x1, blocking collectives, long_filter(): gathered = lax.all_gather(run_state, outer_axis, axis=0)  22.3 us
    all_to_all x1, blocking collectives, shards(): lax.all_to_all(filtered, swap_axis, split_axis=0, concat_axis=1, tiled=True)  21.5 us
    all_to_all x1, waiting for transfers between devices, shards(): lax.all_to_all(product, swap_axis, split_axis=1, concat_axis=0, tiled=True)  9.96 us
    all_to_all x1, starting transfers between devices, shards(): lax.all_to_all(product, swap_axis, split_axis=1, concat_axis=0, tiled=True)  6.68 us
    slice x1, local copies, waits for them, and re-layouts, short_convolution(): conv_weight[:, position_shift, :][None] * earlier  4.22 us
    ppermute x1, starting transfers between devices, shifted(): return lax.ppermute(block, axis, route)  4.02 us
    add x1, other arithmetic, short_convolution(): result + conv_weight[:, position_shift, :][None] * earlier * keep_mask.as...  3.98 us
    ppermute x1, waiting for transfers between devices, shifted(): return lax.ppermute(block, axis, route)  3.77 us
  transfers between devices with their start and end apart: 2, of which 2 were waited for; matrix products, arithmetic and copies ran while one was open for 9% of the time, Pallas kernels for 0%

profile of v10, /device:TPU:1, one launch (start us, length us, event | category | flops | bytes accessed | tf_op | source)
XLA Modules:
  0.0 94.1 jit_solution(3760912497373616264)
XLA Ops:
  0.0 0.0 copy-start.1
  0.0 1.2 %slice.97 = bf16[6,3,8192]{2,0,1:T(8,128)(2,1)S(1)} slice(bf16[32,3,8192]{2,0,1:T(8,128)(2,1)} %param.5), slice={[26:32], [0:3], [0:8192]} | slice | bytes 589824 | tf_op jit(solution)/shard_map/slice | solution.py:99
  1.2 4.0 %collective-permute-start = (bf16[6,3,8192]{2,0,1:T(8,128)(2,1)S(1)}, bf16[6,3,8192]{2,0,1:T(8,128)(2,1)S(1)}, u32[]{:S(2)}, u32[]{:S(2)}) collective-permute-start(bf16[6,3,8192]{2,0,1:T(8,128)(2,1)S(1)} %slice.97), channel_id=1, source_target_pairs={{0,1},{1,2},{2,3},{3,4},{4,5},{5,6},{6,7},{7,8},{8,9},{9,10},{10,1... | collective-permute-start | bytes 884744 | tf_op jit(solution)/shard_map/ppermute | solution.py:12
  5.4 0.7 copy.47
  6.1 0.1 reduce-window.9
  6.2 0.1 reduce
  6.3 0.7 sub.82
  7.0 0.1 compare_convert_fusion
  7.1 0.2 convert_reduce_fusion
  7.2 0.1 and_convert_fusion.5
  7.3 4.2 %fusion.47 = (f32[3,1,8192]{2,1,0:T(1,128)S(1)}, f32[3,1,8192]{2,1,0:T(1,128)S(1)}, f32[3,1,8192]{2,1,0:T(1,128)S(1)}, f32[3,1,8192]{2,1,0:T(1,128)S(1)}, f32[3,...) fusion(f32[3,7,8192]{2,1,0:T(8,128)} %param.6), kind=kLoop, calls=%fused_computation.100 | loop fusion | bytes 1376256 | tf_op jit(solution)/shard_map/slice | solution.py:33
  11.6 0.1 copy.88
  11.6 0.7 sqrt_multiply_fusion
  12.4 0.1 convert_multiply_fusion
  12.4 0.1 copy_bitcast_fusion
  12.6 0.1 copy_bitcast_fusion.2
  12.7 0.1 copy_bitcast_fusion.4
  12.9 0.1 exponential_select_fusion
  13.0 3.8 %collective-permute-done = bf16[6,3,8192]{2,0,1:T(8,128)(2,1)S(1)} collective-permute-done((bf16[6,3,8192]{2,0,1:T(8,128)(2,1)S(1)}, bf16[6,3,8192]{2,0,1:T(8,128)(2,1)S(1)}, u32[]{:S(2)}, u32[]{:S(2)}) %collective-permute-start) | collective-permute-done | bytes 294944 | tf_op jit(solution)/shard_map/ppermute | solution.py:12
  16.8 0.0 copy-done.1
  16.8 4.0 %multiply_add_fusion = f32[32,3,8192]{2,0,1:T(8,128)S(1)} fusion(bf16[32,3,8192]{2,0,1:T(8,128)(2,1)S(1)} %copy-done.1, bf16[6,3,8192]{2,0,1:T(8,128)(2,1)S(1)} %collective-permute-done, f32[32]{0:T(128)S(1)} %get-tuple-element.17, f32[3,8192]{1,0:T(4,128)S(1)} %get-tuple-element.22, f32[32]{0:T(128)S(1)} %get-tuple-element.18, ...), kind=kLoop, calls=%fused_computation.5 | loop fusion | flops 35389440 | bytes 5702528 | tf_op jit(solution)/shard_map/add | solution.py:32
  20.7 0.0 copy-start
  20.8 1.6 %copy-done = f32[32,3,8192]{2,0,1:T(8,128)} copy-done((f32[32,3,8192]{2,0,1:T(8,128)}, f32[32,3,8192]{2,0,1:T(8,128)S(1)}, u32[]{:S(2)}) %copy-start) | copy-done | bytes 3145752
  22.4 0.1 fusion.7
  22.5 0.1 copy.74
  22.6 1.1 %copy.48 = bf16[32,32,256]{2,0,1:T(8,128)(2,1)} copy(bf16[32,32,256]{2,1,0:T(8,128)(2,1)S(1)} %bitcast.81) | data formatting | bytes 1048576 | tf_op jit(solution)/shard_map/convert_element_type | solution.py:106
  23.7 6.7 %all-to-all-start = ((bf16[32,32,256]{2,0,1:T(8,128)(2,1)}), bf16[32,32,256]{2,0,1:T(8,128)(2,1)S(1)}, u32[]{:S(2)}, u32[]{:S(2)}) async-start(bf16[32,32,256]{2,0,1:T(8,128)(2,1)} %copy.48), calls=%async_computation | async-start | bytes 1048576 | tf_op jit(solution)/shard_map/all_to_all | solution.py:109
  30.4 0.1 multiply_exponential_fusion.2
  30.5 1.2 %convolution_select_fusion = f32[4,256,256]{2,1,0:T(8,128)S(1)} fusion(pred[256,256]{1,0:T(8,128)(4,1)S(1)} %subtract_compare_fusion, f32[4,16]{1,0:T(4,128)S(1)} %get-tuple-element.6, f32[4,16]{1,0:T(4,128)S(1)} %neg.12, f32[4,16]{1,0:T(4,128)S(1)} %get-tuple-element.5), kind=kOutput, calls=%fused_computation.19 | convolution fusion | flops 50642944 | bytes 1114880 | tf_op jit(solution)/shard_map/grm,gms->grs/dot_general | solution.py:56
  31.7 10.0 %all-to-all-done = bf16[32,32,256]{2,0,1:T(8,128)(2,1)S(1)} async-done(((bf16[32,32,256]{2,0,1:T(8,128)(2,1)}), bf16[32,32,256]{2,0,1:T(8,128)(2,1)S(1)}, u32[]{:S(2)}, u32[]{:S(2)}) %all-to-all-start) | async-done | bytes 524320 | tf_op jit(solution)/shard_map/all_to_all | solution.py:109
  41.7 0.4 reshape_reshape.3
  42.1 0.6 copy.50
  42.8 0.3 fusion.12
  43.1 0.3 convolution_add_fusion.1
  43.4 0.3 fusion.35
  43.8 0.4 convolution_add_fusion.2
  44.1 0.6 fusion.20
  44.7 22.3 %all-gather = f32[32,16,64]{2,1,0:T(8,128)S(1)} all-gather(f32[4,16,64]{2,1,0:T(8,128)S(1)} %bitcast.85), channel_id=2, replica_groups=mesh['zo'=8,'zi'=4,'mp'=8] {'zo'}, dimensions={0}, use_global_device_ids=true | all-gather | bytes 147456 | tf_op jit(solution)/shard_map/all_gather | solution.py:69
  67.0 0.1 multiply_reduce_fusion
  67.1 0.6 convolution_add_fusion.3
  67.8 1.1 %fusion.6 = bf16[4,256,4,64]{1,3,0,2:T(8,128)(2,1)S(1)} fusion(f32[4,4,64,256]{3,2,1,0:T(8,128)S(1)} %convolution_add_fusion.1, f32[4,16,4,64]{3,2,1,0:T(4,128)S(1)} %convolution_add_fusion.3, f32[4,16]{1,0:T(4,128)S(1)} %neg.12, f32[4,16]{1,0:T(4,128)S(1)} %get-tuple-element.5), kind=kOutput, calls=%fused_computation.21 | convolution fusion | flops 50888704 | bytes 1638912 | tf_op jit(solution)/shard_map/grm,gmbc->brgc/dot_general | solution.py:88
  68.9 0.7 copy.56
  69.5 0.7 convert_element_type.133
  70.3 21.5 %all_to_all.26 = bf16[32,32,256]{2,1,0:T(8,128)(2,1)S(1)} all-to-all(bf16[32,32,256]{2,1,0:T(8,128)(2,1)S(1)} %bitcast.82), channel_id=1, replica_groups=mesh['zo'=8,'zi'=4,'mp'=8] {'mp','zi'}, dimensions={0} | all-to-all | bytes 1048576 | tf_op jit(solution)/shard_map/all_to_all | solution.py:121
  91.8 0.1 convert_bitcast_fusion
  91.9 0.1 copy.73
  92.0 2.1 %fusion.9 = bf16[32,8192]{1,0:T(8,128)(2,1)} fusion(f32[32,8192]{1,0:T(8,128)S(1)} %bitcast.77, f32[32,3,8192]{2,0,1:T(8,128)} %copy-done), kind=kLoop, calls=%fused_computation.28 | loop fusion | flops 524288 | bytes 2621440 | tf_op jit(solution)/shard_map/convert_element_type | solution.py:122
  (12 shorter events, 0.2 us)
Async XLA Ops:
  0.0 16.8 %copy-start.1 = (bf16[32,3,8192]{2,0,1:T(8,128)(2,1)S(1)}, bf16[32,3,8192]{2,0,1:T(8,128)(2,1)}, u32[]{:S(2)}) copy-start(bf16[32,3,8192]{2,0,1:T(8,128)(2,1)} %param.5) | copy-start | bytes 4718596
  1.2 15.5 %collective-permute-start = (bf16[6,3,8192]{2,0,1:T(8,128)(2,1)S(1)}, bf16[6,3,8192]{2,0,1:T(8,128)(2,1)S(1)}, u32[]{:S(2)}, u32[]{:S(2)}) collective-permute-start(bf16[6,3,8192]{2,0,1:T(8,128)(2,1)S(1)} %slice.97), channel_id=1, source_target_pairs={{0,1},{1,2},{2,3},{3,4},{4,5},{5,6},{6,7},{7,8},{8,9},{9,10},{10,1... | collective-permute-start | bytes 884744 | tf_op jit(solution)/shard_map/ppermute | solution.py:12
  20.7 1.7 %copy-start = (f32[32,3,8192]{2,0,1:T(8,128)}, f32[32,3,8192]{2,0,1:T(8,128)S(1)}, u32[]{:S(2)}) copy-start(f32[32,3,8192]{2,0,1:T(8,128)S(1)} %multiply_add_fusion) | copy-start | bytes 9437188
  23.7 17.9 %all-to-all-start = ((bf16[32,32,256]{2,0,1:T(8,128)(2,1)}), bf16[32,32,256]{2,0,1:T(8,128)(2,1)S(1)}, u32[]{:S(2)}, u32[]{:S(2)}) async-start(bf16[32,32,256]{2,0,1:T(8,128)(2,1)} %copy.48), calls=%async_computation | async-start | bytes 1048576 | tf_op jit(solution)/shard_map/all_to_all | solution.py:109

commit v11 on v6

--- a/solution.py
+++ b/solution.py
@@ -104,9 +104,8 @@
     padded_pos = lin_index * rows - (kernel_len - 1) + jnp.arange(rows + kernel_len - 1, dtype=jnp.int32)
     padded_document_ids = document_number_index(doc_lengths, padded_pos)
     padded = jnp.concatenate([tail_rows, proj], axis=0)
-    conv = short_convolution(padded, conv_weight, padded_document_ids, padded_pos, rows)
-    query_part = conv[:, 0]
-    product = (conv[:, 1] * conv[:, 2]).astype(jnp.bfloat16)
+    pair = short_convolution(padded[:, 1:], conv_weight[1:], padded_document_ids, padded_pos, rows)
+    product = (pair[:, 0] * pair[:, 1]).astype(jnp.bfloat16)
 
     swap_axis = ("mp", "zi")
     gathered = lax.all_to_all(product, swap_axis, split_axis=1, concat_axis=0, tiled=True)
@@ -122,6 +121,7 @@
     filtered = filtered.reshape(inner_size, mp_size, rows, width).transpose(1, 0, 2, 3)
     filtered = filtered.reshape(inner_size * mp_size * rows, width)
     filtered = lax.all_to_all(filtered, swap_axis, split_axis=0, concat_axis=1, tiled=True)
+    query_part = short_convolution(padded[:, :1], conv_weight[:1], padded_document_ids, padded_pos, rows)[:, 0]
     return (query_part * filtered.astype(jnp.float32)).astype(jnp.bfloat16)
 
 

time: 85.6 us -> 94.3 us (1.10)
  blocking collectives: 16.6 us -> 0 us
  local copies, waits for them, and re-layouts: 13.2 us -> 21.1 us
  starting transfers between devices: 18.9 us -> 24.5 us
  matrix products: 7.09 us -> 11.7 us
  waiting for transfers between devices: 20.4 us -> 24.5 us
  other arithmetic: 8.71 us -> 11.3 us
    all_to_all x1 -> x0, blocking collectives: 16.6 us -> none  [shards(): lax.all_to_all(filtered, swap_axis, split_axis=0, concat_axis=1, tiled=True)]
    all_to_all x0 -> x1, waiting for transfers between devices: none -> 8.77 us  [shards(): lax.all_to_all(filtered, swap_axis, split_axis=0, concat_axis=1, tiled=True)]
    all_to_all x0 -> x1, starting transfers between devices: none -> 5.48 us  [shards(): lax.all_to_all(filtered, swap_axis, split_axis=0, concat_axis=1, tiled=True)]
    all_to_all x1, waiting for transfers between devices: 9.64 us -> 7 us  [shards(): lax.all_to_all(product, swap_axis, split_axis=1, concat_axis=0, tiled=True)]
    broadcast_in_dim x2, local copies, waits for them, and re-layouts: 0.8 us -> 2.86 us  [long_filter(): sent = jnp.broadcast_to(flat, (count, flat.shape[1]))]
    another operation x2, local copies, waits for them, and re-layouts: 1.04 us -> 2.99 us  [long_filter(): inputs = product.reshape(block_count, block_len, group_count, group_width)]
    slice x1 -> x2, local copies, waits for them, and re-layouts: 4.22 us -> 5.82 us  [short_convolution(): conv_weight[:, position_shift, :][None] * earlier]
    add x1, other arithmetic: 3.98 us -> 2.64 us  [short_convolution(): result + conv_weight[:, position_shift, :][None] * earlier * keep_mask.as...]
  transfers between devices with their start and end apart: 3 -> 4, of which waited for: 3 -> 4; matrix products, arithmetic and copies ran while one was open for 12% -> 19% of each run, Pallas kernels for 0% -> 0%
where the time goes in v11:
time: 94.3 us; the launch traced here: 93.5 us
  starting transfers between devices  24.5 us (26%)
  waiting for transfers between devices  24.5 us (26%)
  local copies, waits for them, and re-layouts  21.1 us (22%)
  matrix products  11.7 us (12%)
  other arithmetic  11.3 us (12%)
    all_to_all x1, waiting for transfers between devices, shards(): lax.all_to_all(filtered, swap_axis, split_axis=0, concat_axis=1, tiled=True)  8.77 us
    all_to_all x1, starting transfers between devices, long_filter(): lax.all_to_all(sent, outer_axis, split_axis=0, concat_axis=0, tiled=True)  8.32 us
    all_to_all x1, waiting for transfers between devices, shards(): lax.all_to_all(product, swap_axis, split_axis=1, concat_axis=0, tiled=True)  7 us
    all_to_all x1, starting transfers between devices, shards(): lax.all_to_all(product, swap_axis, split_axis=1, concat_axis=0, tiled=True)  6.69 us
    all_to_all x1, waiting for transfers between devices, long_filter(): lax.all_to_all(sent, outer_axis, split_axis=0, concat_axis=0, tiled=True)  5.86 us
    slice x2, local copies, waits for them, and re-layouts, short_convolution(): conv_weight[:, position_shift, :][None] * earlier  5.82 us
    all_to_all x1, starting transfers between devices, shards(): lax.all_to_all(filtered, swap_axis, split_axis=0, concat_axis=1, tiled=True)  5.48 us
    ppermute x1, starting transfers between devices, shifted(): return lax.ppermute(block, axis, route)  4.02 us
  transfers between devices with their start and end apart: 4, of which 4 were waited for; matrix products, arithmetic and copies ran while one was open for 19% of the time, Pallas kernels for 0%

profile of v11, /device:TPU:1, one launch (start us, length us, event | category | flops | bytes accessed | tf_op | source)
XLA Modules:
  0.0 93.5 jit_solution(17647679129823817935)
XLA Ops:
  0.0 1.2 %slice.189 = bf16[6,3,8192]{2,0,1:T(8,128)(2,1)S(1)} slice(bf16[32,3,8192]{2,0,1:T(8,128)(2,1)} %param.5), slice={[26:32], [0:3], [0:8192]} | slice | bytes 589824 | tf_op jit(solution)/shard_map/slice | solution.py:102
  1.2 4.0 %collective-permute-start = (bf16[6,3,8192]{2,0,1:T(8,128)(2,1)S(1)}, bf16[6,3,8192]{2,0,1:T(8,128)(2,1)S(1)}, u32[]{:S(2)}, u32[]{:S(2)}) collective-permute-start(bf16[6,3,8192]{2,0,1:T(8,128)(2,1)S(1)} %slice.189), channel_id=1, source_target_pairs={{0,1},{1,2},{2,3},{3,4},{4,5},{5,6},{6,7},{7,8},{8,9},{9,10},{10,1... | collective-permute-start | bytes 884744 | tf_op jit(solution)/shard_map/ppermute | solution.py:12
  5.2 0.7 subtract_compare_fusion
  5.9 0.6 iota_subtract_fusion
  6.5 0.7 copy.47
  7.3 0.1 reduce-window.9
  7.4 0.1 reduce.3
  7.5 0.7 sub.82
  8.1 0.1 compare_convert_fusion
  8.2 0.2 convert_reduce_fusion
  8.4 0.1 and_convert_fusion.5
  8.5 0.0 copy-start.4
  8.5 0.0 copy-start.6
  8.5 0.0 copy-start.8
  8.5 0.0 copy-start.10
  8.6 3.4 %fusion.53 = (f32[2,1,8192]{2,1,0:T(1,128)S(1)}, f32[2,1,8192]{2,1,0:T(1,128)S(1)}, f32[2,1,8192]{2,1,0:T(1,128)S(1)}, f32[2,1,8192]{2,1,0:T(1,128)S(1)}, f32[2,...) fusion(f32[3,7,8192]{2,1,0:T(8,128)} %param.6), kind=kLoop, calls=%fused_computation.118 | loop fusion | bytes 917504 | tf_op jit(solution)/shard_map/slice | solution.py:33
  12.0 0.1 copy.88
  12.0 0.7 sqrt_multiply_fusion
  12.7 0.7 convert_multiply_fusion
  13.4 0.1 copy_bitcast_fusion
  13.5 0.1 copy_bitcast_fusion.2
  13.6 0.1 copy_bitcast_fusion.4
  13.7 0.1 exponential_select_fusion
  13.8 2.9 %collective-permute-done = bf16[6,3,8192]{2,0,1:T(8,128)(2,1)S(1)} collective-permute-done((bf16[6,3,8192]{2,0,1:T(8,128)(2,1)S(1)}, bf16[6,3,8192]{2,0,1:T(8,128)(2,1)S(1)}, u32[]{:S(2)}, u32[]{:S(2)}) %collective-permute-start) | collective-permute-done | bytes 294944 | tf_op jit(solution)/shard_map/ppermute | solution.py:12
  16.8 0.0 copy-done
  16.8 2.6 %multiply_add_fusion = f32[32,2,8192]{2,0,1:T(8,128)S(1)} fusion(bf16[32,3,8192]{2,0,1:T(8,128)(2,1)S(1)} %copy-done, bf16[6,3,8192]{2,0,1:T(8,128)(2,1)S(1)} %collective-permute-done, f32[32]{0:T(128)S(1)} %get-tuple-element.24, f32[2,8192]{1,0:T(2,128)S(1)} %get-tuple-element.29, f32[32]{0:T(128)S(1)} %get-tuple-element.25, ...), kind=kLoop, calls=%fused_computation.11 | loop fusion | flops 23592960 | bytes 5574144 | tf_op jit(solution)/shard_map/add | solution.py:32
  19.5 0.1 fusion.7
  19.6 0.1 copy.74
  19.7 1.1 %copy.48 = bf16[32,32,256]{2,0,1:T(8,128)(2,1)} copy(bf16[32,32,256]{2,1,0:T(8,128)(2,1)S(1)} %bitcast.87) | data formatting | bytes 1048576 | tf_op jit(solution)/shard_map/convert_element_type | solution.py:108
  20.8 6.7 %all-to-all-start = ((bf16[32,32,256]{2,0,1:T(8,128)(2,1)}), bf16[32,32,256]{2,0,1:T(8,128)(2,1)S(1)}, u32[]{:S(2)}, u32[]{:S(2)}) async-start(bf16[32,32,256]{2,0,1:T(8,128)(2,1)} %copy.48), calls=%async_computation | async-start | bytes 1048576 | tf_op jit(solution)/shard_map/all_to_all | solution.py:111
  27.5 0.5 iota_compare_fusion
  28.0 0.1 mul.534
  28.1 0.8 mul.535
  29.0 0.7 multiply_exponential_fusion.2
  29.7 2.0 %convolution_select_fusion = f32[4,256,256]{2,1,0:T(8,128)S(1)} fusion(pred[256,256]{1,0:T(8,128)(4,1)} %subtract_compare_fusion, f32[4,16]{1,0:T(4,128)S(1)} %get-tuple-element.6, f32[4,16]{1,0:T(4,128)S(1)} %neg.12, f32[4,16]{1,0:T(4,128)S(1)} %get-tuple-element.5), kind=kOutput, calls=%fused_computation.25 | convolution fusion | flops 50642944 | bytes 1114880 | tf_op jit(solution)/shard_map/grm,gms->grs/dot_general | solution.py:56
  31.7 7.0 %all-to-all-done = bf16[32,32,256]{2,0,1:T(8,128)(2,1)S(1)} async-done(((bf16[32,32,256]{2,0,1:T(8,128)(2,1)}), bf16[32,32,256]{2,0,1:T(8,128)(2,1)S(1)}, u32[]{:S(2)}, u32[]{:S(2)}) %all-to-all-start) | async-done | bytes 524320 | tf_op jit(solution)/shard_map/all_to_all | solution.py:111
  38.7 0.8 copy-done.1
  39.5 1.1 %copy.49 = bf16[4,8,32,256]{3,2,1,0:T(8,128)(2,1)S(1)} copy(bf16[4,8,32,256]{3,2,0,1:T(8,128)(2,1)} %bitcast.86) | data formatting | bytes 1048576 | tf_op jit(solution)/shard_map/transpose | solution.py:113
  40.6 1.4 %reshape_reshape.3 = bf16[4,256,4,64]{3,2,1,0:T(4,128)(2,1)} reshape(bf16[4,8,32,256]{3,2,1,0:T(8,128)(2,1)S(1)} %copy.49) | data formatting | bytes 1048576 | tf_op jit(solution)/shard_map/reshape;reshape | solution.py:59
  42.0 1.6 %copy.50 = bf16[4,256,4,64]{1,3,0,2:T(8,128)(2,1)S(1)} copy(bf16[4,256,4,64]{3,2,1,0:T(4,128)(2,1)} %reshape_reshape.3) | data formatting | bytes 1048576 | tf_op jit(solution)/shard_map/reshape;reshape | solution.py:59
  43.6 1.3 %fusion.17 = f32[4,4,64,256]{3,2,1,0:T(8,128)} fusion(bf16[4,256,4,64]{1,3,0,2:T(8,128)(2,1)S(1)} %copy.50, f32[4,256,256]{2,1,0:T(8,128)S(1)} %convolution_select_fusion), kind=kOutput, calls=%fused_computation.49 | convolution fusion | flops 134479872 | bytes 2621440 | tf_op jit(solution)/shard_map/grs,bsgc->brgc/dot_general | solution.py:43
  44.9 0.3 fusion.40
  45.3 0.4 convolution_add_fusion.2
  45.6 0.7 copy-done.2
  46.3 0.0 copy-done.3
  46.3 1.2 %fusion.25 = f32[4,16,1,64]{3,2,1,0:T(1,128)} fusion(f32[4,16,4,1]{2,3,1,0:T(1,128)S(1)} %bitcast.97, f32[4,16,4,64]{3,1,2,0:T(8,128)S(1)} %convolution_add_fusion.2), kind=kOutput, calls=%fused_computation.59 | convolution fusion | flops 196608 | bytes 82944 | tf_op jit(solution)/shard_map/gmb,gmbc->gmc/dot_general | solution.py:67
  47.5 1.4 %broadcast_in_dim.38 = f32[4096]{0:T(1024)} reshape(f32[4,16,64]{2,1,0:T(8,128)} %bitcast.96) | data formatting | bytes 32768 | tf_op jit(solution)/shard_map/broadcast_in_dim | solution.py:70
  48.9 1.4 %broadcast_in_dim.43 = f32[8,1,4096]{2,1,0:T(1,128)} broadcast(f32[4096]{0:T(1024)} %broadcast_in_dim.38), dimensions={2} | broadcast | bytes 147456 | tf_op jit(solution)/shard_map/broadcast_in_dim | solution.py:70
  50.3 8.3 %all-to-all-start.1 = ((f32[8,1,4096]{2,1,0:T(1,128)}), f32[8,1,4096]{2,1,0:T(1,128)}, u32[]{:S(2)}, u32[]{:S(2)}) async-start(f32[8,1,4096]{2,1,0:T(1,128)} %broadcast_in_dim.43), calls=%async_computation.1 | async-start | bytes 262144 | tf_op jit(solution)/shard_map/all_to_all | solution.py:71
  58.7 2.6 %convolution_add_fusion.1 = f32[4,4,64,256]{3,2,1,0:T(8,128)} fusion(f32[4,4,64,256]{3,2,1,0:T(8,128)} %fusion.17, bf16[4,256,4,64]{1,3,0,2:T(8,128)(2,1)S(1)} %copy.50, f32[4,256,256]{2,1,0:T(8,128)S(1)} %convolution_select_fusion), kind=kOutput, calls=%fused_computation.24 | convolution fusion | flops 135528448 | bytes 3670016 | tf_op jit(solution)/shard_map/grs,bsgc->brgc/dot_general | solution.py:44
  61.2 5.9 %all-to-all-done.1 = f32[8,1,4096]{2,1,0:T(1,128)} async-done(((f32[8,1,4096]{2,1,0:T(1,128)}), f32[8,1,4096]{2,1,0:T(1,128)}, u32[]{:S(2)}, u32[]{:S(2)}) %all-to-all-start.1) | async-done | bytes 131104 | tf_op jit(solution)/shard_map/all_to_all | solution.py:71
  67.1 1.1 %multiply_reduce_fusion = f32[4096]{0:T(1024)S(1)} fusion(f32[8,1,4096]{2,1,0:T(1,128)} %mul.535, f32[8,1,4096]{2,1,0:T(1,128)} %all-to-all-done.1), kind=kLoop, calls=%fused_computation.55 | loop fusion | flops 61440 | bytes 278528 | tf_op jit(solution)/shard_map/reduce_sum | solution.py:81
  68.2 0.1 reduce_sum.22
  68.3 1.5 %convolution_add_fusion.3 = f32[4,16,4,64]{3,2,1,0:T(4,128)S(1)} fusion(f32[4,16,4,64]{3,1,2,0:T(8,128)} %copy-done.2, f32[4,16,64]{2,1,0:T(8,128)S(1)} %reduce_sum.22, f32[4,16,4]{2,1,0:T(8,128)} %get-tuple-element.21, f32[4,4]{1,0:T(4,128)S(1)} %copy-done.17, f32[4,16]{1,0:T(4,128)S(1)} %neg.12, pred[4,4]{1,0:T(4,128)(4,1)} %iota_compare_fusion), kind=kOutput, calls=%fused_computation.29 | convolution fusion | flops 821248 | bytes 148816 | tf_op jit(solution)/shard_map/gmab,gmbc->gmac/dot_general | solution.py:88
  69.8 2.3 %fusion.1 = bf16[4,256,4,64]{1,3,0,2:T(8,128)(2,1)S(1)} fusion(f32[4,4,64,256]{3,2,1,0:T(8,128)} %convolution_add_fusion.1, f32[4,16,4,64]{3,2,1,0:T(4,128)S(1)} %convolution_add_fusion.3, f32[4,16]{1,0:T(4,128)S(1)} %neg.12, f32[4,16]{1,0:T(4,128)S(1)} %get-tuple-element.5), kind=kOutput, calls=%fused_computation.27 | convolution fusion | flops 50888704 | bytes 1638912 | tf_op jit(solution)/shard_map/grm,gmbc->brgc/dot_general | solution.py:91
  72.2 0.7 copy.56
  72.9 0.7 convert_element_type.168
  73.5 0.8 copy.57
  74.4 5.5 %all-to-all-start.2 = ((bf16[32,32,256]{2,1,0:T(8,128)(2,1)}), bf16[32,32,256]{2,1,0:T(8,128)(2,1)S(1)}, u32[]{:S(2)}, u32[]{:S(2)}) async-start(bf16[32,32,256]{2,1,0:T(8,128)(2,1)} %bitcast.28), calls=%async_computation.2 | async-start | bytes 1048576 | tf_op jit(solution)/shard_map/all_to_all | solution.py:123
  79.9 2.4 %fusion.52 = (f32[1,1,8192]{2,1,0:T(1,128)S(1)}, f32[1,1,8192]{2,1,0:T(1,128)S(1)}, f32[1,1,8192]{2,1,0:T(1,128)S(1)}, f32[1,1,8192]{2,1,0:T(1,128)S(1)}, f32[1,...) fusion(f32[3,7,8192]{2,1,0:T(8,128)} %param.6), kind=kLoop, calls=%fused_computation.117 | loop fusion | bytes 458752 | tf_op jit(solution)/shard_map/slice | solution.py:33
  82.3 8.8 %all-to-all-done.2 = bf16[32,32,256]{2,1,0:T(8,128)(2,1)S(1)} async-done(((bf16[32,32,256]{2,1,0:T(8,128)(2,1)}), bf16[32,32,256]{2,1,0:T(8,128)(2,1)S(1)}, u32[]{:S(2)}, u32[]{:S(2)}) %all-to-all-start.2) | async-done | bytes 524320 | tf_op jit(solution)/shard_map/all_to_all | solution.py:123
  91.1 0.1 convert_bitcast_fusion
  91.2 0.1 copy.73
  91.4 2.1 %fusion.8 = bf16[32,8192]{1,0:T(8,128)(2,1)} fusion(f32[32,8192]{1,0:T(8,128)S(1)} %bitcast.83, bf16[32,3,8192]{2,0,1:T(8,128)(2,1)S(1)} %copy-done, bf16[6,3,8192]{2,0,1:T(8,128)(2,1)S(1)} %collective-permute-done, f32[32]{0:T(128)S(1)} %copy-done.5, f32[8192]{0:T(1024)S(1)} %bitcast.90, f32[32]{0:T(128)S(1)} %copy-done.7, f32[8192]{0:T(1024)S(1)} %bitcast.91, ...), kind=kLoop, calls=%fused_computation.39 | loop fusion | flops 12320768 | bytes 4296192 | tf_op jit(solution)/shard_map/convert_element_type | solution.py:125
  (35 shorter events, 0.1 us)
Async XLA Ops:
  0.0 16.8 %copy-start = (bf16[32,3,8192]{2,0,1:T(8,128)(2,1)S(1)}, bf16[32,3,8192]{2,0,1:T(8,128)(2,1)}, u32[]{:S(2)}) copy-start(bf16[32,3,8192]{2,0,1:T(8,128)(2,1)} %param.5) | copy-start | bytes 4718596
  1.2 15.5 %collective-permute-start = (bf16[6,3,8192]{2,0,1:T(8,128)(2,1)S(1)}, bf16[6,3,8192]{2,0,1:T(8,128)(2,1)S(1)}, u32[]{:S(2)}, u32[]{:S(2)}) collective-permute-start(bf16[6,3,8192]{2,0,1:T(8,128)(2,1)S(1)} %slice.189), channel_id=1, source_target_pairs={{0,1},{1,2},{2,3},{3,4},{4,5},{5,6},{6,7},{7,8},{8,9},{9,10},{10,1... | collective-permute-start | bytes 884744 | tf_op jit(solution)/shard_map/ppermute | solution.py:12
  8.2 11.2 %copy-start.15 = (f32[32]{0:T(128)}, f32[32]{0:T(128)S(1)}, u32[]{:S(2)}) copy-start(f32[32]{0:T(128)S(1)} %compare_convert_fusion) | copy-start | bytes 388
  8.5 10.9 %copy-start.4 = (f32[32]{0:T(128)}, f32[32]{0:T(128)S(1)}, u32[]{:S(2)}) copy-start(f32[32]{0:T(128)S(1)} %get-tuple-element.24) | copy-start | bytes 388
  8.5 10.9 %copy-start.6 = (f32[32]{0:T(128)}, f32[32]{0:T(128)S(1)}, u32[]{:S(2)}) copy-start(f32[32]{0:T(128)S(1)} %get-tuple-element.25) | copy-start | bytes 388
  8.5 10.9 %copy-start.8 = (f32[32]{0:T(128)}, f32[32]{0:T(128)S(1)}, u32[]{:S(2)}) copy-start(f32[32]{0:T(128)S(1)} %get-tuple-element.26) | copy-start | bytes 388
  8.5 10.9 %copy-start.10 = (f32[32]{0:T(128)}, f32[32]{0:T(128)S(1)}, u32[]{:S(2)}) copy-start(f32[32]{0:T(128)S(1)} %get-tuple-element.27) | copy-start | bytes 388
  8.5 10.9 %copy-start.12 = (f32[32]{0:T(128)}, f32[32]{0:T(128)S(1)}, u32[]{:S(2)}) copy-start(f32[32]{0:T(128)S(1)} %get-tuple-element.28) | copy-start | bytes 388
  20.8 17.9 %all-to-all-start = ((bf16[32,32,256]{2,0,1:T(8,128)(2,1)}), bf16[32,32,256]{2,0,1:T(8,128)(2,1)S(1)}, u32[]{:S(2)}, u32[]{:S(2)}) async-start(bf16[32,32,256]{2,0,1:T(8,128)(2,1)} %copy.48), calls=%async_computation | async-start | bytes 1048576 | tf_op jit(solution)/shard_map/all_to_all | solution.py:111
  38.7 0.8 copy-start.1
  42.0 2.9 %copy-start.14 = (f32[256]{0:T(256)S(1)}, f32[256]{0:T(256)}, u32[]{:S(2)}) copy-start(f32[256]{0:T(256)} %iota_subtract_fusion) | copy-start | bytes 3076
  43.6 2.7 %copy-start.3 = (f32[4,16,4]{2,1,0:T(8,128)S(1)}, f32[4,16,4]{2,1,0:T(8,128)}, u32[]{:S(2)}) copy-start(f32[4,16,4]{2,1,0:T(8,128)} %get-tuple-element.22) | copy-start | bytes 3076
  45.6 0.7 copy-start.2
  50.3 17.9 %copy-start.17 = (f32[4,4]{1,0:T(4,128)S(1)}, f32[4,4]{1,0:T(4,128)}, u32[]{:S(2)}) copy-start(f32[4,4]{1,0:T(4,128)} %convert_multiply_fusion) | copy-start | bytes 196
  50.3 16.7 %all-to-all-start.1 = ((f32[8,1,4096]{2,1,0:T(1,128)}), f32[8,1,4096]{2,1,0:T(1,128)}, u32[]{:S(2)}, u32[]{:S(2)}) async-start(f32[8,1,4096]{2,1,0:T(1,128)} %broadcast_in_dim.43), calls=%async_computation.1 | async-start | bytes 262144 | tf_op jit(solution)/shard_map/all_to_all | solution.py:71
  74.4 16.7 %all-to-all-start.2 = ((bf16[32,32,256]{2,1,0:T(8,128)(2,1)}), bf16[32,32,256]{2,1,0:T(8,128)(2,1)S(1)}, u32[]{:S(2)}, u32[]{:S(2)}) async-start(bf16[32,32,256]{2,1,0:T(8,128)(2,1)} %bitcast.28), calls=%async_computation.2 | async-start | bytes 1048576 | tf_op jit(solution)/shard_map/all_to_all | solution.py:123
  79.9 11.5 %copy-start.5 = (f32[32]{0:T(128)S(1)}, f32[32]{0:T(128)}, u32[]{:S(2)}) copy-start(f32[32]{0:T(128)} %copy-done.4) | copy-start | bytes 388
  79.9 11.5 %copy-start.7 = (f32[32]{0:T(128)S(1)}, f32[32]{0:T(128)}, u32[]{:S(2)}) copy-start(f32[32]{0:T(128)} %copy-done.6) | copy-start | bytes 388
  79.9 11.5 %copy-start.9 = (f32[32]{0:T(128)S(1)}, f32[32]{0:T(128)}, u32[]{:S(2)}) copy-start(f32[32]{0:T(128)} %copy-done.8) | copy-start | bytes 388
  79.9 11.5 %copy-start.11 = (f32[32]{0:T(128)S(1)}, f32[32]{0:T(128)}, u32[]{:S(2)}) copy-start(f32[32]{0:T(128)} %copy-done.10) | copy-start | bytes 388
  79.9 11.5 %copy-start.13 = (f32[32]{0:T(128)S(1)}, f32[32]{0:T(128)}, u32[]{:S(2)}) copy-start(f32[32]{0:T(128)} %copy-done.12) | copy-start | bytes 388
  79.9 11.5 %copy-start.16 = (f32[32]{0:T(128)S(1)}, f32[32]{0:T(128)}, u32[]{:S(2)}) copy-start(f32[32]{0:T(128)} %copy-done.15) | copy-start | bytes 388

commit v12 on v10

--- a/solution.py
+++ b/solution.py
@@ -66,16 +66,12 @@
     to_end = jnp.exp(-decays[:, :, None] * (float(block_len) * (block_count - 1 - blocks))[None, None, :])
     run_state = jnp.einsum("gmb,gmbc->gmc", to_end, block_state, precision=HIGHEST)
     count = lax.axis_size(outer_axis)
-    gathered = lax.all_gather(run_state, outer_axis, axis=0)
-    here = lax.axis_index(outer_axis)
-    earlier = jnp.arange(count, dtype=jnp.int32)
-    gap = (here - 1 - earlier).astype(jnp.float32) * float(positions)
-    weight = jnp.where(
-        (earlier < here)[:, None, None],
-        jnp.exp(-decays[None] * jnp.maximum(gap, 0.0)[:, None, None]),
-        0.0,
-    )
-    incoming = jnp.sum(weight[:, :, :, None] * gathered, axis=0)
+    incoming = shifted(run_state, outer_axis, 1)
+    distance = 1
+    while distance < count - 1:
+        decay_k = jnp.exp(-decays * float(positions * distance))[:, :, None]
+        incoming = incoming + decay_k * shifted(incoming, outer_axis, distance)
+        distance *= 2
 
     later = jnp.arange(block_count)[:, None]
     before = jnp.arange(block_count)[None, :]

time: 94.5 us -> 98.8 us (1.046)
  starting transfers between devices: 10.7 us -> 35 us
  blocking collectives: 43.8 us -> 19.6 us
  other arithmetic: 8.69 us -> 11.7 us
  waiting for transfers between devices: 13.7 us -> 14.8 us
    ppermute x1 -> x5, starting transfers between devices: 4.02 us -> 28.3 us  [shifted(): return lax.ppermute(block, axis, route)]
    all_gather x1 -> x0, blocking collectives: 22.3 us -> none  [long_filter(): gathered = lax.all_gather(run_state, outer_axis, axis=0)]
    all_to_all x1, blocking collectives: 21.5 us -> 19.6 us  [shards(): lax.all_to_all(filtered, swap_axis, split_axis=0, concat_axis=1, tiled=True)]
    exp x0 -> x2, other arithmetic: none -> 1.4 us  [long_filter(): decay_k = jnp.exp(-decays * float(positions * distance))[:, :, None]]
    ppermute x1 -> x5, waiting for transfers between devices: 3.77 us -> 4.88 us  [shifted(): return lax.ppermute(block, axis, route)]
    convert_element_type x2, other arithmetic: 0.16 us -> 1.27 us  [short_convolution(): keep_mask.astype(jnp.float32)[:, None, None]]
    unnamed x9 -> x13, local copies, waits for them, and re-layouts: 2.25 us -> 2.23 us
  transfers between devices with their start and end apart: 2 -> 6, of which waited for: 2 -> 6; matrix products, arithmetic and copies ran while one was open for 9% -> 12% of each run, Pallas kernels for 0% -> 0%
where the time goes in v12:
time: 98.8 us; the launch traced here: 98.3 us
  starting transfers between devices  35 us (35%)
  blocking collectives  19.6 us (20%)
  waiting for transfers between devices  14.8 us (15%)
  local copies, waits for them, and re-layouts  12 us (12%)
  other arithmetic  11.7 us (12%)
  matrix products  4.88 us (5%)
    ppermute x5, starting transfers between devices, shifted(): return lax.ppermute(block, axis, route)  28.3 us
    all_to_all x1, blocking collectives, shards(): lax.all_to_all(filtered, swap_axis, split_axis=0, concat_axis=1, tiled=True)  19.6 us
    all_to_all x1, waiting for transfers between devices, shards(): lax.all_to_all(product, swap_axis, split_axis=1, concat_axis=0, tiled=True)  9.94 us
    all_to_all x1, starting transfers between devices, shards(): lax.all_to_all(product, swap_axis, split_axis=1, concat_axis=0, tiled=True)  6.69 us
    ppermute x5, waiting for transfers between devices, shifted(): return lax.ppermute(block, axis, route)  4.88 us
    add x1, other arithmetic, short_convolution(): result + conv_weight[:, position_shift, :][None] * earlier * keep_mask.as...  4.64 us
    slice x1, local copies, waits for them, and re-layouts, short_convolution(): conv_weight[:, position_shift, :][None] * earlier  4.23 us
    unnamed x13, local copies, waits for them, and re-layouts  2.23 us
  transfers between devices with their start and end apart: 6, of which 6 were waited for; matrix products, arithmetic and copies ran while one was open for 12% of the time, Pallas kernels for 0%

profile of v12, /device:TPU:1, one launch (start us, length us, event | category | flops | bytes accessed | tf_op | source)
XLA Modules:
  0.0 98.3 jit_solution(6417165313849359470)
XLA Ops:
  0.0 0.0 copy-start.1
  0.0 1.2 %slice.97 = bf16[6,3,8192]{2,0,1:T(8,128)(2,1)S(1)} slice(bf16[32,3,8192]{2,0,1:T(8,128)(2,1)} %param.5), slice={[26:32], [0:3], [0:8192]} | slice | bytes 589824 | tf_op jit(solution)/shard_map/slice | solution.py:95
  1.2 4.0 %collective-permute-start = (bf16[6,3,8192]{2,0,1:T(8,128)(2,1)S(1)}, bf16[6,3,8192]{2,0,1:T(8,128)(2,1)S(1)}, u32[]{:S(2)}, u32[]{:S(2)}) collective-permute-start(bf16[6,3,8192]{2,0,1:T(8,128)(2,1)S(1)} %slice.97), channel_id=1, source_target_pairs={{0,1},{1,2},{2,3},{3,4},{4,5},{5,6},{6,7},{7,8},{8,9},{9,10},{10,1... | collective-permute-start | bytes 884744 | tf_op jit(solution)/shard_map/ppermute | solution.py:12
  5.3 0.6 subtract_multiply_fusion
  5.9 0.7 copy.47
  6.6 0.1 reduce-window.9
  6.7 0.1 reduce
  6.8 0.7 sub.69
  7.5 0.6 compare_convert_fusion
  8.1 0.2 convert_reduce_fusion
  8.3 0.7 and_convert_fusion.5
  9.0 4.2 %fusion.52 = (f32[3,1,8192]{2,1,0:T(1,128)S(1)}, f32[3,1,8192]{2,1,0:T(1,128)S(1)}, f32[3,1,8192]{2,1,0:T(1,128)S(1)}, f32[3,1,8192]{2,1,0:T(1,128)S(1)}, f32[3,...) fusion(f32[3,7,8192]{2,1,0:T(8,128)} %param.6), kind=kLoop, calls=%fused_computation.103 | loop fusion | bytes 1376256 | tf_op jit(solution)/shard_map/slice | solution.py:33
  13.2 0.1 copy.90
  13.3 0.1 copy_bitcast_fusion
  13.4 0.1 copy_bitcast_fusion.2
  13.6 0.1 copy_bitcast_fusion.4
  13.7 0.7 multiply_exponential_fusion.3
  14.4 0.7 multiply_exponential_fusion.4
  15.1 1.6 %collective-permute-done = bf16[6,3,8192]{2,0,1:T(8,128)(2,1)S(1)} collective-permute-done((bf16[6,3,8192]{2,0,1:T(8,128)(2,1)S(1)}, bf16[6,3,8192]{2,0,1:T(8,128)(2,1)S(1)}, u32[]{:S(2)}, u32[]{:S(2)}) %collective-permute-start) | collective-permute-done | bytes 294944 | tf_op jit(solution)/shard_map/ppermute | solution.py:12
  16.8 0.0 copy-done.1
  16.8 4.6 %multiply_add_fusion = f32[32,3,8192]{2,0,1:T(8,128)S(1)} fusion(bf16[32,3,8192]{2,0,1:T(8,128)(2,1)S(1)} %copy-done.1, bf16[6,3,8192]{2,0,1:T(8,128)(2,1)S(1)} %collective-permute-done, f32[32]{0:T(128)S(1)} %get-tuple-element.21, f32[3,8192]{1,0:T(4,128)S(1)} %get-tuple-element.26, f32[32]{0:T(128)S(1)} %get-tuple-element.22, ...), kind=kLoop, calls=%fused_computation.5 | loop fusion | flops 35389440 | bytes 5702528 | tf_op jit(solution)/shard_map/add | solution.py:32
  21.4 0.0 copy-start
  21.4 1.6 %copy-done = f32[32,3,8192]{2,0,1:T(8,128)} copy-done((f32[32,3,8192]{2,0,1:T(8,128)}, f32[32,3,8192]{2,0,1:T(8,128)S(1)}, u32[]{:S(2)}) %copy-start) | copy-done | bytes 3145752
  23.0 0.0 copy-start.2
  23.0 0.0 copy-start.3
  23.0 0.1 fusion.7
  23.1 0.1 copy.74
  23.3 1.1 %copy.48 = bf16[32,32,256]{2,0,1:T(8,128)(2,1)} copy(bf16[32,32,256]{2,1,0:T(8,128)(2,1)S(1)} %bitcast.80) | data formatting | bytes 1048576 | tf_op jit(solution)/shard_map/convert_element_type | solution.py:102
  24.3 6.7 %all-to-all-start = ((bf16[32,32,256]{2,0,1:T(8,128)(2,1)}), bf16[32,32,256]{2,0,1:T(8,128)(2,1)S(1)}, u32[]{:S(2)}, u32[]{:S(2)}) async-start(bf16[32,32,256]{2,0,1:T(8,128)(2,1)} %copy.48), calls=%async_computation | async-start | bytes 1048576 | tf_op jit(solution)/shard_map/all_to_all | solution.py:105
  31.0 0.0 copy-done.2
  31.1 0.0 copy-done.3
  31.1 0.1 multiply_exponential_fusion.2
  31.2 1.2 %convolution_select_fusion = f32[4,256,256]{2,1,0:T(8,128)S(1)} fusion(pred[256,256]{1,0:T(8,128)(4,1)S(1)} %subtract_compare_fusion, f32[4,16]{1,0:T(4,128)S(1)} %get-tuple-element.6, f32[4,16]{1,0:T(4,128)S(1)} %get-tuple-element.18, f32[4,16]{1,0:T(4,128)S(1)} %get-tuple-element.19), kind=kOutput, calls=%fused_computation.19 | convolution fusion | flops 50642944 | bytes 1114880 | tf_op jit(solution)/shard_map/grm,gms->grs/dot_general | solution.py:56
  32.3 9.9 %all-to-all-done = bf16[32,32,256]{2,0,1:T(8,128)(2,1)S(1)} async-done(((bf16[32,32,256]{2,0,1:T(8,128)(2,1)}), bf16[32,32,256]{2,0,1:T(8,128)(2,1)S(1)}, u32[]{:S(2)}, u32[]{:S(2)}) %all-to-all-start) | async-done | bytes 524320 | tf_op jit(solution)/shard_map/all_to_all | solution.py:105
  42.3 0.4 reshape_reshape.3
  42.7 0.6 copy.50
  43.4 0.3 fusion.40
  43.7 0.4 convolution_add_fusion.2
  44.1 0.6 fusion.21
  44.7 3.5 %collective-permute-start.1 = (f32[4,16,64]{2,1,0:T(8,128)S(1)}, f32[4,16,64]{2,1,0:T(8,128)S(1)}, u32[]{:S(2)}, u32[]{:S(2)}) collective-permute-start(f32[4,16,64]{2,1,0:T(8,128)S(1)} %bitcast.85), channel_id=1, source_target_pairs={{0,32},{32,64},{64,96},{96,128},{128,160},{160,192},{192,224},{1,3... | collective-permute-start | bytes 49160 | tf_op jit(solution)/shard_map/ppermute | solution.py:12
  48.2 0.1 convert_multiply_fusion
  48.3 0.9 collective-permute-done.1
  49.2 3.6 %collective-permute-start.2 = (f32[4,16,64]{2,1,0:T(8,128)S(1)}, f32[4,16,64]{2,1,0:T(8,128)S(1)}, u32[]{:S(2)}, u32[]{:S(2)}) collective-permute-start(f32[4,16,64]{2,1,0:T(8,128)S(1)} %collective-permute-done.1), channel_id=1, source_target_pairs={{0,32},{32,64},{64,96},{96,128},{128,160},{160,192},{192,224},{1,3... | collective-permute-start | bytes 49160 | tf_op jit(solution)/shard_map/ppermute | solution.py:12
  52.9 1.0 %collective-permute-done.2 = f32[4,16,64]{2,1,0:T(8,128)S(1)} collective-permute-done((f32[4,16,64]{2,1,0:T(8,128)S(1)}, f32[4,16,64]{2,1,0:T(8,128)S(1)}, u32[]{:S(2)}, u32[]{:S(2)}) %collective-permute-start.2) | collective-permute-done | bytes 16416 | tf_op jit(solution)/shard_map/ppermute | solution.py:12
  53.9 0.1 multiply_add_fusion.4
  53.9 6.0 %collective-permute-start.3 = (f32[4,16,64]{2,1,0:T(8,128)S(1)}, f32[4,16,64]{2,1,0:T(8,128)S(1)}, u32[]{:S(2)}, u32[]{:S(2)}) collective-permute-start(f32[4,16,64]{2,1,0:T(8,128)S(1)} %multiply_add_fusion.4), channel_id=1, source_target_pairs={{0,64},{32,96},{64,128},{96,160},{128,192},{160,224},{1,65},{33,97... | collective-permute-start | bytes 49160 | tf_op jit(solution)/shard_map/ppermute | solution.py:12
  59.9 0.3 fusion.12
  60.3 0.7 collective-permute-done.3
  60.9 0.1 multiply_add_fusion.3
  61.0 11.1 %collective-permute-start.4 = (f32[4,16,64]{2,1,0:T(8,128)S(1)}, f32[4,16,64]{2,1,0:T(8,128)S(1)}, u32[]{:S(2)}, u32[]{:S(2)}) collective-permute-start(f32[4,16,64]{2,1,0:T(8,128)S(1)} %multiply_add_fusion.3), channel_id=1, source_target_pairs={{0,128},{32,160},{64,192},{96,224},{1,129},{33,161},{65,193},{97,2... | collective-permute-start | bytes 49160 | tf_op jit(solution)/shard_map/ppermute | solution.py:12
  72.1 0.3 convolution_add_fusion.1
  72.5 0.7 collective-permute-done.4
  73.1 0.1 multiply_add_fusion.2
  73.2 0.6 multiply_add_fusion.1
  73.9 1.1 %fusion.6 = bf16[4,256,4,64]{1,3,0,2:T(8,128)(2,1)S(1)} fusion(f32[4,4,64,256]{3,2,1,0:T(8,128)S(1)} %convolution_add_fusion.1, f32[4,16,4,64]{3,2,1,0:T(4,128)S(1)} %multiply_add_fusion.1, f32[4,16]{1,0:T(4,128)S(1)} %get-tuple-element.18, f32[4,16]{1,0:T(4,128)S(1)} %get-tuple-element.19), kind=kOutput, calls=%fused_computation.21 | convolution fusion | flops 50888704 | bytes 1638912 | tf_op jit(solution)/shard_map/grm,gmbc->brgc/dot_general | solution.py:84
  75.0 0.7 copy.56
  75.6 0.7 convert_element_type.125
  76.4 19.6 %all_to_all.26 = bf16[32,32,256]{2,1,0:T(8,128)(2,1)S(1)} all-to-all(bf16[32,32,256]{2,1,0:T(8,128)(2,1)S(1)} %bitcast.81), channel_id=1, replica_groups=mesh['zo'=8,'zi'=4,'mp'=8] {'mp','zi'}, dimensions={0} | all-to-all | bytes 1048576 | tf_op jit(solution)/shard_map/all_to_all | solution.py:117
  96.0 0.1 convert_bitcast_fusion
  96.1 0.1 copy.73
  96.2 2.1 %fusion.9 = bf16[32,8192]{1,0:T(8,128)(2,1)} fusion(f32[32,8192]{1,0:T(8,128)S(1)} %bitcast.76, f32[32,3,8192]{2,0,1:T(8,128)} %copy-done), kind=kLoop, calls=%fused_computation.27 | loop fusion | flops 524288 | bytes 2621440 | tf_op jit(solution)/shard_map/convert_element_type | solution.py:118
  (8 shorter events, 0.1 us)
Async XLA Ops:
  0.0 16.8 %copy-start.1 = (bf16[32,3,8192]{2,0,1:T(8,128)(2,1)S(1)}, bf16[32,3,8192]{2,0,1:T(8,128)(2,1)}, u32[]{:S(2)}) copy-start(bf16[32,3,8192]{2,0,1:T(8,128)(2,1)} %param.5) | copy-start | bytes 4718596
  1.2 15.5 %collective-permute-start = (bf16[6,3,8192]{2,0,1:T(8,128)(2,1)S(1)}, bf16[6,3,8192]{2,0,1:T(8,128)(2,1)S(1)}, u32[]{:S(2)}, u32[]{:S(2)}) collective-permute-start(bf16[6,3,8192]{2,0,1:T(8,128)(2,1)S(1)} %slice.97), channel_id=1, source_target_pairs={{0,1},{1,2},{2,3},{3,4},{4,5},{5,6},{6,7},{7,8},{8,9},{9,10},{10,1... | collective-permute-start | bytes 884744 | tf_op jit(solution)/shard_map/ppermute | solution.py:12
  21.4 1.6 %copy-start = (f32[32,3,8192]{2,0,1:T(8,128)}, f32[32,3,8192]{2,0,1:T(8,128)S(1)}, u32[]{:S(2)}) copy-start(f32[32,3,8192]{2,0,1:T(8,128)S(1)} %multiply_add_fusion) | copy-start | bytes 9437188
  23.0 8.0 %copy-start.2 = (f32[4]{0:T(128)S(1)}, f32[4]{0:T(128)}, u32[]{:S(2)}) copy-start(f32[4]{0:T(128)} %get-tuple-element.32) | copy-start | bytes 52
  23.0 8.0 %copy-start.3 = (f32[4]{0:T(128)S(1)}, f32[4]{0:T(128)}, u32[]{:S(2)}) copy-start(f32[4]{0:T(128)} %get-tuple-element.33) | copy-start | bytes 52
  24.3 17.9 %all-to-all-start = ((bf16[32,32,256]{2,0,1:T(8,128)(2,1)}), bf16[32,32,256]{2,0,1:T(8,128)(2,1)S(1)}, u32[]{:S(2)}, u32[]{:S(2)}) async-start(bf16[32,32,256]{2,0,1:T(8,128)(2,1)} %copy.48), calls=%async_computation | async-start | bytes 1048576 | tf_op jit(solution)/shard_map/all_to_all | solution.py:105
  44.7 4.6 %collective-permute-start.1 = (f32[4,16,64]{2,1,0:T(8,128)S(1)}, f32[4,16,64]{2,1,0:T(8,128)S(1)}, u32[]{:S(2)}, u32[]{:S(2)}) collective-permute-start(f32[4,16,64]{2,1,0:T(8,128)S(1)} %bitcast.85), channel_id=1, source_target_pairs={{0,32},{32,64},{64,96},{96,128},{128,160},{160,192},{192,224},{1,3... | collective-permute-start | bytes 49160 | tf_op jit(solution)/shard_map/ppermute | solution.py:12
  49.2 4.6 %collective-permute-start.2 = (f32[4,16,64]{2,1,0:T(8,128)S(1)}, f32[4,16,64]{2,1,0:T(8,128)S(1)}, u32[]{:S(2)}, u32[]{:S(2)}) collective-permute-start(f32[4,16,64]{2,1,0:T(8,128)S(1)} %collective-permute-done.1), channel_id=1, source_target_pairs={{0,32},{32,64},{64,96},{96,128},{128,160},{160,192},{192,224},{1,3... | collective-permute-start | bytes 49160 | tf_op jit(solution)/shard_map/ppermute | solution.py:12
  53.9 7.0 %collective-permute-start.3 = (f32[4,16,64]{2,1,0:T(8,128)S(1)}, f32[4,16,64]{2,1,0:T(8,128)S(1)}, u32[]{:S(2)}, u32[]{:S(2)}) collective-permute-start(f32[4,16,64]{2,1,0:T(8,128)S(1)} %multiply_add_fusion.4), channel_id=1, source_target_pairs={{0,64},{32,96},{64,128},{96,160},{128,192},{160,224},{1,65},{33,97... | collective-permute-start | bytes 49160 | tf_op jit(solution)/shard_map/ppermute | solution.py:12
  61.0 12.1 %collective-permute-start.4 = (f32[4,16,64]{2,1,0:T(8,128)S(1)}, f32[4,16,64]{2,1,0:T(8,128)S(1)}, u32[]{:S(2)}, u32[]{:S(2)}) collective-permute-start(f32[4,16,64]{2,1,0:T(8,128)S(1)} %multiply_add_fusion.3), channel_id=1, source_target_pairs={{0,128},{32,160},{64,192},{96,224},{1,129},{33,161},{65,193},{97,2... | collective-permute-start | bytes 49160 | tf_op jit(solution)/shard_map/ppermute | solution.py:12

commit v13 on v6

--- a/solution.py
+++ b/solution.py
@@ -4,6 +4,7 @@
 from jax.sharding import Mesh, NamedSharding, PartitionSpec as P
 
 HIGHEST = lax.Precision.HIGHEST
+HIGH = lax.Precision.HIGH
 
 
 def shifted(block, axis, distance):
@@ -64,7 +65,7 @@
 
     blocks = jnp.arange(block_count, dtype=jnp.float32)
     to_end = jnp.exp(-decays[:, :, None] * (float(block_len) * (block_count - 1 - blocks))[None, None, :])
-    run_state = jnp.einsum("gmb,gmbc->gmc", to_end, block_state, precision=HIGHEST)
+    run_state = jnp.einsum("gmb,gmbc->gmc", to_end, block_state, precision=HIGH)
     count = lax.axis_size(outer_axis)
     flat = run_state.reshape(1, -1)
     sent = jnp.broadcast_to(flat, (count, flat.shape[1]))
@@ -84,12 +85,13 @@
     before = jnp.arange(block_count)[None, :]
     block_gap = jnp.maximum(later - 1 - before, 0).astype(jnp.float32) * float(block_len)
     carry = jnp.where((before < later)[None, None], jnp.exp(-decays[:, :, None, None] * block_gap[None, None]), 0.0)
+    state = jnp.einsum("gmab,gmbc->gmac", carry, block_state, precision=HIGH)
+    partial = intra + jnp.einsum("grm,gmbc->brgc", left, state, precision=HIGH)
+
     start_decay = jnp.exp(-decays[:, :, None] * (float(block_len) * blocks)[None, None, :])
-    state = jnp.einsum("gmab,gmbc->gmac", carry, block_state, precision=HIGHEST)
-    state = state + start_decay[:, :, :, None] * incoming[:, :, None, :]
-
-    inter = jnp.einsum("grm,gmbc->brgc", left, state, precision=HIGHEST)
-    return (intra + inter).reshape(positions, channels).astype(jnp.bfloat16)
+    run_left = left[:, None, :, :] * jnp.transpose(start_decay, (0, 2, 1))[:, :, None, :]
+    outer = jnp.einsum("gbrm,gmc->brgc", run_left, incoming, precision=HIGH)
+    return (partial + outer).reshape(positions, channels).astype(jnp.bfloat16)
 
 
 def shards(proj, conv_weight, residues, decays, doc_lengths):

time: 85.6 us -> 84.2 us (0.984)
  matrix products: 7.09 us -> 4.68 us
    dot_general x3 -> x4, matrix products: 3.58 us -> 2.16 us  [the longest x1 0.73 us: long_filter(): partial = intra + jnp.einsum('grm,gmbc->brgc', left, state, precision=HIGH)]
    dot_general x2, matrix products: 1.68 us -> 0.7 us  [split_product(): jnp.einsum(form, lower_part, inputs, preferred_element_type=jnp.float32)]
    all_to_all x1, waiting for transfers between devices: 6.99 us -> 7.91 us  [long_filter(): lax.all_to_all(sent, outer_axis, split_axis=0, concat_axis=0, tiled=True)]
where the time goes in v13:
time: 84.2 us; the launch traced here: 83.7 us
  waiting for transfers between devices  21.1 us (25%)
  starting transfers between devices  18.9 us (22%)
  blocking collectives  16.5 us (20%)
  local copies, waits for them, and re-layouts  13.2 us (16%)
  other arithmetic  8.87 us (11%)
  matrix products  4.68 us (6%)
    all_to_all x1, blocking collectives, shards(): lax.all_to_all(filtered, swap_axis, split_axis=0, concat_axis=1, tiled=True)  16.5 us
    all_to_all x1, waiting for transfers between devices, shards(): lax.all_to_all(product, swap_axis, split_axis=1, concat_axis=0, tiled=True)  9.64 us
    all_to_all x1, starting transfers between devices, long_filter(): lax.all_to_all(sent, outer_axis, split_axis=0, concat_axis=0, tiled=True)  8.19 us
    all_to_all x1, waiting for transfers between devices, long_filter(): lax.all_to_all(sent, outer_axis, split_axis=0, concat_axis=0, tiled=True)  7.91 us
    all_to_all x1, starting transfers between devices, shards(): lax.all_to_all(product, swap_axis, split_axis=1, concat_axis=0, tiled=True)  6.68 us
    slice x1, local copies, waits for them, and re-layouts, short_convolution(): conv_weight[:, position_shift, :][None] * earlier  4.22 us
    ppermute x1, starting transfers between devices, shifted(): return lax.ppermute(block, axis, route)  4.02 us
    add x1, other arithmetic, short_convolution(): result + conv_weight[:, position_shift, :][None] * earlier * keep_mask.as...  3.98 us
  transfers between devices with their start and end apart: 3, of which 3 were waited for; matrix products, arithmetic and copies ran while one was open for 12% of the time, Pallas kernels for 0%

profile of v13, /device:TPU:1, one launch (start us, length us, event | category | flops | bytes accessed | tf_op | source)
XLA Modules:
  0.0 83.7 jit_solution(5901944600787423640)
XLA Ops:
  0.0 0.0 copy-start.1
  0.0 1.2 %slice.97 = bf16[6,3,8192]{2,0,1:T(8,128)(2,1)S(1)} slice(bf16[32,3,8192]{2,0,1:T(8,128)(2,1)} %param.5), slice={[26:32], [0:3], [0:8192]} | slice | bytes 589824 | tf_op jit(solution)/shard_map/slice | solution.py:104
  1.2 4.0 %collective-permute-start = (bf16[6,3,8192]{2,0,1:T(8,128)(2,1)S(1)}, bf16[6,3,8192]{2,0,1:T(8,128)(2,1)S(1)}, u32[]{:S(2)}, u32[]{:S(2)}) collective-permute-start(bf16[6,3,8192]{2,0,1:T(8,128)(2,1)S(1)} %slice.97), channel_id=1, source_target_pairs={{0,1},{1,2},{2,3},{3,4},{4,5},{5,6},{6,7},{7,8},{8,9},{9,10},{10,1... | collective-permute-start | bytes 884744 | tf_op jit(solution)/shard_map/ppermute | solution.py:13
  5.4 0.7 copy.47
  6.1 0.1 reduce-window.9
  6.2 0.1 reduce.3
  6.3 0.7 sub.82
  7.0 0.1 compare_convert_fusion
  7.1 0.2 convert_reduce_fusion
  7.2 0.1 and_convert_fusion.5
  7.3 4.2 %fusion.53 = (f32[3,1,8192]{2,1,0:T(1,128)S(1)}, f32[3,1,8192]{2,1,0:T(1,128)S(1)}, f32[3,1,8192]{2,1,0:T(1,128)S(1)}, f32[3,1,8192]{2,1,0:T(1,128)S(1)}, f32[3,...) fusion(f32[3,7,8192]{2,1,0:T(8,128)} %param.6), kind=kLoop, calls=%fused_computation.106 | loop fusion | bytes 1376256 | tf_op jit(solution)/shard_map/slice | solution.py:34
  11.6 0.1 copy.89
  11.6 0.7 sqrt_multiply_fusion
  12.4 0.1 convert_multiply_fusion
  12.5 0.1 copy_bitcast_fusion
  12.6 0.1 copy_bitcast_fusion.2
  12.7 0.1 copy_bitcast_fusion.4
  12.9 0.1 multiply_exponential_fusion.2
  13.0 0.1 exponential_select_fusion
  13.1 0.1 multiply_exponential_fusion.1
  13.2 3.6 %collective-permute-done = bf16[6,3,8192]{2,0,1:T(8,128)(2,1)S(1)} collective-permute-done((bf16[6,3,8192]{2,0,1:T(8,128)(2,1)S(1)}, bf16[6,3,8192]{2,0,1:T(8,128)(2,1)S(1)}, u32[]{:S(2)}, u32[]{:S(2)}) %collective-permute-start) | collective-permute-done | bytes 294944 | tf_op jit(solution)/shard_map/ppermute | solution.py:13
  16.8 0.0 copy-done.1
  16.8 4.0 %multiply_add_fusion = f32[32,3,8192]{2,0,1:T(8,128)S(1)} fusion(bf16[32,3,8192]{2,0,1:T(8,128)(2,1)S(1)} %copy-done.1, bf16[6,3,8192]{2,0,1:T(8,128)(2,1)S(1)} %collective-permute-done, f32[32]{0:T(128)S(1)} %get-tuple-element.15, f32[3,8192]{1,0:T(4,128)S(1)} %get-tuple-element.20, f32[32]{0:T(128)S(1)} %get-tuple-element.16, ...), kind=kLoop, calls=%fused_computation.5 | loop fusion | flops 35389440 | bytes 5702528 | tf_op jit(solution)/shard_map/add | solution.py:33
  20.7 0.0 copy-start
  20.8 1.6 %copy-done = f32[32,3,8192]{2,0,1:T(8,128)} copy-done((f32[32,3,8192]{2,0,1:T(8,128)}, f32[32,3,8192]{2,0,1:T(8,128)S(1)}, u32[]{:S(2)}) %copy-start) | copy-done | bytes 3145752
  22.4 0.1 fusion.8
  22.5 0.1 copy.75
  22.6 1.1 %copy.48 = bf16[32,32,256]{2,0,1:T(8,128)(2,1)} copy(bf16[32,32,256]{2,1,0:T(8,128)(2,1)S(1)} %bitcast.91) | data formatting | bytes 1048576 | tf_op jit(solution)/shard_map/convert_element_type | solution.py:111
  23.7 6.7 %all-to-all-start = ((bf16[32,32,256]{2,0,1:T(8,128)(2,1)}), bf16[32,32,256]{2,0,1:T(8,128)(2,1)S(1)}, u32[]{:S(2)}, u32[]{:S(2)}) async-start(bf16[32,32,256]{2,0,1:T(8,128)(2,1)} %copy.48), calls=%async_computation | async-start | bytes 1048576 | tf_op jit(solution)/shard_map/all_to_all | solution.py:114
  30.4 0.1 mul.379
  30.5 0.2 mul.380
  30.7 0.1 exponential_multiply_fusion
  30.8 1.2 %convolution_select_fusion = f32[4,256,256]{2,1,0:T(8,128)S(1)} fusion(pred[256,256]{1,0:T(8,128)(4,1)S(1)} %subtract_compare_fusion, f32[4,16]{1,0:T(4,128)S(1)} %get-tuple-element.6, f32[4,16]{1,0:T(4,128)S(1)} %neg.12, f32[4,16]{1,0:T(4,128)S(1)} %get-tuple-element.5), kind=kOutput, calls=%fused_computation.22 | convolution fusion | flops 50642944 | bytes 1114880 | tf_op jit(solution)/shard_map/grm,gms->grs/dot_general | solution.py:57
  32.0 9.6 %all-to-all-done = bf16[32,32,256]{2,0,1:T(8,128)(2,1)S(1)} async-done(((bf16[32,32,256]{2,0,1:T(8,128)(2,1)}), bf16[32,32,256]{2,0,1:T(8,128)(2,1)S(1)}, u32[]{:S(2)}, u32[]{:S(2)}) %all-to-all-start) | async-done | bytes 524320 | tf_op jit(solution)/shard_map/all_to_all | solution.py:114
  41.7 0.4 reshape_reshape.3
  42.1 0.6 copy.50
  42.8 0.3 fusion.13
  43.1 0.3 convolution_add_fusion.1
  43.4 0.3 fusion.40
  43.8 0.4 convolution_add_fusion.2
  44.1 0.4 fusion.25
  44.5 0.1 broadcast_in_dim.38
  44.6 0.7 broadcast_in_dim.43
  45.3 8.2 %all-to-all-start.1 = ((f32[8,1,4096]{2,1,0:T(1,128)}), f32[8,1,4096]{2,1,0:T(1,128)S(1)}, u32[]{:S(2)}, u32[]{:S(2)}) async-start(f32[8,1,4096]{2,1,0:T(1,128)} %broadcast_in_dim.43), calls=%async_computation.1 | async-start | bytes 262144 | tf_op jit(solution)/shard_map/all_to_all | solution.py:72
  53.5 0.4 fusion.21
  53.9 7.9 %all-to-all-done.1 = f32[8,1,4096]{2,1,0:T(1,128)S(1)} async-done(((f32[8,1,4096]{2,1,0:T(1,128)}), f32[8,1,4096]{2,1,0:T(1,128)S(1)}, u32[]{:S(2)}, u32[]{:S(2)}) %all-to-all-start.1) | async-done | bytes 131104 | tf_op jit(solution)/shard_map/all_to_all | solution.py:72
  61.8 0.2 multiply_reduce_fusion
  62.0 0.1 reshape.193
  62.0 0.6 convolution_bitcast_fusion
  62.7 0.7 fusion.7
  63.4 0.7 copy.56
  64.1 0.7 convert_element_type.129
  64.8 16.5 %all_to_all.32 = bf16[32,32,256]{2,1,0:T(8,128)(2,1)S(1)} all-to-all(bf16[32,32,256]{2,1,0:T(8,128)(2,1)S(1)} %bitcast.92), channel_id=1, replica_groups=mesh['zo'=8,'zi'=4,'mp'=8] {'mp','zi'}, dimensions={0} | all-to-all | bytes 1048576 | tf_op jit(solution)/shard_map/all_to_all | solution.py:126
  81.3 0.1 convert_bitcast_fusion
  81.4 0.1 copy.74
  81.5 2.1 %fusion.10 = bf16[32,8192]{1,0:T(8,128)(2,1)} fusion(f32[32,8192]{1,0:T(8,128)S(1)} %bitcast.87, f32[32,3,8192]{2,0,1:T(8,128)} %copy-done), kind=kLoop, calls=%fused_computation.29 | loop fusion | flops 524288 | bytes 2621440 | tf_op jit(solution)/shard_map/convert_element_type | solution.py:127
  (13 shorter events, 0.2 us)
Async XLA Ops:
  0.0 16.8 %copy-start.1 = (bf16[32,3,8192]{2,0,1:T(8,128)(2,1)S(1)}, bf16[32,3,8192]{2,0,1:T(8,128)(2,1)}, u32[]{:S(2)}) copy-start(bf16[32,3,8192]{2,0,1:T(8,128)(2,1)} %param.5) | copy-start | bytes 4718596
  1.2 15.5 %collective-permute-start = (bf16[6,3,8192]{2,0,1:T(8,128)(2,1)S(1)}, bf16[6,3,8192]{2,0,1:T(8,128)(2,1)S(1)}, u32[]{:S(2)}, u32[]{:S(2)}) collective-permute-start(bf16[6,3,8192]{2,0,1:T(8,128)(2,1)S(1)} %slice.97), channel_id=1, source_target_pairs={{0,1},{1,2},{2,3},{3,4},{4,5},{5,6},{6,7},{7,8},{8,9},{9,10},{10,1... | collective-permute-start | bytes 884744 | tf_op jit(solution)/shard_map/ppermute | solution.py:13
  20.7 1.7 %copy-start = (f32[32,3,8192]{2,0,1:T(8,128)}, f32[32,3,8192]{2,0,1:T(8,128)S(1)}, u32[]{:S(2)}) copy-start(f32[32,3,8192]{2,0,1:T(8,128)S(1)} %multiply_add_fusion) | copy-start | bytes 9437188
  23.7 17.9 %all-to-all-start = ((bf16[32,32,256]{2,0,1:T(8,128)(2,1)}), bf16[32,32,256]{2,0,1:T(8,128)(2,1)S(1)}, u32[]{:S(2)}, u32[]{:S(2)}) async-start(bf16[32,32,256]{2,0,1:T(8,128)(2,1)} %copy.48), calls=%async_computation | async-start | bytes 1048576 | tf_op jit(solution)/shard_map/all_to_all | solution.py:114
  45.3 16.5 %all-to-all-start.1 = ((f32[8,1,4096]{2,1,0:T(1,128)}), f32[8,1,4096]{2,1,0:T(1,128)S(1)}, u32[]{:S(2)}, u32[]{:S(2)}) async-start(f32[8,1,4096]{2,1,0:T(1,128)} %broadcast_in_dim.43), calls=%async_computation.1 | async-start | bytes 262144 | tf_op jit(solution)/shard_map/all_to_all | solution.py:72

commit v14 on v13

--- a/solution.py
+++ b/solution.py
@@ -106,9 +106,8 @@
     padded_pos = lin_index * rows - (kernel_len - 1) + jnp.arange(rows + kernel_len - 1, dtype=jnp.int32)
     padded_document_ids = document_number_index(doc_lengths, padded_pos)
     padded = jnp.concatenate([tail_rows, proj], axis=0)
-    conv = short_convolution(padded, conv_weight, padded_document_ids, padded_pos, rows)
-    query_part = conv[:, 0]
-    product = (conv[:, 1] * conv[:, 2]).astype(jnp.bfloat16)
+    pair = short_convolution(padded[:, 1:], conv_weight[1:], padded_document_ids, padded_pos, rows)
+    product = (pair[:, 0] * pair[:, 1]).astype(jnp.bfloat16)
 
     swap_axis = ("mp", "zi")
     gathered = lax.all_to_all(product, swap_axis, split_axis=1, concat_axis=0, tiled=True)
@@ -124,6 +123,7 @@
     filtered = filtered.reshape(inner_size, mp_size, rows, width).transpose(1, 0, 2, 3)
     filtered = filtered.reshape(inner_size * mp_size * rows, width)
     filtered = lax.all_to_all(filtered, swap_axis, split_axis=0, concat_axis=1, tiled=True)
+    query_part = short_convolution(padded[:, :1], conv_weight[:1], padded_document_ids, padded_pos, rows)[:, 0]
     return (query_part * filtered.astype(jnp.float32)).astype(jnp.bfloat16)
 
 

time: 84.2 us -> 91.3 us (1.084)
  blocking collectives: 16.5 us -> 0 us
  local copies, waits for them, and re-layouts: 13.2 us -> 19.9 us
  starting transfers between devices: 18.9 us -> 24.4 us
  matrix products: 4.68 us -> 9.04 us
  waiting for transfers between devices: 21.1 us -> 24.9 us
  other arithmetic: 8.87 us -> 12 us
    all_to_all x1 -> x0, blocking collectives: 16.5 us -> none  [shards(): lax.all_to_all(filtered, swap_axis, split_axis=0, concat_axis=1, tiled=True)]
    all_to_all x0 -> x1, waiting for transfers between devices: none -> 8.76 us  [shards(): lax.all_to_all(filtered, swap_axis, split_axis=0, concat_axis=1, tiled=True)]
    all_to_all x0 -> x1, starting transfers between devices: none -> 5.47 us  [shards(): lax.all_to_all(filtered, swap_axis, split_axis=0, concat_axis=1, tiled=True)]
    all_to_all x1, waiting for transfers between devices: 9.64 us -> 7.03 us  [shards(): lax.all_to_all(product, swap_axis, split_axis=1, concat_axis=0, tiled=True)]
    another operation x2, local copies, waits for them, and re-layouts: 1.04 us -> 2.99 us  [long_filter(): inputs = product.reshape(block_count, block_len, group_count, group_width)]
    slice x1 -> x2, local copies, waits for them, and re-layouts: 4.22 us -> 5.82 us  [short_convolution(): conv_weight[:, position_shift, :][None] * earlier]
    ppermute x1, waiting for transfers between devices: 3.59 us -> 2.11 us  [shifted(): return lax.ppermute(block, axis, route)]
    add x1, other arithmetic: 3.98 us -> 2.64 us  [short_convolution(): result + conv_weight[:, position_shift, :][None] * earlier * keep_mask.as...]
  transfers between devices with their start and end apart: 3 -> 4, of which waited for: 3 -> 4; matrix products, arithmetic and copies ran while one was open for 12% -> 19% of each run, Pallas kernels for 0% -> 0%
where the time goes in v14:
time: 91.3 us; the launch traced here: 90.6 us
  waiting for transfers between devices  24.9 us (27%)
  starting transfers between devices  24.4 us (27%)
  local copies, waits for them, and re-layouts  19.9 us (22%)
  other arithmetic  12 us (13%)
  matrix products  9.04 us (10%)
    all_to_all x1, waiting for transfers between devices, shards(): lax.all_to_all(filtered, swap_axis, split_axis=0, concat_axis=1, tiled=True)  8.76 us
    all_to_all x1, starting transfers between devices, long_filter(): lax.all_to_all(sent, outer_axis, split_axis=0, concat_axis=0, tiled=True)  8.19 us
    all_to_all x1, waiting for transfers between devices, shards(): lax.all_to_all(product, swap_axis, split_axis=1, concat_axis=0, tiled=True)  7.03 us
    all_to_all x1, waiting for transfers between devices, long_filter(): lax.all_to_all(sent, outer_axis, split_axis=0, concat_axis=0, tiled=True)  6.99 us
    all_to_all x1, starting transfers between devices, shards(): lax.all_to_all(product, swap_axis, split_axis=1, concat_axis=0, tiled=True)  6.68 us
    slice x2, local copies, waits for them, and re-layouts, short_convolution(): conv_weight[:, position_shift, :][None] * earlier  5.82 us
    all_to_all x1, starting transfers between devices, shards(): lax.all_to_all(filtered, swap_axis, split_axis=0, concat_axis=1, tiled=True)  5.47 us
    ppermute x1, starting transfers between devices, shifted(): return lax.ppermute(block, axis, route)  4.02 us
  transfers between devices with their start and end apart: 4, of which 4 were waited for; matrix products, arithmetic and copies ran while one was open for 19% of the time, Pallas kernels for 0%

profile of v14, /device:TPU:1, one launch (start us, length us, event | category | flops | bytes accessed | tf_op | source)
XLA Modules:
  0.0 90.6 jit_solution(17096997166888279631)
XLA Ops:
  0.0 1.2 %slice.189 = bf16[6,3,8192]{2,0,1:T(8,128)(2,1)S(1)} slice(bf16[32,3,8192]{2,0,1:T(8,128)(2,1)} %param.5), slice={[26:32], [0:3], [0:8192]} | slice | bytes 589824 | tf_op jit(solution)/shard_map/slice | solution.py:104
  1.2 4.0 %collective-permute-start = (bf16[6,3,8192]{2,0,1:T(8,128)(2,1)S(1)}, bf16[6,3,8192]{2,0,1:T(8,128)(2,1)S(1)}, u32[]{:S(2)}, u32[]{:S(2)}) collective-permute-start(bf16[6,3,8192]{2,0,1:T(8,128)(2,1)S(1)} %slice.189), channel_id=1, source_target_pairs={{0,1},{1,2},{2,3},{3,4},{4,5},{5,6},{6,7},{7,8},{8,9},{9,10},{10,1... | collective-permute-start | bytes 884744 | tf_op jit(solution)/shard_map/ppermute | solution.py:13
  5.2 0.7 subtract_compare_fusion
  5.9 0.6 iota_subtract_fusion
  6.5 0.7 copy.47
  7.3 0.1 reduce-window.9
  7.4 0.1 reduce.3
  7.5 0.7 sub.82
  8.1 0.1 compare_convert_fusion
  8.2 0.2 convert_reduce_fusion
  8.4 0.1 and_convert_fusion.5
  8.5 0.0 copy-start.6
  8.5 0.0 copy-start.8
  8.5 0.0 copy-start.10
  8.6 3.4 %fusion.59 = (f32[2,1,8192]{2,1,0:T(1,128)S(1)}, f32[2,1,8192]{2,1,0:T(1,128)S(1)}, f32[2,1,8192]{2,1,0:T(1,128)S(1)}, f32[2,1,8192]{2,1,0:T(1,128)S(1)}, f32[2,...) fusion(f32[3,7,8192]{2,1,0:T(8,128)} %param.6), kind=kLoop, calls=%fused_computation.124 | loop fusion | bytes 917504 | tf_op jit(solution)/shard_map/slice | solution.py:34
  12.0 0.1 copy.89
  12.0 0.7 sqrt_multiply_fusion
  12.8 0.7 convert_multiply_fusion
  13.4 0.1 copy_bitcast_fusion
  13.5 0.1 copy_bitcast_fusion.2
  13.7 0.1 copy_bitcast_fusion.4
  13.8 0.1 multiply_exponential_fusion.2
  13.9 0.1 exponential_select_fusion
  14.0 0.7 multiply_exponential_fusion.1
  14.6 2.1 %collective-permute-done = bf16[6,3,8192]{2,0,1:T(8,128)(2,1)S(1)} collective-permute-done((bf16[6,3,8192]{2,0,1:T(8,128)(2,1)S(1)}, bf16[6,3,8192]{2,0,1:T(8,128)(2,1)S(1)}, u32[]{:S(2)}, u32[]{:S(2)}) %collective-permute-start) | collective-permute-done | bytes 294944 | tf_op jit(solution)/shard_map/ppermute | solution.py:13
  16.8 2.6 %multiply_add_fusion = f32[32,2,8192]{2,0,1:T(8,128)S(1)} fusion(bf16[32,3,8192]{2,0,1:T(8,128)(2,1)S(1)} %copy-done, bf16[6,3,8192]{2,0,1:T(8,128)(2,1)S(1)} %collective-permute-done, f32[32]{0:T(128)S(1)} %get-tuple-element.22, f32[2,8192]{1,0:T(2,128)S(1)} %get-tuple-element.27, f32[32]{0:T(128)S(1)} %get-tuple-element.23, ...), kind=kLoop, calls=%fused_computation.11 | loop fusion | flops 23592960 | bytes 5574144 | tf_op jit(solution)/shard_map/add | solution.py:33
  19.5 0.1 fusion.8
  19.6 0.1 copy.75
  19.7 1.1 %copy.48 = bf16[32,32,256]{2,0,1:T(8,128)(2,1)} copy(bf16[32,32,256]{2,1,0:T(8,128)(2,1)S(1)} %bitcast.96) | data formatting | bytes 1048576 | tf_op jit(solution)/shard_map/convert_element_type | solution.py:110
  20.8 6.7 %all-to-all-start = ((bf16[32,32,256]{2,0,1:T(8,128)(2,1)}), bf16[32,32,256]{2,0,1:T(8,128)(2,1)S(1)}, u32[]{:S(2)}, u32[]{:S(2)}) async-start(bf16[32,32,256]{2,0,1:T(8,128)(2,1)} %copy.48), calls=%async_computation | async-start | bytes 1048576 | tf_op jit(solution)/shard_map/all_to_all | solution.py:113
  27.5 0.5 iota_compare_fusion
  28.0 0.1 mul.540
  28.1 0.8 mul.541
  29.0 0.7 exponential_multiply_fusion
  29.7 2.0 %convolution_select_fusion = f32[4,256,256]{2,1,0:T(8,128)S(1)} fusion(pred[256,256]{1,0:T(8,128)(4,1)} %subtract_compare_fusion, f32[4,16]{1,0:T(4,128)} %copy-done.5, f32[4,16]{1,0:T(4,128)S(1)} %neg.12, f32[4,16]{1,0:T(4,128)S(1)} %get-tuple-element.5), kind=kOutput, calls=%fused_computation.28 | convolution fusion | flops 50642944 | bytes 1114880 | tf_op jit(solution)/shard_map/grm,gms->grs/dot_general | solution.py:57
  31.7 7.0 %all-to-all-done = bf16[32,32,256]{2,0,1:T(8,128)(2,1)S(1)} async-done(((bf16[32,32,256]{2,0,1:T(8,128)(2,1)}), bf16[32,32,256]{2,0,1:T(8,128)(2,1)S(1)}, u32[]{:S(2)}, u32[]{:S(2)}) %all-to-all-start) | async-done | bytes 524320 | tf_op jit(solution)/shard_map/all_to_all | solution.py:113
  38.7 0.8 copy-done.2
  39.5 1.1 %copy.49 = bf16[4,8,32,256]{3,2,1,0:T(8,128)(2,1)S(1)} copy(bf16[4,8,32,256]{3,2,0,1:T(8,128)(2,1)} %bitcast.95) | data formatting | bytes 1048576 | tf_op jit(solution)/shard_map/transpose | solution.py:115
  40.6 1.4 %reshape_reshape.3 = bf16[4,256,4,64]{3,2,1,0:T(4,128)(2,1)} reshape(bf16[4,8,32,256]{3,2,1,0:T(8,128)(2,1)S(1)} %copy.49) | data formatting | bytes 1048576 | tf_op jit(solution)/shard_map/reshape;reshape | solution.py:60
  42.0 1.6 %copy.50 = bf16[4,256,4,64]{1,3,0,2:T(8,128)(2,1)S(1)} copy(bf16[4,256,4,64]{3,2,1,0:T(4,128)(2,1)} %reshape_reshape.3) | data formatting | bytes 1048576 | tf_op jit(solution)/shard_map/reshape;reshape | solution.py:60
  43.6 0.3 fusion.18
  44.0 1.3 %convolution_add_fusion.1 = f32[4,4,64,256]{3,2,1,0:T(8,128)} fusion(f32[4,4,64,256]{3,2,1,0:T(8,128)S(1)} %fusion.18, bf16[4,256,4,64]{1,3,0,2:T(8,128)(2,1)S(1)} %copy.50, f32[4,256,256]{2,1,0:T(8,128)S(1)} %convolution_select_fusion), kind=kOutput, calls=%fused_computation.26 | convolution fusion | flops 135528448 | bytes 3670016 | tf_op jit(solution)/shard_map/grs,bsgc->brgc/dot_general | solution.py:45
  45.3 0.3 fusion.45
  45.6 0.4 convolution_add_fusion.2
  46.0 0.7 copy-done.3
  46.6 0.3 fusion.30
  47.0 0.1 broadcast_in_dim.38
  47.1 0.7 broadcast_in_dim.43
  47.8 8.2 %all-to-all-start.1 = ((f32[8,1,4096]{2,1,0:T(1,128)}), f32[8,1,4096]{2,1,0:T(1,128)S(1)}, u32[]{:S(2)}, u32[]{:S(2)}) async-start(f32[8,1,4096]{2,1,0:T(1,128)} %broadcast_in_dim.43), calls=%async_computation.1 | async-start | bytes 262144 | tf_op jit(solution)/shard_map/all_to_all | solution.py:72
  56.0 1.3 %fusion.26 = f32[4,16,4,64]{3,2,1,0:T(4,128)S(1)} fusion(f32[4,16,4,64]{3,1,2,0:T(8,128)} %copy-done.3, f32[4,4]{1,0:T(4,128)} %convert_multiply_fusion, f32[4,16]{1,0:T(4,128)S(1)} %neg.12, pred[4,4]{1,0:T(4,128)(4,1)} %iota_compare_fusion), kind=kOutput, calls=%fused_computation.60 | convolution fusion | flops 395264 | bytes 131408 | tf_op jit(solution)/shard_map/gmab,gmbc->gmac/dot_general | solution.py:88
  57.3 7.0 %all-to-all-done.1 = f32[8,1,4096]{2,1,0:T(1,128)S(1)} async-done(((f32[8,1,4096]{2,1,0:T(1,128)}), f32[8,1,4096]{2,1,0:T(1,128)S(1)}, u32[]{:S(2)}, u32[]{:S(2)}) %all-to-all-start.1) | async-done | bytes 131104 | tf_op jit(solution)/shard_map/all_to_all | solution.py:72
  64.3 1.1 %multiply_reduce_fusion = f32[4096]{0:T(1024)S(1)} fusion(f32[8,1,4096]{2,1,0:T(1,128)} %mul.541, f32[8,1,4096]{2,1,0:T(1,128)S(1)} %all-to-all-done.1), kind=kLoop, calls=%fused_computation.59 | loop fusion | flops 61440 | bytes 278528 | tf_op jit(solution)/shard_map/reduce_sum | solution.py:82
  65.4 0.1 reshape.228
  65.4 1.5 %convolution_bitcast_fusion = f32[4,256,4,64]{1,3,0,2:T(8,128)S(1)} fusion(f32[4,4,16]{2,1,0:T(4,128)S(1)} %multiply_exponential_fusion.2, f32[4,256,16]{1,2,0:T(8,128)} %exponential_multiply_fusion, f32[4,16,64,1]{2,1,0,3:T(8,128)S(1)} %reshape.228), kind=kOutput, calls=%fused_computation.23 | convolution fusion | flops 25231360 | bytes 1131520 | tf_op jit(solution)/shard_map/gbrm,gmc->brgc/dot_general | solution.py:93
  66.9 1.5 %fusion.2 = bf16[4,256,4,64]{1,3,0,2:T(8,128)(2,1)} fusion(f32[4,256,4,64]{1,3,0,2:T(8,128)S(1)} %convolution_bitcast_fusion, f32[4,4,64,256]{3,2,1,0:T(8,128)S(1)} %copy-done.1, f32[4,16,4,64]{3,2,1,0:T(4,128)S(1)} %fusion.26, f32[4,16]{1,0:T(4,128)S(1)} %neg.12, f32[4,16]{1,0:T(4,128)S(1)} %get-tuple-element.5), kind=kOutput, calls=%fused_computation.29 | convolution fusion | flops 25985024 | bytes 2687488 | tf_op jit(solution)/shard_map/grm,gmbc->brgc/dot_general | solution.py:89
  68.5 1.6 %copy.56 = bf16[4,256,4,64]{3,2,1,0:T(4,128)(2,1)S(1)} copy(bf16[4,256,4,64]{1,3,0,2:T(8,128)(2,1)} %fusion.2) | data formatting | bytes 1048576 | tf_op jit(solution)/shard_map/convert_element_type | solution.py:94
  70.0 0.7 convert_element_type.164
  70.7 0.8 copy.57
  71.5 5.5 %all-to-all-start.2 = ((bf16[32,32,256]{2,1,0:T(8,128)(2,1)}), bf16[32,32,256]{2,1,0:T(8,128)(2,1)S(1)}, u32[]{:S(2)}, u32[]{:S(2)}) async-start(bf16[32,32,256]{2,1,0:T(8,128)(2,1)} %bitcast.30), calls=%async_computation.2 | async-start | bytes 1048576 | tf_op jit(solution)/shard_map/all_to_all | solution.py:125
  77.1 2.4 %fusion.58 = (f32[1,1,8192]{2,1,0:T(1,128)S(1)}, f32[1,1,8192]{2,1,0:T(1,128)S(1)}, f32[1,1,8192]{2,1,0:T(1,128)S(1)}, f32[1,1,8192]{2,1,0:T(1,128)S(1)}, f32[1,...) fusion(f32[3,7,8192]{2,1,0:T(8,128)} %param.6), kind=kLoop, calls=%fused_computation.123 | loop fusion | bytes 458752 | tf_op jit(solution)/shard_map/slice | solution.py:34
  79.5 8.8 %all-to-all-done.2 = bf16[32,32,256]{2,1,0:T(8,128)(2,1)S(1)} async-done(((bf16[32,32,256]{2,1,0:T(8,128)(2,1)}), bf16[32,32,256]{2,1,0:T(8,128)(2,1)S(1)}, u32[]{:S(2)}, u32[]{:S(2)}) %all-to-all-start.2) | async-done | bytes 524320 | tf_op jit(solution)/shard_map/all_to_all | solution.py:125
  88.3 0.1 convert_bitcast_fusion
  88.4 0.1 copy.74
  88.5 2.1 %fusion.9 = bf16[32,8192]{1,0:T(8,128)(2,1)} fusion(f32[32,8192]{1,0:T(8,128)S(1)} %bitcast.92, bf16[32,3,8192]{2,0,1:T(8,128)(2,1)S(1)} %copy-done, bf16[6,3,8192]{2,0,1:T(8,128)(2,1)S(1)} %collective-permute-done, f32[32]{0:T(128)S(1)} %copy-done.9, f32[8192]{0:T(1024)S(1)} %bitcast.99, f32[32]{0:T(128)S(1)} %copy-done.11, f32[8192]{0:T(1024)S(1)} %bitcast.100, ...), kind=kLoop, calls=%fused_computation.40 | loop fusion | flops 12320768 | bytes 4296192 | tf_op jit(solution)/shard_map/convert_element_type | solution.py:127
  (45 shorter events, 0.1 us)
Async XLA Ops:
  0.0 16.8 %copy-start = (bf16[32,3,8192]{2,0,1:T(8,128)(2,1)S(1)}, bf16[32,3,8192]{2,0,1:T(8,128)(2,1)}, u32[]{:S(2)}) copy-start(bf16[32,3,8192]{2,0,1:T(8,128)(2,1)} %param.5) | copy-start | bytes 4718596
  1.2 15.5 %collective-permute-start = (bf16[6,3,8192]{2,0,1:T(8,128)(2,1)S(1)}, bf16[6,3,8192]{2,0,1:T(8,128)(2,1)S(1)}, u32[]{:S(2)}, u32[]{:S(2)}) collective-permute-start(bf16[6,3,8192]{2,0,1:T(8,128)(2,1)S(1)} %slice.189), channel_id=1, source_target_pairs={{0,1},{1,2},{2,3},{3,4},{4,5},{5,6},{6,7},{7,8},{8,9},{9,10},{10,1... | collective-permute-start | bytes 884744 | tf_op jit(solution)/shard_map/ppermute | solution.py:13
  8.2 11.2 %copy-start.19 = (f32[32]{0:T(128)}, f32[32]{0:T(128)S(1)}, u32[]{:S(2)}) copy-start(f32[32]{0:T(128)S(1)} %compare_convert_fusion) | copy-start | bytes 388
  8.5 10.9 %copy-start.6 = (f32[32]{0:T(128)}, f32[32]{0:T(128)S(1)}, u32[]{:S(2)}) copy-start(f32[32]{0:T(128)S(1)} %get-tuple-element.21) | copy-start | bytes 388
  8.5 10.9 %copy-start.8 = (f32[32]{0:T(128)}, f32[32]{0:T(128)S(1)}, u32[]{:S(2)}) copy-start(f32[32]{0:T(128)S(1)} %get-tuple-element.22) | copy-start | bytes 388
  8.5 10.9 %copy-start.10 = (f32[32]{0:T(128)}, f32[32]{0:T(128)S(1)}, u32[]{:S(2)}) copy-start(f32[32]{0:T(128)S(1)} %get-tuple-element.23) | copy-start | bytes 388
  8.5 10.9 %copy-start.12 = (f32[32]{0:T(128)}, f32[32]{0:T(128)S(1)}, u32[]{:S(2)}) copy-start(f32[32]{0:T(128)S(1)} %get-tuple-element.24) | copy-start | bytes 388
  8.5 10.9 %copy-start.14 = (f32[32]{0:T(128)}, f32[32]{0:T(128)S(1)}, u32[]{:S(2)}) copy-start(f32[32]{0:T(128)S(1)} %get-tuple-element.25) | copy-start | bytes 388
  8.5 10.9 %copy-start.16 = (f32[32]{0:T(128)}, f32[32]{0:T(128)S(1)}, u32[]{:S(2)}) copy-start(f32[32]{0:T(128)S(1)} %get-tuple-element.26) | copy-start | bytes 388
  12.7 0.9 %copy-start.5 = (f32[4,16]{1,0:T(4,128)}, f32[4,16]{1,0:T(4,128)S(1)}, u32[]{:S(2)}) copy-start(f32[4,16]{1,0:T(4,128)S(1)} %get-tuple-element.6) | copy-start | bytes 772
  20.8 17.9 %all-to-all-start = ((bf16[32,32,256]{2,0,1:T(8,128)(2,1)}), bf16[32,32,256]{2,0,1:T(8,128)(2,1)S(1)}, u32[]{:S(2)}, u32[]{:S(2)}) async-start(bf16[32,32,256]{2,0,1:T(8,128)(2,1)} %copy.48), calls=%async_computation | async-start | bytes 1048576 | tf_op jit(solution)/shard_map/all_to_all | solution.py:113
  38.7 0.8 copy-start.2
  43.9 1.4 %copy-start.18 = (f32[256]{0:T(256)S(1)}, f32[256]{0:T(256)}, u32[]{:S(2)}) copy-start(f32[256]{0:T(256)} %iota_subtract_fusion) | copy-start | bytes 3076
  43.9 2.7 %copy-start.4 = (f32[4,16,4]{2,1,0:T(8,128)S(1)}, f32[4,16,4]{2,1,0:T(8,128)}, u32[]{:S(2)}) copy-start(f32[4,16,4]{2,1,0:T(8,128)} %multiply_exponential_fusion.1) | copy-start | bytes 3076
  45.3 21.6 %copy-start.1 = (f32[4,4,64,256]{3,2,1,0:T(8,128)S(1)}, f32[4,4,64,256]{3,2,1,0:T(8,128)}, u32[]{:S(2)}) copy-start(f32[4,4,64,256]{3,2,1,0:T(8,128)} %convolution_add_fusion.1) | copy-start | bytes 3145732
  46.0 0.7 copy-start.3
  47.8 16.5 %all-to-all-start.1 = ((f32[8,1,4096]{2,1,0:T(1,128)}), f32[8,1,4096]{2,1,0:T(1,128)S(1)}, u32[]{:S(2)}, u32[]{:S(2)}) async-start(f32[8,1,4096]{2,1,0:T(1,128)} %broadcast_in_dim.43), calls=%async_computation.1 | async-start | bytes 262144 | tf_op jit(solution)/shard_map/all_to_all | solution.py:72
  71.5 16.7 %all-to-all-start.2 = ((bf16[32,32,256]{2,1,0:T(8,128)(2,1)}), bf16[32,32,256]{2,1,0:T(8,128)(2,1)S(1)}, u32[]{:S(2)}, u32[]{:S(2)}) async-start(bf16[32,32,256]{2,1,0:T(8,128)(2,1)} %bitcast.30), calls=%async_computation.2 | async-start | bytes 1048576 | tf_op jit(solution)/shard_map/all_to_all | solution.py:125
  77.0 11.5 %copy-start.7 = (f32[32]{0:T(128)S(1)}, f32[32]{0:T(128)}, u32[]{:S(2)}) copy-start(f32[32]{0:T(128)} %copy-done.6) | copy-start | bytes 388
  77.0 11.5 %copy-start.9 = (f32[32]{0:T(128)S(1)}, f32[32]{0:T(128)}, u32[]{:S(2)}) copy-start(f32[32]{0:T(128)} %copy-done.8) | copy-start | bytes 388
  77.0 11.5 %copy-start.11 = (f32[32]{0:T(128)S(1)}, f32[32]{0:T(128)}, u32[]{:S(2)}) copy-start(f32[32]{0:T(128)} %copy-done.10) | copy-start | bytes 388
  77.0 11.5 %copy-start.13 = (f32[32]{0:T(128)S(1)}, f32[32]{0:T(128)}, u32[]{:S(2)}) copy-start(f32[32]{0:T(128)} %copy-done.12) | copy-start | bytes 388
  77.0 11.5 %copy-start.15 = (f32[32]{0:T(128)S(1)}, f32[32]{0:T(128)}, u32[]{:S(2)}) copy-start(f32[32]{0:T(128)} %copy-done.14) | copy-start | bytes 388
  77.1 11.5 %copy-start.17 = (f32[32]{0:T(128)S(1)}, f32[32]{0:T(128)}, u32[]{:S(2)}) copy-start(f32[32]{0:T(128)} %copy-done.16) | copy-start | bytes 388
  77.1 11.5 %copy-start.20 = (f32[32]{0:T(128)S(1)}, f32[32]{0:T(128)}, u32[]{:S(2)}) copy-start(f32[32]{0:T(128)} %copy-done.19) | copy-start | bytes 388

commit v15 on v14

--- a/solution.py
+++ b/solution.py
@@ -111,6 +111,8 @@
 
     swap_axis = ("mp", "zi")
     gathered = lax.all_to_all(product, swap_axis, split_axis=1, concat_axis=0, tiled=True)
+    query_part = short_convolution(padded[:, :1], conv_weight[:1], padded_document_ids, padded_pos, rows)[:, 0]
+    gathered, query_part = lax.optimization_barrier((gathered, query_part))
     width = gathered.shape[1]
     gathered = gathered.reshape(mp_size, inner_size, rows, width).transpose(1, 0, 2, 3)
     gathered = gathered.reshape(inner_size * mp_size * rows, width)
@@ -123,7 +125,6 @@
     filtered = filtered.reshape(inner_size, mp_size, rows, width).transpose(1, 0, 2, 3)
     filtered = filtered.reshape(inner_size * mp_size * rows, width)
     filtered = lax.all_to_all(filtered, swap_axis, split_axis=0, concat_axis=1, tiled=True)
-    query_part = short_convolution(padded[:, :1], conv_weight[:1], padded_document_ids, padded_pos, rows)[:, 0]
     return (query_part * filtered.astype(jnp.float32)).astype(jnp.bfloat16)
 
 

time: 91.3 us -> 90.2 us (0.988)
  blocking collectives: 0 us -> 16.5 us
  waiting for transfers between devices: 24.9 us -> 16.1 us
  starting transfers between devices: 24.4 us -> 20 us
  matrix products: 9.04 us -> 5.53 us
  local copies, waits for them, and re-layouts: 19.9 us -> 16.8 us
  other arithmetic: 12 us -> 14.3 us
    all_to_all x0 -> x1, blocking collectives: none -> 16.5 us  [shards(): lax.all_to_all(filtered, swap_axis, split_axis=0, concat_axis=1, tiled=True)]
    all_to_all x1 -> x0, waiting for transfers between devices: 8.76 us -> none  [shards(): lax.all_to_all(filtered, swap_axis, split_axis=0, concat_axis=1, tiled=True)]
    all_to_all x1 -> x0, starting transfers between devices: 5.47 us -> none  [shards(): lax.all_to_all(filtered, swap_axis, split_axis=0, concat_axis=1, tiled=True)]
    squeeze x0 -> x1, other arithmetic: none -> 3.05 us  [shards(): short_convolution(padded[:, :1], conv_weight[:1], padded_document_ids, pa...]
    ppermute x1, waiting for transfers between devices: 2.11 us -> 0.01 us  [shifted(): return lax.ppermute(block, axis, route)]
    another operation x2, local copies, waits for them, and re-layouts: 2.99 us -> 1.04 us  [long_filter(): inputs = product.reshape(block_count, block_len, group_count, group_width)]
    unnamed x47 -> x25, local copies, waits for them, and re-layouts: 2.02 us -> 3.72 us
    convert_element_type x1, other arithmetic: 2.11 us -> 0.89 us  [shards(): return (query_part * filtered.astype(jnp.float32)).astype(jnp.bfloat16)]
  transfers between devices with their start and end apart: 4 -> 3, of which waited for: 4 -> 2; matrix products, arithmetic and copies ran while one was open for 19% -> 24% of each run, Pallas kernels for 0% -> 0%
where the time goes in v15:
time: 90.2 us; the launch traced here: 89.6 us
  starting transfers between devices  20 us (22%)
  local copies, waits for them, and re-layouts  16.8 us (19%)
  blocking collectives  16.5 us (18%)
  waiting for transfers between devices  16.1 us (18%)
  other arithmetic  14.3 us (16%)
  matrix products  5.53 us (6%)
    all_to_all x1, blocking collectives, shards(): lax.all_to_all(filtered, swap_axis, split_axis=0, concat_axis=1, tiled=True)  16.5 us
    all_to_all x1, waiting for transfers between devices, shards(): lax.all_to_all(product, swap_axis, split_axis=1, concat_axis=0, tiled=True)  8.2 us
    all_to_all x1, starting transfers between devices, long_filter(): lax.all_to_all(sent, outer_axis, split_axis=0, concat_axis=0, tiled=True)  8.19 us
    all_to_all x1, waiting for transfers between devices, long_filter(): lax.all_to_all(sent, outer_axis, split_axis=0, concat_axis=0, tiled=True)  7.9 us
    all_to_all x1, starting transfers between devices, shards(): lax.all_to_all(product, swap_axis, split_axis=1, concat_axis=0, tiled=True)  7.74 us
    slice x2, local copies, waits for them, and re-layouts, short_convolution(): conv_weight[:, position_shift, :][None] * earlier  6.49 us
    ppermute x1, starting transfers between devices, shifted(): return lax.ppermute(block, axis, route)  4.02 us
    unnamed x25, local copies, waits for them, and re-layouts  3.72 us
  transfers between devices with their start and end apart: 3, of which 2 were waited for; matrix products, arithmetic and copies ran while one was open for 24% of the time, Pallas kernels for 0%

profile of v15, /device:TPU:1, one launch (start us, length us, event | category | flops | bytes accessed | tf_op | source)
XLA Modules:
  0.0 89.6 jit_solution(6231326803795282832)
XLA Ops:
  0.0 1.1 %slice.189 = bf16[6,3,8192]{2,0,1:T(8,128)(2,1)S(1)} slice(bf16[32,3,8192]{2,0,1:T(8,128)(2,1)} %param.5), slice={[26:32], [0:3], [0:8192]} | slice | bytes 589824 | tf_op jit(solution)/shard_map/slice | solution.py:104
  1.1 4.0 %collective-permute-start = (bf16[6,3,8192]{2,0,1:T(8,128)(2,1)S(1)}, bf16[6,3,8192]{2,0,1:T(8,128)(2,1)S(1)}, u32[]{:S(2)}, u32[]{:S(2)}) collective-permute-start(bf16[6,3,8192]{2,0,1:T(8,128)(2,1)S(1)} %slice.189), channel_id=1, source_target_pairs={{0,1},{1,2},{2,3},{3,4},{4,5},{5,6},{6,7},{7,8},{8,9},{9,10},{10,1... | collective-permute-start | bytes 884744 | tf_op jit(solution)/shard_map/ppermute | solution.py:13
  5.1 0.0 copy-start
  5.2 3.4 %fusion.58 = (f32[2,1,8192]{2,1,0:T(1,128)S(1)}, f32[2,1,8192]{2,1,0:T(1,128)S(1)}, f32[2,1,8192]{2,1,0:T(1,128)S(1)}, f32[2,1,8192]{2,1,0:T(1,128)S(1)}, f32[2,...) fusion(f32[3,7,8192]{2,1,0:T(8,128)} %param.6), kind=kLoop, calls=%fused_computation.125 | loop fusion | bytes 917504 | tf_op jit(solution)/shard_map/slice | solution.py:34
  8.6 3.1 %fusion.57 = (f32[1,1,8192]{2,1,0:T(1,128)}, f32[1,1,8192]{2,1,0:T(1,128)}, f32[1,1,8192]{2,1,0:T(1,128)}, f32[1,1,8192]{2,1,0:T(1,128)}, f32[1,1,8192]{2,1,0:T(...) fusion(f32[3,7,8192]{2,1,0:T(8,128)} %param.6), kind=kLoop, calls=%fused_computation.124 | loop fusion | bytes 458752 | tf_op jit(solution)/shard_map/slice | solution.py:34
  11.7 0.7 subtract_compare_fusion
  12.3 0.6 iota_subtract_fusion
  13.0 0.0 copy-done.8
  13.0 0.1 copy.49
  13.1 0.1 reduce-window.9
  13.2 0.1 reduce.3
  13.3 0.6 compare_convert_fusion
  13.9 0.2 convert_reduce_fusion
  14.1 0.7 and_convert_fusion.5
  14.8 0.7 sqrt_multiply_fusion
  15.5 0.7 multiply_exponential_fusion.1
  16.2 0.0 copy-done.5
  16.2 0.7 exponential_multiply_fusion
  16.9 0.1 multiply_exponential_fusion.2
  17.0 0.7 convert_multiply_fusion
  17.6 0.7 copy_bitcast_fusion.1
  18.4 0.8 copy_bitcast_fusion.3
  19.1 0.8 copy_bitcast_fusion.5
  19.9 0.1 exponential_select_fusion
  20.0 0.5 iota_compare_fusion
  20.5 0.1 copy.93
  20.5 0.1 mul.540
  20.7 0.8 mul.541
  21.5 2.0 %convolution_select_fusion = f32[4,256,256]{2,1,0:T(8,128)S(1)} fusion(pred[256,256]{1,0:T(8,128)(4,1)} %subtract_compare_fusion, f32[4,16]{1,0:T(4,128)} %copy-done.5, f32[4,16]{1,0:T(4,128)S(1)} %neg.12, f32[4,16]{1,0:T(4,128)S(1)} %get-tuple-element.9), kind=kOutput, calls=%fused_computation.28 | convolution fusion | flops 50642944 | bytes 1114880 | tf_op jit(solution)/shard_map/grm,gms->grs/dot_general | solution.py:57
  23.6 0.0 collective-permute-done
  23.6 0.0 copy-done
  23.6 3.6 %multiply_add_fusion = f32[32,2,8192]{2,0,1:T(8,128)S(1)} fusion(bf16[32,3,8192]{2,0,1:T(8,128)(2,1)S(1)} %copy-done, bf16[6,3,8192]{2,0,1:T(8,128)(2,1)S(1)} %collective-permute-done, f32[32]{0:T(128)} %get-tuple-element.26, f32[2,8192]{1,0:T(2,128)S(1)} %get-tuple-element.31, f32[32]{0:T(128)} %get-tuple-element.27, f32[2,8192]{1,0:T(2,128)} %get-tuple-element.32, ...), kind=kLoop, calls=%fused_computation.11 | loop fusion | flops 23592960 | bytes 5571456 | tf_op jit(solution)/shard_map/add | solution.py:33
  27.1 0.1 fusion.9
  27.2 0.1 copy.77
  27.4 1.1 %copy.50 = bf16[32,32,256]{2,0,1:T(8,128)(2,1)} copy(bf16[32,32,256]{2,1,0:T(8,128)(2,1)S(1)} %bitcast.97) | data formatting | bytes 1048576 | tf_op jit(solution)/shard_map/convert_element_type | solution.py:110
  28.4 7.7 %all-to-all-start = ((bf16[32,32,256]{2,0,1:T(8,128)(2,1)}), bf16[32,32,256]{2,0,1:T(8,128)(2,1)S(1)}, u32[]{:S(2)}, u32[]{:S(2)}) async-start(bf16[32,32,256]{2,0,1:T(8,128)(2,1)} %copy.50), calls=%async_computation | async-start | bytes 1048576 | tf_op jit(solution)/shard_map/all_to_all | solution.py:113
  36.2 3.1 %add_bitcast_fusion = f32[32,8192]{1,0:T(8,128)} fusion(bf16[32,3,8192]{2,0,1:T(8,128)(2,1)S(1)} %copy-done, bf16[6,3,8192]{2,0,1:T(8,128)(2,1)S(1)} %collective-permute-done, f32[32]{0:T(128)} %get-tuple-element.26, f32[8192]{0:T(1024)} %bitcast.105, f32[32]{0:T(128)} %get-tuple-element.27, f32[8192]{0:T(1024)} %bitcast.106, f32[32]{0:T(128)} %get-tuple-element.28, ...), kind=kLoop, calls=%fused_computation.42 | loop fusion | flops 11796480 | bytes 3769216 | tf_op jit(solution)/shard_map/squeeze | solution.py:114
  39.2 8.2 %all-to-all-done = bf16[32,32,256]{2,0,1:T(8,128)(2,1)S(1)} async-done(((bf16[32,32,256]{2,0,1:T(8,128)(2,1)}), bf16[32,32,256]{2,0,1:T(8,128)(2,1)S(1)}, u32[]{:S(2)}, u32[]{:S(2)}) %all-to-all-start) | async-done | bytes 524320 | tf_op jit(solution)/shard_map/all_to_all | solution.py:113
  47.5 0.4 reshape_reshape.3
  47.9 0.6 copy.52
  48.5 0.3 fusion.17
  48.9 0.3 convolution_add_fusion.1
  49.3 0.3 copy-done.6
  49.6 0.3 fusion.44
  49.9 0.4 convolution_add_fusion.2
  50.2 0.4 fusion.29
  50.6 0.1 broadcast_in_dim.38
  50.7 0.7 broadcast_in_dim.39
  51.4 8.2 %all-to-all-start.1 = ((f32[8,1,4096]{2,1,0:T(1,128)}), f32[8,1,4096]{2,1,0:T(1,128)S(1)}, u32[]{:S(2)}, u32[]{:S(2)}) async-start(f32[8,1,4096]{2,1,0:T(1,128)} %broadcast_in_dim.39), calls=%async_computation.1 | async-start | bytes 262144 | tf_op jit(solution)/shard_map/all_to_all | solution.py:72
  59.6 0.0 copy-done.7
  59.6 0.4 fusion.25
  60.0 7.9 %all-to-all-done.1 = f32[8,1,4096]{2,1,0:T(1,128)S(1)} async-done(((f32[8,1,4096]{2,1,0:T(1,128)}), f32[8,1,4096]{2,1,0:T(1,128)S(1)}, u32[]{:S(2)}, u32[]{:S(2)}) %all-to-all-start.1) | async-done | bytes 131104 | tf_op jit(solution)/shard_map/all_to_all | solution.py:72
  67.9 0.2 multiply_reduce_fusion
  68.1 0.1 reshape.213
  68.2 0.0 copy-done.3
  68.2 0.6 convolution_bitcast_fusion
  68.8 0.7 fusion.2
  69.6 0.7 copy.58
  70.2 0.7 convert_element_type.164
  70.9 16.5 %all_to_all.35 = bf16[32,32,256]{2,1,0:T(8,128)(2,1)S(1)} all-to-all(bf16[32,32,256]{2,1,0:T(8,128)(2,1)S(1)} %bitcast.98), channel_id=1, replica_groups=mesh['zo'=8,'zi'=4,'mp'=8] {'mp','zi'}, dimensions={0} | all-to-all | bytes 1048576 | tf_op jit(solution)/shard_map/all_to_all | solution.py:127
  87.5 0.1 convert_bitcast_fusion
  87.6 0.1 copy.76
  87.7 1.0 %copy-done.1 = f32[32,8192]{1,0:T(8,128)S(1)} copy-done((f32[32,8192]{1,0:T(8,128)S(1)}, f32[32,8192]{1,0:T(8,128)}, u32[]{:S(2)}) %copy-start.1) | copy-done | bytes 1048600
  88.7 0.9 multiply_convert_fusion
  (23 shorter events, 0.1 us)
Async XLA Ops:
  0.0 13.0 %copy-start.8 = (s32[64]{0:T(128)S(1)}, s32[64]{0:T(128)}, u32[]{:S(2)}) copy-start(s32[64]{0:T(128)} %param.9) | copy-start | bytes 772
  1.1 22.4 %collective-permute-start = (bf16[6,3,8192]{2,0,1:T(8,128)(2,1)S(1)}, bf16[6,3,8192]{2,0,1:T(8,128)(2,1)S(1)}, u32[]{:S(2)}, u32[]{:S(2)}) collective-permute-start(bf16[6,3,8192]{2,0,1:T(8,128)(2,1)S(1)} %slice.189), channel_id=1, source_target_pairs={{0,1},{1,2},{2,3},{3,4},{4,5},{5,6},{6,7},{7,8},{8,9},{9,10},{10,1... | collective-permute-start | bytes 884744 | tf_op jit(solution)/shard_map/ppermute | solution.py:13
  5.1 18.4 %copy-start = (bf16[32,3,8192]{2,0,1:T(8,128)(2,1)S(1)}, bf16[32,3,8192]{2,0,1:T(8,128)(2,1)}, u32[]{:S(2)}) copy-start(bf16[32,3,8192]{2,0,1:T(8,128)(2,1)} %param.5) | copy-start | bytes 4718596
  15.5 0.7 copy-start.5
  28.4 19.0 %all-to-all-start = ((bf16[32,32,256]{2,0,1:T(8,128)(2,1)}), bf16[32,32,256]{2,0,1:T(8,128)(2,1)S(1)}, u32[]{:S(2)}, u32[]{:S(2)}) async-start(bf16[32,32,256]{2,0,1:T(8,128)(2,1)} %copy.50), calls=%async_computation | async-start | bytes 1048576 | tf_op jit(solution)/shard_map/all_to_all | solution.py:113
  48.9 0.7 copy-start.6
  48.9 1.3 %copy-start.4 = (f32[4,16,4]{2,1,0:T(8,128)S(1)}, f32[4,16,4]{2,1,0:T(8,128)}, u32[]{:S(2)}) copy-start(f32[4,16,4]{2,1,0:T(8,128)} %multiply_exponential_fusion.1) | copy-start | bytes 3076
  48.9 10.7 %copy-start.7 = (f32[4,4]{1,0:T(4,128)S(1)}, f32[4,4]{1,0:T(4,128)}, u32[]{:S(2)}) copy-start(f32[4,4]{1,0:T(4,128)} %convert_multiply_fusion) | copy-start | bytes 196
  48.9 10.7 %copy-start.9 = (pred[4,4]{1,0:T(4,128)(4,1)S(1)}, pred[4,4]{1,0:T(4,128)(4,1)}, u32[]{:S(2)}) copy-start(pred[4,4]{1,0:T(4,128)(4,1)} %iota_compare_fusion) | copy-start | bytes 52
  49.6 18.4 %copy-start.2 = (f32[8,1,4096]{2,1,0:T(1,128)S(1)}, f32[8,1,4096]{2,1,0:T(1,128)}, u32[]{:S(2)}) copy-start(f32[8,1,4096]{2,1,0:T(1,128)} %mul.541) | copy-start | bytes 393220
  49.6 18.6 %copy-start.3 = (f32[4,256,16]{1,2,0:T(8,128)S(1)}, f32[4,256,16]{1,2,0:T(8,128)}, u32[]{:S(2)}) copy-start(f32[4,256,16]{1,2,0:T(8,128)} %exponential_multiply_fusion) | copy-start | bytes 196612
  51.4 16.5 %all-to-all-start.1 = ((f32[8,1,4096]{2,1,0:T(1,128)}), f32[8,1,4096]{2,1,0:T(1,128)S(1)}, u32[]{:S(2)}, u32[]{:S(2)}) async-start(f32[8,1,4096]{2,1,0:T(1,128)} %broadcast_in_dim.39), calls=%async_computation.1 | async-start | bytes 262144 | tf_op jit(solution)/shard_map/all_to_all | solution.py:72
  87.4 1.2 %copy-start.1 = (f32[32,8192]{1,0:T(8,128)S(1)}, f32[32,8192]{1,0:T(8,128)}, u32[]{:S(2)}) copy-start(f32[32,8192]{1,0:T(8,128)} %add_bitcast_fusion) | copy-start | bytes 3145732

commit v16 on v13

--- a/solution.py
+++ b/solution.py
@@ -64,8 +64,9 @@
     block_state = split_product("gms,bsgc->gmbc", end_weight, inputs)
 
     blocks = jnp.arange(block_count, dtype=jnp.float32)
-    to_end = jnp.exp(-decays[:, :, None] * (float(block_len) * (block_count - 1 - blocks))[None, None, :])
-    run_state = jnp.einsum("gmb,gmbc->gmc", to_end, block_state, precision=HIGH)
+    run_offsets = jnp.arange(positions, dtype=jnp.float32).reshape(block_count, block_len)
+    run_weight = jnp.exp(-decays[:, :, None, None] * (float(positions) - run_offsets)[None, None])
+    run_state = split_product("gmbs,bsgc->gmc", run_weight, inputs)
     count = lax.axis_size(outer_axis)
     flat = run_state.reshape(1, -1)
     sent = jnp.broadcast_to(flat, (count, flat.shape[1]))
@@ -97,7 +98,6 @@
 def shards(proj, conv_weight, residues, decays, doc_lengths):
     kernel_len = conv_weight.shape[1]
     rows = proj.shape[0]
-    outer_size = lax.axis_size("zo")
     inner_size = lax.axis_size("zi")
     mp_size = lax.axis_size("mp")
     lin_axis = ("zo", "zi", "mp")

time: 84.2 us -> 84.5 us (level)
  no operation moved by 1% of the time
where the time goes in v16:
time: 84.5 us; the launch traced here: 83.9 us
  waiting for transfers between devices  21.2 us (25%)
  starting transfers between devices  18.9 us (22%)
  blocking collectives  16.5 us (20%)
  local copies, waits for them, and re-layouts  13.2 us (16%)
  other arithmetic  8.8 us (10%)
  matrix products  4.95 us (6%)
    all_to_all x1, blocking collectives, shards(): lax.all_to_all(filtered, swap_axis, split_axis=0, concat_axis=1, tiled=True)  16.5 us
    all_to_all x1, waiting for transfers between devices, shards(): lax.all_to_all(product, swap_axis, split_axis=1, concat_axis=0, tiled=True)  9.64 us
    all_to_all x1, starting transfers between devices, long_filter(): lax.all_to_all(sent, outer_axis, split_axis=0, concat_axis=0, tiled=True)  8.18 us
    all_to_all x1, waiting for transfers between devices, long_filter(): lax.all_to_all(sent, outer_axis, split_axis=0, concat_axis=0, tiled=True)  7.89 us
    all_to_all x1, starting transfers between devices, shards(): lax.all_to_all(product, swap_axis, split_axis=1, concat_axis=0, tiled=True)  6.68 us
    slice x1, local copies, waits for them, and re-layouts, short_convolution(): conv_weight[:, position_shift, :][None] * earlier  4.22 us
    ppermute x1, starting transfers between devices, shifted(): return lax.ppermute(block, axis, route)  4.02 us
    add x1, other arithmetic, short_convolution(): result + conv_weight[:, position_shift, :][None] * earlier * keep_mask.as...  3.98 us
  transfers between devices with their start and end apart: 3, of which 3 were waited for; matrix products, arithmetic and copies ran while one was open for 12% of the time, Pallas kernels for 0%

profile of v16, /device:TPU:1, one launch (start us, length us, event | category | flops | bytes accessed | tf_op | source)
XLA Modules:
  0.0 83.9 jit_solution(4847829151048968735)
XLA Ops:
  0.0 0.0 copy-start.1
  0.0 1.2 %slice.97 = bf16[6,3,8192]{2,0,1:T(8,128)(2,1)S(1)} slice(bf16[32,3,8192]{2,0,1:T(8,128)(2,1)} %param.5), slice={[26:32], [0:3], [0:8192]} | slice | bytes 589824 | tf_op jit(solution)/shard_map/slice | solution.py:104
  1.2 4.0 %collective-permute-start = (bf16[6,3,8192]{2,0,1:T(8,128)(2,1)S(1)}, bf16[6,3,8192]{2,0,1:T(8,128)(2,1)S(1)}, u32[]{:S(2)}, u32[]{:S(2)}) collective-permute-start(bf16[6,3,8192]{2,0,1:T(8,128)(2,1)S(1)} %slice.97), channel_id=1, source_target_pairs={{0,1},{1,2},{2,3},{3,4},{4,5},{5,6},{6,7},{7,8},{8,9},{9,10},{10,1... | collective-permute-start | bytes 884744 | tf_op jit(solution)/shard_map/ppermute | solution.py:13
  5.4 0.7 copy.53
  6.1 0.1 reduce-window.9
  6.2 0.1 reduce.3
  6.3 0.7 sub.88
  7.0 0.1 compare_convert_fusion
  7.1 0.2 convert_reduce_fusion
  7.3 0.1 and_convert_fusion.5
  7.4 4.2 %fusion.58 = (f32[3,1,8192]{2,1,0:T(1,128)S(1)}, f32[3,1,8192]{2,1,0:T(1,128)S(1)}, f32[3,1,8192]{2,1,0:T(1,128)S(1)}, f32[3,1,8192]{2,1,0:T(1,128)S(1)}, f32[3,...) fusion(f32[3,7,8192]{2,1,0:T(8,128)} %param.6), kind=kLoop, calls=%fused_computation.113 | loop fusion | bytes 1376256 | tf_op jit(solution)/shard_map/slice | solution.py:34
  11.6 0.1 copy.95
  11.7 0.7 sqrt_multiply_fusion
  12.4 0.1 convert_multiply_fusion
  12.5 0.1 copy_bitcast_fusion
  12.6 0.1 copy_bitcast_fusion.2
  12.8 0.1 copy_bitcast_fusion.4
  12.9 0.1 multiply_exponential_fusion.2
  13.0 0.1 exponential_select_fusion
  13.1 3.7 %collective-permute-done = bf16[6,3,8192]{2,0,1:T(8,128)(2,1)S(1)} collective-permute-done((bf16[6,3,8192]{2,0,1:T(8,128)(2,1)S(1)}, bf16[6,3,8192]{2,0,1:T(8,128)(2,1)S(1)}, u32[]{:S(2)}, u32[]{:S(2)}) %collective-permute-start) | collective-permute-done | bytes 294944 | tf_op jit(solution)/shard_map/ppermute | solution.py:13
  16.8 0.0 copy-done.1
  16.8 4.0 %multiply_add_fusion = f32[32,3,8192]{2,0,1:T(8,128)S(1)} fusion(bf16[32,3,8192]{2,0,1:T(8,128)(2,1)S(1)} %copy-done.1, bf16[6,3,8192]{2,0,1:T(8,128)(2,1)S(1)} %collective-permute-done, f32[32]{0:T(128)S(1)} %get-tuple-element.15, f32[3,8192]{1,0:T(4,128)S(1)} %get-tuple-element.20, f32[32]{0:T(128)S(1)} %get-tuple-element.16, ...), kind=kLoop, calls=%fused_computation.5 | loop fusion | flops 35389440 | bytes 5702528 | tf_op jit(solution)/shard_map/add | solution.py:33
  20.7 0.0 copy-start
  20.8 1.6 %copy-done = f32[32,3,8192]{2,0,1:T(8,128)} copy-done((f32[32,3,8192]{2,0,1:T(8,128)}, f32[32,3,8192]{2,0,1:T(8,128)S(1)}, u32[]{:S(2)}) %copy-start) | copy-done | bytes 3145752
  22.4 0.1 fusion.9
  22.5 0.1 copy.83
  22.6 1.1 %copy.54 = bf16[32,32,256]{2,0,1:T(8,128)(2,1)} copy(bf16[32,32,256]{2,1,0:T(8,128)(2,1)S(1)} %bitcast.95) | data formatting | bytes 1048576 | tf_op jit(solution)/shard_map/convert_element_type | solution.py:111
  23.7 6.7 %all-to-all-start = ((bf16[32,32,256]{2,0,1:T(8,128)(2,1)}), bf16[32,32,256]{2,0,1:T(8,128)(2,1)S(1)}, u32[]{:S(2)}, u32[]{:S(2)}) async-start(bf16[32,32,256]{2,0,1:T(8,128)(2,1)} %copy.54), calls=%async_computation | async-start | bytes 1048576 | tf_op jit(solution)/shard_map/all_to_all | solution.py:114
  30.4 0.1 mul.372
  30.5 0.2 mul.373
  30.7 0.1 exponential_multiply_fusion
  30.8 1.2 %convolution_select_fusion = f32[4,256,256]{2,1,0:T(8,128)S(1)} fusion(pred[256,256]{1,0:T(8,128)(4,1)S(1)} %subtract_compare_fusion, f32[4,16]{1,0:T(4,128)S(1)} %get-tuple-element.6, f32[4,16]{1,0:T(4,128)S(1)} %neg.12, f32[4,16]{1,0:T(4,128)S(1)} %get-tuple-element.5), kind=kOutput, calls=%fused_computation.22 | convolution fusion | flops 50642944 | bytes 1114880 | tf_op jit(solution)/shard_map/grm,gms->grs/dot_general | solution.py:57
  32.0 9.6 %all-to-all-done = bf16[32,32,256]{2,0,1:T(8,128)(2,1)S(1)} async-done(((bf16[32,32,256]{2,0,1:T(8,128)(2,1)}), bf16[32,32,256]{2,0,1:T(8,128)(2,1)S(1)}, u32[]{:S(2)}, u32[]{:S(2)}) %all-to-all-start) | async-done | bytes 524320 | tf_op jit(solution)/shard_map/all_to_all | solution.py:114
  41.7 0.4 reshape_reshape.3
  42.1 0.6 copy.56
  42.7 0.3 fusion.45
  43.1 0.4 convolution_add_fusion.2
  43.4 0.4 fusion.14
  43.8 0.3 convolution_add_fusion.1
  44.1 0.3 convolution_bitcast_fusion.2
  44.4 0.3 fusion.8
  44.8 0.1 broadcast_in_dim.38
  44.8 0.7 broadcast_in_dim.43
  45.6 8.2 %all-to-all-start.1 = ((f32[8,1,4096]{2,1,0:T(1,128)}), f32[8,1,4096]{2,1,0:T(1,128)S(1)}, u32[]{:S(2)}, u32[]{:S(2)}) async-start(f32[8,1,4096]{2,1,0:T(1,128)} %broadcast_in_dim.43), calls=%async_computation.1 | async-start | bytes 262144 | tf_op jit(solution)/shard_map/all_to_all | solution.py:73
  53.8 0.4 fusion.22
  54.2 7.9 %all-to-all-done.1 = f32[8,1,4096]{2,1,0:T(1,128)S(1)} async-done(((f32[8,1,4096]{2,1,0:T(1,128)}), f32[8,1,4096]{2,1,0:T(1,128)S(1)}, u32[]{:S(2)}, u32[]{:S(2)}) %all-to-all-start.1) | async-done | bytes 131104 | tf_op jit(solution)/shard_map/all_to_all | solution.py:73
  62.1 0.2 multiply_reduce_fusion
  62.2 0.1 reshape.207
  62.3 0.6 convolution_bitcast_fusion
  62.9 0.7 fusion.7
  63.7 0.7 copy.64
  64.3 0.7 convert_element_type.141
  65.0 16.5 %all_to_all.32 = bf16[32,32,256]{2,1,0:T(8,128)(2,1)S(1)} all-to-all(bf16[32,32,256]{2,1,0:T(8,128)(2,1)S(1)} %bitcast.96), channel_id=1, replica_groups=mesh['zo'=8,'zi'=4,'mp'=8] {'mp','zi'}, dimensions={0} | all-to-all | bytes 1048576 | tf_op jit(solution)/shard_map/all_to_all | solution.py:126
  81.6 0.1 convert_bitcast_fusion
  81.7 0.1 copy.82
  81.8 2.1 %fusion.11 = bf16[32,8192]{1,0:T(8,128)(2,1)} fusion(f32[32,8192]{1,0:T(8,128)S(1)} %bitcast.91, f32[32,3,8192]{2,0,1:T(8,128)} %copy-done), kind=kLoop, calls=%fused_computation.32 | loop fusion | flops 524288 | bytes 2621440 | tf_op jit(solution)/shard_map/convert_element_type | solution.py:127
  (13 shorter events, 0.2 us)
Async XLA Ops:
  0.0 16.8 %copy-start.1 = (bf16[32,3,8192]{2,0,1:T(8,128)(2,1)S(1)}, bf16[32,3,8192]{2,0,1:T(8,128)(2,1)}, u32[]{:S(2)}) copy-start(bf16[32,3,8192]{2,0,1:T(8,128)(2,1)} %param.5) | copy-start | bytes 4718596
  1.2 15.5 %collective-permute-start = (bf16[6,3,8192]{2,0,1:T(8,128)(2,1)S(1)}, bf16[6,3,8192]{2,0,1:T(8,128)(2,1)S(1)}, u32[]{:S(2)}, u32[]{:S(2)}) collective-permute-start(bf16[6,3,8192]{2,0,1:T(8,128)(2,1)S(1)} %slice.97), channel_id=1, source_target_pairs={{0,1},{1,2},{2,3},{3,4},{4,5},{5,6},{6,7},{7,8},{8,9},{9,10},{10,1... | collective-permute-start | bytes 884744 | tf_op jit(solution)/shard_map/ppermute | solution.py:13
  20.7 1.7 %copy-start = (f32[32,3,8192]{2,0,1:T(8,128)}, f32[32,3,8192]{2,0,1:T(8,128)S(1)}, u32[]{:S(2)}) copy-start(f32[32,3,8192]{2,0,1:T(8,128)S(1)} %multiply_add_fusion) | copy-start | bytes 9437188
  23.7 17.9 %all-to-all-start = ((bf16[32,32,256]{2,0,1:T(8,128)(2,1)}), bf16[32,32,256]{2,0,1:T(8,128)(2,1)S(1)}, u32[]{:S(2)}, u32[]{:S(2)}) async-start(bf16[32,32,256]{2,0,1:T(8,128)(2,1)} %copy.54), calls=%async_computation | async-start | bytes 1048576 | tf_op jit(solution)/shard_map/all_to_all | solution.py:114
  45.6 16.5 %all-to-all-start.1 = ((f32[8,1,4096]{2,1,0:T(1,128)}), f32[8,1,4096]{2,1,0:T(1,128)S(1)}, u32[]{:S(2)}, u32[]{:S(2)}) async-start(f32[8,1,4096]{2,1,0:T(1,128)} %broadcast_in_dim.43), calls=%async_computation.1 | async-start | bytes 262144 | tf_op jit(solution)/shard_map/all_to_all | solution.py:73

commit v17 on v15

--- a/solution.py
+++ b/solution.py
@@ -45,7 +45,7 @@
     return first + jnp.einsum(form, lower_part, inputs, preferred_element_type=jnp.float32)
 
 
-def long_filter(product, residues, decays, block_len, outer_axis):
+def long_filter(product, residues, decays, block_len, outer_axis, run_state):
     positions, channels = product.shape
     group_count = residues.shape[0]
     group_width = channels // group_count
@@ -64,8 +64,6 @@
     block_state = split_product("gms,bsgc->gmbc", end_weight, inputs)
 
     blocks = jnp.arange(block_count, dtype=jnp.float32)
-    to_end = jnp.exp(-decays[:, :, None] * (float(block_len) * (block_count - 1 - blocks))[None, None, :])
-    run_state = jnp.einsum("gmb,gmbc->gmc", to_end, block_state, precision=HIGH)
     count = lax.axis_size(outer_axis)
     flat = run_state.reshape(1, -1)
     sent = jnp.broadcast_to(flat, (count, flat.shape[1]))
@@ -97,7 +95,6 @@
 def shards(proj, conv_weight, residues, decays, doc_lengths):
     kernel_len = conv_weight.shape[1]
     rows = proj.shape[0]
-    outer_size = lax.axis_size("zo")
     inner_size = lax.axis_size("zi")
     mp_size = lax.axis_size("mp")
     lin_axis = ("zo", "zi", "mp")
@@ -114,14 +111,24 @@
     query_part = short_convolution(padded[:, :1], conv_weight[:1], padded_document_ids, padded_pos, rows)[:, 0]
     gathered, query_part = lax.optimization_barrier((gathered, query_part))
     width = gathered.shape[1]
-    gathered = gathered.reshape(mp_size, inner_size, rows, width).transpose(1, 0, 2, 3)
-    gathered = gathered.reshape(inner_size * mp_size * rows, width)
     groups_here = residues.shape[0] // inner_size
     first_group = lax.axis_index("zi") * groups_here
     local_residues = lax.dynamic_slice_in_dim(residues, first_group, groups_here, 0)
     local_decays = lax.dynamic_slice_in_dim(decays, first_group, groups_here, 0)
+    arrived = gathered.reshape(mp_size, inner_size, rows, groups_here, width // groups_here)
+    position_of = (
+        jnp.arange(inner_size, dtype=jnp.float32)[None, :, None] * float(mp_size * rows)
+        + jnp.arange(mp_size, dtype=jnp.float32)[:, None, None] * float(rows)
+        + jnp.arange(rows, dtype=jnp.float32)[None, None, :]
+    )
+    run_weight = jnp.exp(
+        -local_decays[:, :, None, None, None] * (float(inner_size * mp_size * rows) - position_of)[None, None]
+    )
+    run_state = split_product("gmabr,abrgc->gmc", run_weight, arrived)
+    gathered = gathered.reshape(mp_size, inner_size, rows, width).transpose(1, 0, 2, 3)
+    gathered = gathered.reshape(inner_size * mp_size * rows, width)
     block_len = min(256, gathered.shape[0])
-    filtered = long_filter(gathered, local_residues, local_decays, block_len, "zo")
+    filtered = long_filter(gathered, local_residues, local_decays, block_len, "zo", run_state)
     filtered = filtered.reshape(inner_size, mp_size, rows, width).transpose(1, 0, 2, 3)
     filtered = filtered.reshape(inner_size * mp_size * rows, width)
     filtered = lax.all_to_all(filtered, swap_axis, split_axis=0, concat_axis=1, tiled=True)

time: 90.2 us -> 92.8 us (1.029)
  local copies, waits for them, and re-layouts: 16.8 us -> 18.6 us
    reshape x0 -> x1, local copies, waits for them, and re-layouts: none -> 1.42 us  [shards(): gathered.reshape(mp_size, inner_size, rows, groups_here, width // groups_...]
    unnamed x25 -> x27, local copies, waits for them, and re-layouts: 3.72 us -> 4.31 us
  transfers between devices with their start and end apart: 3 -> 3, of which waited for: 2 -> 2; matrix products, arithmetic and copies ran while one was open for 24% -> 23% of each run, Pallas kernels for 0% -> 0%
where the time goes in v17:
time: 92.8 us; the launch traced here: 92.1 us
  starting transfers between devices  20 us (22%)
  local copies, waits for them, and re-layouts  18.6 us (20%)
  blocking collectives  16.6 us (18%)
  waiting for transfers between devices  16.1 us (17%)
  other arithmetic  14.2 us (15%)
  matrix products  6.32 us (7%)
    all_to_all x1, blocking collectives, shards(): lax.all_to_all(filtered, swap_axis, split_axis=0, concat_axis=1, tiled=True)  16.6 us
    all_to_all x1, waiting for transfers between devices, shards(): lax.all_to_all(product, swap_axis, split_axis=1, concat_axis=0, tiled=True)  8.24 us
    all_to_all x1, starting transfers between devices, long_filter(): lax.all_to_all(sent, outer_axis, split_axis=0, concat_axis=0, tiled=True)  8.19 us
    all_to_all x1, waiting for transfers between devices, long_filter(): lax.all_to_all(sent, outer_axis, split_axis=0, concat_axis=0, tiled=True)  7.87 us
    all_to_all x1, starting transfers between devices, shards(): lax.all_to_all(product, swap_axis, split_axis=1, concat_axis=0, tiled=True)  7.75 us
    slice x2, local copies, waits for them, and re-layouts, short_convolution(): conv_weight[:, position_shift, :][None] * earlier  6.23 us
    unnamed x27, local copies, waits for them, and re-layouts  4.31 us
    ppermute x1, starting transfers between devices, shifted(): return lax.ppermute(block, axis, route)  4.02 us
  transfers between devices with their start and end apart: 3, of which 2 were waited for; matrix products, arithmetic and copies ran while one was open for 23% of the time, Pallas kernels for 0%

profile of v17, /device:TPU:1, one launch (start us, length us, event | category | flops | bytes accessed | tf_op | source)
XLA Modules:
  0.0 92.1 jit_solution(15428475301504701744)
XLA Ops:
  0.0 1.1 %slice.189 = bf16[6,3,8192]{2,0,1:T(8,128)(2,1)S(1)} slice(bf16[32,3,8192]{2,0,1:T(8,128)(2,1)} %param.5), slice={[26:32], [0:3], [0:8192]} | slice | bytes 589824 | tf_op jit(solution)/shard_map/slice | solution.py:101
  1.1 4.0 %collective-permute-start = (bf16[6,3,8192]{2,0,1:T(8,128)(2,1)S(1)}, bf16[6,3,8192]{2,0,1:T(8,128)(2,1)S(1)}, u32[]{:S(2)}, u32[]{:S(2)}) collective-permute-start(bf16[6,3,8192]{2,0,1:T(8,128)(2,1)S(1)} %slice.189), channel_id=1, source_target_pairs={{0,1},{1,2},{2,3},{3,4},{4,5},{5,6},{6,7},{7,8},{8,9},{9,10},{10,1... | collective-permute-start | bytes 884744 | tf_op jit(solution)/shard_map/ppermute | solution.py:13
  5.1 0.0 copy-start
  5.2 3.2 %fusion.65 = (f32[2,1,8192]{2,1,0:T(1,128)S(1)}, f32[2,1,8192]{2,1,0:T(1,128)S(1)}, f32[2,1,8192]{2,1,0:T(1,128)S(1)}, f32[2,1,8192]{2,1,0:T(1,128)S(1)}, f32[2,...) fusion(f32[3,7,8192]{2,1,0:T(8,128)} %param.6), kind=kLoop, calls=%fused_computation.136 | loop fusion | bytes 917504 | tf_op jit(solution)/shard_map/slice | solution.py:34
  8.4 3.0 %fusion.64 = (f32[1,1,8192]{2,1,0:T(1,128)}, f32[1,1,8192]{2,1,0:T(1,128)}, f32[1,1,8192]{2,1,0:T(1,128)}, f32[1,1,8192]{2,1,0:T(1,128)}, f32[1,1,8192]{2,1,0:T(...) fusion(f32[3,7,8192]{2,1,0:T(8,128)} %param.6), kind=kLoop, calls=%fused_computation.135 | loop fusion | bytes 458752 | tf_op jit(solution)/shard_map/slice | solution.py:34
  11.4 0.5 iota_subtract_fusion
  11.9 0.6 subtract_compare_fusion
  12.6 0.0 copy-done.9
  12.6 0.1 copy.55
  12.7 0.1 reduce-window.9
  12.8 0.1 reduce.3
  13.0 0.6 compare_convert_fusion
  13.6 0.2 convert_reduce_fusion
  13.8 0.7 and_convert_fusion.5
  14.4 0.7 sqrt_multiply_fusion
  15.2 0.7 convert_multiply_fusion
  15.8 0.1 broadcast_add_fusion
  15.9 0.7 add_subtract_fusion
  16.6 0.1 multiply_exponential_fusion.2
  16.7 0.7 exponential_multiply_fusion
  17.4 0.7 copy_bitcast_fusion.1
  18.1 0.8 copy_bitcast_fusion.3
  18.9 0.8 copy_bitcast_fusion.5
  19.6 0.1 exponential_select_fusion
  19.7 0.5 iota_compare_fusion
  20.2 0.1 copy.103
  20.3 0.1 mul.549
  20.4 0.8 mul.550
  21.3 2.0 %convolution_select_fusion = f32[4,256,256]{2,1,0:T(8,128)S(1)} fusion(pred[256,256]{1,0:T(8,128)(4,1)} %subtract_compare_fusion, f32[4,16]{1,0:T(4,128)} %copy-done.5, f32[4,16]{1,0:T(4,128)S(1)} %neg.13, f32[4,16]{1,0:T(4,128)S(1)} %get-tuple-element.9), kind=kOutput, calls=%fused_computation.28 | convolution fusion | flops 50642944 | bytes 1114880 | tf_op jit(solution)/shard_map/grm,gms->grs/dot_general | solution.py:57
  23.3 0.0 collective-permute-done
  23.3 0.0 copy-done
  23.3 3.6 %multiply_add_fusion = f32[32,2,8192]{2,0,1:T(8,128)S(1)} fusion(bf16[32,3,8192]{2,0,1:T(8,128)(2,1)S(1)} %copy-done, bf16[6,3,8192]{2,0,1:T(8,128)(2,1)S(1)} %collective-permute-done, f32[32]{0:T(128)} %get-tuple-element.26, f32[2,8192]{1,0:T(2,128)S(1)} %get-tuple-element.31, f32[32]{0:T(128)} %get-tuple-element.27, f32[2,8192]{1,0:T(2,128)} %get-tuple-element.32, ...), kind=kLoop, calls=%fused_computation.11 | loop fusion | flops 23592960 | bytes 5571456 | tf_op jit(solution)/shard_map/add | solution.py:33
  26.9 0.1 fusion.10
  27.0 0.1 copy.85
  27.1 1.1 %copy.56 = bf16[32,32,256]{2,0,1:T(8,128)(2,1)} copy(bf16[32,32,256]{2,1,0:T(8,128)(2,1)S(1)} %bitcast.102) | data formatting | bytes 1048576 | tf_op jit(solution)/shard_map/convert_element_type | solution.py:107
  28.2 7.7 %all-to-all-start = ((bf16[32,32,256]{2,0,1:T(8,128)(2,1)}), bf16[32,32,256]{2,0,1:T(8,128)(2,1)S(1)}, u32[]{:S(2)}, u32[]{:S(2)}) async-start(bf16[32,32,256]{2,0,1:T(8,128)(2,1)} %copy.56), calls=%async_computation | async-start | bytes 1048576 | tf_op jit(solution)/shard_map/all_to_all | solution.py:110
  35.9 3.0 %add_bitcast_fusion = f32[32,8192]{1,0:T(8,128)} fusion(bf16[32,3,8192]{2,0,1:T(8,128)(2,1)S(1)} %copy-done, bf16[6,3,8192]{2,0,1:T(8,128)(2,1)S(1)} %collective-permute-done, f32[32]{0:T(128)} %get-tuple-element.26, f32[8192]{0:T(1024)} %bitcast.110, f32[32]{0:T(128)} %get-tuple-element.27, f32[8192]{0:T(1024)} %bitcast.111, f32[32]{0:T(128)} %get-tuple-element.28, ...), kind=kLoop, calls=%fused_computation.48 | loop fusion | flops 11796480 | bytes 3769216 | tf_op jit(solution)/shard_map/squeeze | solution.py:111
  39.0 8.2 %all-to-all-done = bf16[32,32,256]{2,0,1:T(8,128)(2,1)S(1)} async-done(((bf16[32,32,256]{2,0,1:T(8,128)(2,1)}), bf16[32,32,256]{2,0,1:T(8,128)(2,1)S(1)}, u32[]{:S(2)}, u32[]{:S(2)}) %all-to-all-start) | async-done | bytes 524320 | tf_op jit(solution)/shard_map/all_to_all | solution.py:110
  47.2 1.4 %reshape.251 = bf16[8,4,32,4,64]{4,3,2,1,0:T(4,128)(2,1)} reshape(bf16[1024,256]{1,0:T(8,128)(2,1)S(1)} %bitcast.96) | data formatting | bytes 1048576 | tf_op jit(solution)/shard_map/reshape | solution.py:118
  48.7 0.4 reshape_reshape.3
  49.1 0.6 copy.58
  49.7 0.3 fusion.51
  50.0 0.4 convolution_add_fusion.2
  50.4 0.4 fusion.22
  50.8 0.3 convolution_add_fusion.1
  51.1 0.9 copy-done.2
  52.0 0.6 convolution_bitcast_fusion.1
  52.6 0.6 fusion.3
  53.2 0.1 broadcast_in_dim.38
  53.2 0.7 broadcast_in_dim.39
  54.0 8.2 %all-to-all-start.1 = ((f32[8,1,4096]{2,1,0:T(1,128)}), f32[8,1,4096]{2,1,0:T(1,128)S(1)}, u32[]{:S(2)}, u32[]{:S(2)}) async-start(f32[8,1,4096]{2,1,0:T(1,128)} %broadcast_in_dim.39), calls=%async_computation.1 | async-start | bytes 262144 | tf_op jit(solution)/shard_map/all_to_all | solution.py:70
  62.2 0.4 fusion.32
  62.6 7.9 %all-to-all-done.1 = f32[8,1,4096]{2,1,0:T(1,128)S(1)} async-done(((f32[8,1,4096]{2,1,0:T(1,128)}), f32[8,1,4096]{2,1,0:T(1,128)S(1)}, u32[]{:S(2)}, u32[]{:S(2)}) %all-to-all-start.1) | async-done | bytes 131104 | tf_op jit(solution)/shard_map/all_to_all | solution.py:70
  70.5 0.2 multiply_reduce_fusion
  70.6 0.1 reshape.260
  70.7 0.6 convolution_bitcast_fusion
  71.4 0.7 fusion.2
  72.1 0.7 copy.66
  72.8 0.7 convert_element_type.176
  73.5 16.6 %all_to_all.35 = bf16[32,32,256]{2,1,0:T(8,128)(2,1)S(1)} all-to-all(bf16[32,32,256]{2,1,0:T(8,128)(2,1)S(1)} %bitcast.103), channel_id=1, replica_groups=mesh['zo'=8,'zi'=4,'mp'=8] {'mp','zi'}, dimensions={0} | all-to-all | bytes 1048576 | tf_op jit(solution)/shard_map/all_to_all | solution.py:134
  90.0 0.1 convert_bitcast_fusion
  90.1 0.1 copy.84
  90.2 1.0 %copy-done.1 = f32[32,8192]{1,0:T(8,128)S(1)} copy-done((f32[32,8192]{1,0:T(8,128)S(1)}, f32[32,8192]{1,0:T(8,128)}, u32[]{:S(2)}) %copy-start.1) | copy-done | bytes 1048600
  91.2 0.9 multiply_convert_fusion
  (28 shorter events, 0.2 us)
Async XLA Ops:
  0.0 12.6 %copy-start.9 = (s32[64]{0:T(128)S(1)}, s32[64]{0:T(128)}, u32[]{:S(2)}) copy-start(s32[64]{0:T(128)} %param.9) | copy-start | bytes 772
  1.1 22.2 %collective-permute-start = (bf16[6,3,8192]{2,0,1:T(8,128)(2,1)S(1)}, bf16[6,3,8192]{2,0,1:T(8,128)(2,1)S(1)}, u32[]{:S(2)}, u32[]{:S(2)}) collective-permute-start(bf16[6,3,8192]{2,0,1:T(8,128)(2,1)S(1)} %slice.189), channel_id=1, source_target_pairs={{0,1},{1,2},{2,3},{3,4},{4,5},{5,6},{6,7},{7,8},{8,9},{9,10},{10,1... | collective-permute-start | bytes 884744 | tf_op jit(solution)/shard_map/ppermute | solution.py:13
  5.1 18.2 %copy-start = (bf16[32,3,8192]{2,0,1:T(8,128)(2,1)S(1)}, bf16[32,3,8192]{2,0,1:T(8,128)(2,1)}, u32[]{:S(2)}) copy-start(bf16[32,3,8192]{2,0,1:T(8,128)(2,1)} %param.5) | copy-start | bytes 4718596
  15.1 1.4 %copy-start.5 = (f32[4,16]{1,0:T(4,128)}, f32[4,16]{1,0:T(4,128)S(1)}, u32[]{:S(2)}) copy-start(f32[4,16]{1,0:T(4,128)S(1)} %get-tuple-element.10) | copy-start | bytes 772
  28.2 19.0 %all-to-all-start = ((bf16[32,32,256]{2,0,1:T(8,128)(2,1)}), bf16[32,32,256]{2,0,1:T(8,128)(2,1)S(1)}, u32[]{:S(2)}, u32[]{:S(2)}) async-start(bf16[32,32,256]{2,0,1:T(8,128)(2,1)} %copy.56), calls=%async_computation | async-start | bytes 1048576 | tf_op jit(solution)/shard_map/all_to_all | solution.py:110
  48.6 1.1 %copy-start.7 = (f32[256]{0:T(256)S(1)}, f32[256]{0:T(256)}, u32[]{:S(2)}) copy-start(f32[256]{0:T(256)} %iota_subtract_fusion) | copy-start | bytes 3076
  50.8 1.2 %copy-start.2 = (bf16[8,4,32,4,64]{4,3,2,1,0:T(4,128)(2,1)S(1)}, bf16[8,4,32,4,64]{4,3,2,1,0:T(4,128)(2,1)}, u32[]{:S(2)}) copy-start(bf16[8,4,32,4,64]{4,3,2,1,0:T(4,128)(2,1)} %reshape.251) | copy-start | bytes 1572868
  50.8 1.2 %copy-start.6 = (f32[8,4,32]{2,1,0:T(4,128)S(1)}, f32[8,4,32]{2,1,0:T(4,128)}, u32[]{:S(2)}) copy-start(f32[8,4,32]{2,1,0:T(4,128)} %add_subtract_fusion) | copy-start | bytes 12292
  52.0 10.2 %copy-start.8 = (f32[4,4]{1,0:T(4,128)S(1)}, f32[4,4]{1,0:T(4,128)}, u32[]{:S(2)}) copy-start(f32[4,4]{1,0:T(4,128)} %convert_multiply_fusion) | copy-start | bytes 196
  52.0 10.2 %copy-start.10 = (pred[4,4]{1,0:T(4,128)(4,1)S(1)}, pred[4,4]{1,0:T(4,128)(4,1)}, u32[]{:S(2)}) copy-start(pred[4,4]{1,0:T(4,128)(4,1)} %iota_compare_fusion) | copy-start | bytes 52
  52.0 18.5 %copy-start.3 = (f32[8,1,4096]{2,1,0:T(1,128)S(1)}, f32[8,1,4096]{2,1,0:T(1,128)}, u32[]{:S(2)}) copy-start(f32[8,1,4096]{2,1,0:T(1,128)} %mul.550) | copy-start | bytes 393220
  52.6 18.1 %copy-start.4 = (f32[4,256,16]{1,2,0:T(8,128)S(1)}, f32[4,256,16]{1,2,0:T(8,128)}, u32[]{:S(2)}) copy-start(f32[4,256,16]{1,2,0:T(8,128)} %exponential_multiply_fusion) | copy-start | bytes 196612
  54.0 16.5 %all-to-all-start.1 = ((f32[8,1,4096]{2,1,0:T(1,128)}), f32[8,1,4096]{2,1,0:T(1,128)S(1)}, u32[]{:S(2)}, u32[]{:S(2)}) async-start(f32[8,1,4096]{2,1,0:T(1,128)} %broadcast_in_dim.39), calls=%async_computation.1 | async-start | bytes 262144 | tf_op jit(solution)/shard_map/all_to_all | solution.py:70
  90.0 1.2 %copy-start.1 = (f32[32,8192]{1,0:T(8,128)S(1)}, f32[32,8192]{1,0:T(8,128)}, u32[]{:S(2)}) copy-start(f32[32,8192]{1,0:T(8,128)} %add_bitcast_fusion) | copy-start | bytes 3145732

commit v18 on v15

--- a/solution.py
+++ b/solution.py
@@ -64,8 +64,9 @@
     block_state = split_product("gms,bsgc->gmbc", end_weight, inputs)
 
     blocks = jnp.arange(block_count, dtype=jnp.float32)
-    to_end = jnp.exp(-decays[:, :, None] * (float(block_len) * (block_count - 1 - blocks))[None, None, :])
-    run_state = jnp.einsum("gmb,gmbc->gmc", to_end, block_state, precision=HIGH)
+    run_offsets = jnp.arange(positions, dtype=jnp.float32).reshape(block_count, block_len)
+    run_weight = jnp.exp(-decays[:, :, None, None] * (float(positions) - run_offsets)[None, None])
+    run_state = split_product("gmbs,bsgc->gmc", run_weight, inputs)
     count = lax.axis_size(outer_axis)
     flat = run_state.reshape(1, -1)
     sent = jnp.broadcast_to(flat, (count, flat.shape[1]))
@@ -86,7 +87,7 @@
     block_gap = jnp.maximum(later - 1 - before, 0).astype(jnp.float32) * float(block_len)
     carry = jnp.where((before < later)[None, None], jnp.exp(-decays[:, :, None, None] * block_gap[None, None]), 0.0)
     state = jnp.einsum("gmab,gmbc->gmac", carry, block_state, precision=HIGH)
-    partial = intra + jnp.einsum("grm,gmbc->brgc", left, state, precision=HIGH)
+    partial = lax.optimization_barrier(intra + jnp.einsum("grm,gmbc->brgc", left, state, precision=HIGH))
 
     start_decay = jnp.exp(-decays[:, :, None] * (float(block_len) * blocks)[None, None, :])
     run_left = left[:, None, :, :] * jnp.transpose(start_decay, (0, 2, 1))[:, :, None, :]
@@ -97,7 +98,6 @@
 def shards(proj, conv_weight, residues, decays, doc_lengths):
     kernel_len = conv_weight.shape[1]
     rows = proj.shape[0]
-    outer_size = lax.axis_size("zo")
     inner_size = lax.axis_size("zi")
     mp_size = lax.axis_size("mp")
     lin_axis = ("zo", "zi", "mp")

time: 90.2 us -> 89 us (0.987)
    unnamed x25 -> x27, local copies, waits for them, and re-layouts: 3.72 us -> 3.76 us
  transfers between devices with their start and end apart: 3 -> 3, of which waited for: 2 -> 2; matrix products, arithmetic and copies ran while one was open for 24% -> 25% of each run, Pallas kernels for 0% -> 0%
where the time goes in v18:
time: 89 us; the launch traced here: 88.4 us
  starting transfers between devices  20 us (22%)
  local copies, waits for them, and re-layouts  16.9 us (19%)
  blocking collectives  16.5 us (19%)
  waiting for transfers between devices  15.4 us (17%)
  other arithmetic  13.5 us (15%)
  matrix products  5.77 us (6%)
    all_to_all x1, blocking collectives, shards(): lax.all_to_all(filtered, swap_axis, split_axis=0, concat_axis=1, tiled=True)  16.5 us
    all_to_all x1, waiting for transfers between devices, shards(): lax.all_to_all(product, swap_axis, split_axis=1, concat_axis=0, tiled=True)  8.22 us
    all_to_all x1, starting transfers between devices, long_filter(): lax.all_to_all(sent, outer_axis, split_axis=0, concat_axis=0, tiled=True)  8.19 us
    all_to_all x1, starting transfers between devices, shards(): lax.all_to_all(product, swap_axis, split_axis=1, concat_axis=0, tiled=True)  7.75 us
    all_to_all x1, waiting for transfers between devices, long_filter(): lax.all_to_all(sent, outer_axis, split_axis=0, concat_axis=0, tiled=True)  7.16 us
    slice x2, local copies, waits for them, and re-layouts, short_convolution(): conv_weight[:, position_shift, :][None] * earlier  6.45 us
    ppermute x1, starting transfers between devices, shifted(): return lax.ppermute(block, axis, route)  4.02 us
    unnamed x27, local copies, waits for them, and re-layouts  3.76 us
  transfers between devices with their start and end apart: 3, of which 2 were waited for; matrix products, arithmetic and copies ran while one was open for 25% of the time, Pallas kernels for 0%

profile of v18, /device:TPU:1, one launch (start us, length us, event | category | flops | bytes accessed | tf_op | source)
XLA Modules:
  0.0 88.4 jit_solution(878549558242343620)
XLA Ops:
  0.0 1.1 %slice.189 = bf16[6,3,8192]{2,0,1:T(8,128)(2,1)S(1)} slice(bf16[32,3,8192]{2,0,1:T(8,128)(2,1)} %param.5), slice={[26:32], [0:3], [0:8192]} | slice | bytes 589824 | tf_op jit(solution)/shard_map/slice | solution.py:104
  1.1 4.0 %collective-permute-start = (bf16[6,3,8192]{2,0,1:T(8,128)(2,1)S(1)}, bf16[6,3,8192]{2,0,1:T(8,128)(2,1)S(1)}, u32[]{:S(2)}, u32[]{:S(2)}) collective-permute-start(bf16[6,3,8192]{2,0,1:T(8,128)(2,1)S(1)} %slice.189), channel_id=1, source_target_pairs={{0,1},{1,2},{2,3},{3,4},{4,5},{5,6},{6,7},{7,8},{8,9},{9,10},{10,1... | collective-permute-start | bytes 884744 | tf_op jit(solution)/shard_map/ppermute | solution.py:13
  5.1 0.0 copy-start
  5.2 3.4 %fusion.63 = (f32[2,1,8192]{2,1,0:T(1,128)S(1)}, f32[2,1,8192]{2,1,0:T(1,128)S(1)}, f32[2,1,8192]{2,1,0:T(1,128)S(1)}, f32[2,1,8192]{2,1,0:T(1,128)S(1)}, f32[2,...) fusion(f32[3,7,8192]{2,1,0:T(8,128)} %param.6), kind=kLoop, calls=%fused_computation.132 | loop fusion | bytes 917504 | tf_op jit(solution)/shard_map/slice | solution.py:34
  8.6 3.1 %fusion.62 = (f32[1,1,8192]{2,1,0:T(1,128)}, f32[1,1,8192]{2,1,0:T(1,128)}, f32[1,1,8192]{2,1,0:T(1,128)}, f32[1,1,8192]{2,1,0:T(1,128)}, f32[1,1,8192]{2,1,0:T(...) fusion(f32[3,7,8192]{2,1,0:T(8,128)} %param.6), kind=kLoop, calls=%fused_computation.131 | loop fusion | bytes 458752 | tf_op jit(solution)/shard_map/slice | solution.py:34
  11.6 0.6 subtract_compare_fusion
  12.3 0.6 iota_subtract_fusion
  12.9 0.0 copy-done.9
  12.9 0.1 copy.55
  13.0 0.1 reduce-window.9
  13.1 0.1 reduce.3
  13.2 0.6 compare_convert_fusion
  13.8 0.2 convert_reduce_fusion
  14.0 0.7 and_convert_fusion.5
  14.7 0.7 sqrt_multiply_fusion
  15.4 0.0 copy-start.6
  15.4 0.7 convert_multiply_fusion
  16.1 0.1 multiply_exponential_fusion.2
  16.2 0.7 exponential_multiply_fusion
  16.9 0.0 copy-done.4
  16.9 0.7 copy_bitcast_fusion.1
  17.6 0.8 copy_bitcast_fusion.3
  18.4 0.8 copy_bitcast_fusion.5
  19.1 0.1 exponential_select_fusion
  19.2 0.5 iota_compare_fusion
  19.8 0.1 copy.99
  19.8 0.1 mul.533
  19.9 0.8 mul.534
  20.8 2.0 %convolution_select_fusion = f32[4,256,256]{2,1,0:T(8,128)S(1)} fusion(pred[256,256]{1,0:T(8,128)(4,1)} %subtract_compare_fusion, f32[4,16]{1,0:T(4,128)} %copy-done.6, f32[4,16]{1,0:T(4,128)S(1)} %neg.12, f32[4,16]{1,0:T(4,128)} %copy-done.4), kind=kOutput, calls=%fused_computation.28 | convolution fusion | flops 50642944 | bytes 1114880 | tf_op jit(solution)/shard_map/grm,gms->grs/dot_general | solution.py:57
  22.8 0.0 collective-permute-done
  22.8 3.6 %multiply_add_fusion = f32[32,2,8192]{2,0,1:T(8,128)S(1)} fusion(bf16[32,3,8192]{2,0,1:T(8,128)(2,1)S(1)} %copy-done, bf16[6,3,8192]{2,0,1:T(8,128)(2,1)S(1)} %collective-permute-done, f32[32]{0:T(128)} %get-tuple-element.26, f32[2,8192]{1,0:T(2,128)S(1)} %get-tuple-element.31, f32[32]{0:T(128)} %get-tuple-element.27, f32[2,8192]{1,0:T(2,128)} %get-tuple-element.32, ...), kind=kLoop, calls=%fused_computation.11 | loop fusion | flops 23592960 | bytes 5571456 | tf_op jit(solution)/shard_map/add | solution.py:33
  26.4 0.1 fusion.10
  26.5 0.1 copy.85
  26.6 1.1 %copy.56 = bf16[32,32,256]{2,0,1:T(8,128)(2,1)} copy(bf16[32,32,256]{2,1,0:T(8,128)(2,1)S(1)} %bitcast.101) | data formatting | bytes 1048576 | tf_op jit(solution)/shard_map/convert_element_type | solution.py:110
  27.7 7.7 %all-to-all-start = ((bf16[32,32,256]{2,0,1:T(8,128)(2,1)}), bf16[32,32,256]{2,0,1:T(8,128)(2,1)S(1)}, u32[]{:S(2)}, u32[]{:S(2)}) async-start(bf16[32,32,256]{2,0,1:T(8,128)(2,1)} %copy.56), calls=%async_computation | async-start | bytes 1048576 | tf_op jit(solution)/shard_map/all_to_all | solution.py:113
  35.4 3.0 %add_bitcast_fusion = f32[32,8192]{1,0:T(8,128)} fusion(bf16[32,3,8192]{2,0,1:T(8,128)(2,1)S(1)} %copy-done, bf16[6,3,8192]{2,0,1:T(8,128)(2,1)S(1)} %collective-permute-done, f32[32]{0:T(128)} %get-tuple-element.26, f32[8192]{0:T(1024)} %bitcast.109, f32[32]{0:T(128)} %get-tuple-element.27, f32[8192]{0:T(1024)} %bitcast.110, f32[32]{0:T(128)} %get-tuple-element.28, ...), kind=kLoop, calls=%fused_computation.45 | loop fusion | flops 11796480 | bytes 3769216 | tf_op jit(solution)/shard_map/squeeze | solution.py:114
  38.5 8.2 %all-to-all-done = bf16[32,32,256]{2,0,1:T(8,128)(2,1)S(1)} async-done(((bf16[32,32,256]{2,0,1:T(8,128)(2,1)}), bf16[32,32,256]{2,0,1:T(8,128)(2,1)S(1)}, u32[]{:S(2)}, u32[]{:S(2)}) %all-to-all-start) | async-done | bytes 524320 | tf_op jit(solution)/shard_map/all_to_all | solution.py:113
  46.7 0.4 reshape_reshape.3
  47.1 0.6 copy.58
  47.8 0.3 fusion.18
  48.1 0.0 copy-start.7
  48.1 0.3 convolution_add_fusion.1
  48.5 0.3 copy-done.7
  48.8 0.3 fusion.49
  49.1 0.4 convolution_add_fusion.2
  49.5 0.3 convolution_bitcast_fusion.2
  49.8 0.3 fusion.3
  50.1 0.1 broadcast_in_dim.38
  50.2 0.7 broadcast_in_dim.39
  50.9 8.2 %all-to-all-start.1 = ((f32[8,1,4096]{2,1,0:T(1,128)}), f32[8,1,4096]{2,1,0:T(1,128)S(1)}, u32[]{:S(2)}, u32[]{:S(2)}) async-start(f32[8,1,4096]{2,1,0:T(1,128)} %broadcast_in_dim.39), calls=%async_computation.1 | async-start | bytes 262144 | tf_op jit(solution)/shard_map/all_to_all | solution.py:73
  59.1 0.4 fusion.26
  59.6 0.7 fusion
  60.3 7.2 %all-to-all-done.1 = f32[8,1,4096]{2,1,0:T(1,128)S(1)} async-done(((f32[8,1,4096]{2,1,0:T(1,128)}), f32[8,1,4096]{2,1,0:T(1,128)S(1)}, u32[]{:S(2)}, u32[]{:S(2)}) %all-to-all-start.1) | async-done | bytes 131104 | tf_op jit(solution)/shard_map/all_to_all | solution.py:73
  67.5 0.0 copy-done.2
  67.5 0.2 multiply_reduce_fusion
  67.6 0.1 reshape.227
  67.7 0.6 fusion.2
  68.3 0.7 copy.66
  69.0 0.7 convert_element_type.176
  69.7 16.5 %all_to_all.35 = bf16[32,32,256]{2,1,0:T(8,128)(2,1)S(1)} all-to-all(bf16[32,32,256]{2,1,0:T(8,128)(2,1)S(1)} %bitcast.102), channel_id=1, replica_groups=mesh['zo'=8,'zi'=4,'mp'=8] {'mp','zi'}, dimensions={0} | all-to-all | bytes 1048576 | tf_op jit(solution)/shard_map/all_to_all | solution.py:127
  86.3 0.1 convert_bitcast_fusion
  86.4 0.1 copy.84
  86.5 1.0 %copy-done.1 = f32[32,8192]{1,0:T(8,128)S(1)} copy-done((f32[32,8192]{1,0:T(8,128)S(1)}, f32[32,8192]{1,0:T(8,128)}, u32[]{:S(2)}) %copy-start.1) | copy-done | bytes 1048600
  87.5 0.9 %multiply_convert_fusion = bf16[32,8192]{1,0:T(8,128)(2,1)} fusion(f32[32,8192]{1,0:T(8,128)S(1)} %copy-done.1, f32[32,8192]{1,0:T(8,128)S(1)} %bitcast.96), kind=kLoop, calls=%fused_computation.43 | loop fusion | flops 524288 | bytes 2621440 | tf_op jit(solution)/shard_map/convert_element_type | solution.py:128
  (25 shorter events, 0.1 us)
Async XLA Ops:
  0.0 12.9 %copy-start.9 = (s32[64]{0:T(128)S(1)}, s32[64]{0:T(128)}, u32[]{:S(2)}) copy-start(s32[64]{0:T(128)} %param.9) | copy-start | bytes 772
  1.1 21.7 %collective-permute-start = (bf16[6,3,8192]{2,0,1:T(8,128)(2,1)S(1)}, bf16[6,3,8192]{2,0,1:T(8,128)(2,1)S(1)}, u32[]{:S(2)}, u32[]{:S(2)}) collective-permute-start(bf16[6,3,8192]{2,0,1:T(8,128)(2,1)S(1)} %slice.189), channel_id=1, source_target_pairs={{0,1},{1,2},{2,3},{3,4},{4,5},{5,6},{6,7},{7,8},{8,9},{9,10},{10,1... | collective-permute-start | bytes 884744 | tf_op jit(solution)/shard_map/ppermute | solution.py:13
  5.1 17.7 %copy-start = (bf16[32,3,8192]{2,0,1:T(8,128)(2,1)S(1)}, bf16[32,3,8192]{2,0,1:T(8,128)(2,1)}, u32[]{:S(2)}) copy-start(bf16[32,3,8192]{2,0,1:T(8,128)(2,1)} %param.5) | copy-start | bytes 4718596
  15.4 1.5 %copy-start.4 = (f32[4,16]{1,0:T(4,128)}, f32[4,16]{1,0:T(4,128)S(1)}, u32[]{:S(2)}) copy-start(f32[4,16]{1,0:T(4,128)S(1)} %get-tuple-element.9) | copy-start | bytes 772
  15.4 1.5 %copy-start.6 = (f32[4,16]{1,0:T(4,128)}, f32[4,16]{1,0:T(4,128)S(1)}, u32[]{:S(2)}) copy-start(f32[4,16]{1,0:T(4,128)S(1)} %get-tuple-element.10) | copy-start | bytes 772
  27.7 19.0 %all-to-all-start = ((bf16[32,32,256]{2,0,1:T(8,128)(2,1)}), bf16[32,32,256]{2,0,1:T(8,128)(2,1)S(1)}, u32[]{:S(2)}, u32[]{:S(2)}) async-start(bf16[32,32,256]{2,0,1:T(8,128)(2,1)} %copy.56), calls=%async_computation | async-start | bytes 1048576 | tf_op jit(solution)/shard_map/all_to_all | solution.py:113
  48.1 0.7 copy-start.7
  48.8 10.3 %copy-start.8 = (f32[4,4]{1,0:T(4,128)S(1)}, f32[4,4]{1,0:T(4,128)}, u32[]{:S(2)}) copy-start(f32[4,4]{1,0:T(4,128)} %convert_multiply_fusion) | copy-start | bytes 196
  48.8 10.3 %copy-start.10 = (pred[4,4]{1,0:T(4,128)(4,1)S(1)}, pred[4,4]{1,0:T(4,128)(4,1)}, u32[]{:S(2)}) copy-start(pred[4,4]{1,0:T(4,128)(4,1)} %iota_compare_fusion) | copy-start | bytes 52
  48.8 10.8 %copy-start.5 = (f32[4,16]{1,0:T(4,128)S(1)}, f32[4,16]{1,0:T(4,128)}, u32[]{:S(2)}) copy-start(f32[4,16]{1,0:T(4,128)} %copy-done.4) | copy-start | bytes 772
  49.5 18.0 %copy-start.2 = (f32[8,1,4096]{2,1,0:T(1,128)S(1)}, f32[8,1,4096]{2,1,0:T(1,128)}, u32[]{:S(2)}) copy-start(f32[8,1,4096]{2,1,0:T(1,128)} %mul.534) | copy-start | bytes 393220
  49.8 17.9 %copy-start.3 = (f32[4,256,16]{1,2,0:T(8,128)S(1)}, f32[4,256,16]{1,2,0:T(8,128)}, u32[]{:S(2)}) copy-start(f32[4,256,16]{1,2,0:T(8,128)} %exponential_multiply_fusion) | copy-start | bytes 196612
  50.9 16.5 %all-to-all-start.1 = ((f32[8,1,4096]{2,1,0:T(1,128)}), f32[8,1,4096]{2,1,0:T(1,128)S(1)}, u32[]{:S(2)}, u32[]{:S(2)}) async-start(f32[8,1,4096]{2,1,0:T(1,128)} %broadcast_in_dim.39), calls=%async_computation.1 | async-start | bytes 262144 | tf_op jit(solution)/shard_map/all_to_all | solution.py:73
  86.3 1.2 %copy-start.1 = (f32[32,8192]{1,0:T(8,128)S(1)}, f32[32,8192]{1,0:T(8,128)}, u32[]{:S(2)}) copy-start(f32[32,8192]{1,0:T(8,128)} %add_bitcast_fusion) | copy-start | bytes 3145732
